TPU v7x, 256 devices: a whole 4x4x8 slice. The times are simulated.
256 devices in a mesh: gx: 8 (over x, core), gy: 16 (over y, z_lo), lev: 2 (over z_hi).
Axes of the slice: x: 4, y: 4, z: 8 (z_hi: 2, z_lo: 4; z = z_hi * 4 + z_lo), core: 2. Of those that a mesh axis runs over, the one named last changes fastest.
Arguments:
- source: float32 [32, 512, 1024], P('lev', 'gy', 'gx'), may hold values from -6 to 6
- remap_weights: float32 [4096, 4, 128, 128], P(('gx', 'gy'))
- intersection_devices: int32 [4096, 4], replicated, may hold values from 0 to 127, all different within a row; in each aligned block of 32 rows (0 to 31, 32 to 63, ...) at most 2 rows name the same one
- intersection_rows: int32 [4096, 4], replicated, may hold values from 0 to 31
- smoothing: float32 [256, 2048], P('gx', 'gy'), may hold values from 0.04 to 0.24
Outputs:
- face_field: float32 [32, 256, 2048], P('lev', 'gx', 'gy')
Inputs may be any that keep to these rules, and one draw needn't show every extreme that they name: `intersection_devices`: each row names 4 different source tiles. Among the rows of one destination device (32 aligned rows), no source tile is named more than 2 times, and in every draw some source tile is named exactly 2 times.
All inputs are finite; a program needn't handle non-finite values.
Results may differ from a plain program's by a relative error of at most 0.00011.
Values sent between devices are 32-bit elements; how exact they have to be, the bound alone decides.
No kernel may reach another device: no remote copies, remote signals or barrier semaphores. Data moves between devices by JAX's collectives and lax.ppermute only.
A program may use at most 64 MiB of HBM per device.

v0:
```python
import jax
import jax.numpy as jnp
from jax import lax
from jax.sharding import PartitionSpec as P

PASSES = 3


def padded_2(block, sides, width):
    for axis, dim in sides:
        count = lax.axis_size(axis)
        forward = [(i, i + 1) for i in range(count - 1)]
        backward = [(target, source) for source, target in forward]
        low = lax.ppermute(
            lax.slice_in_dim(block, block.shape[dim] - width, None, axis=dim), axis, forward
        )
        high = lax.ppermute(lax.slice_in_dim(block, 0, width, axis=dim), axis, backward)
        block = jnp.concatenate([low, block, high], axis=dim)
    return block


def ranks(entries):
    same = entries[:, :, None] == entries[:, None, :]
    order = jnp.arange(entries.shape[1])
    before = order[None, :] < order[:, None]
    return jnp.sum(jnp.logical_and(same, before[None]), axis=2)


def smooth_step(values, gained):
    laplace = (
        values[:, 2:, 1:-1]
        + values[:, :-2, 1:-1]
        + values[:, 1:-1, 2:]
        + values[:, 1:-1, :-2]
        - 4.0 * values[:, 1:-1, 1:-1]
    )
    return values[:, 1:-1, 1:-1] + gained * laplace


def shards(source, remap_weights, intersection_devices, intersection_rows, smoothing):
    along_x = lax.axis_size("gx")
    along_y = lax.axis_size("gy")
    devices = along_x * along_y
    frows = remap_weights.shape[0]
    fanin = remap_weights.shape[1]
    block = remap_weights.shape[2]
    capacity = 2 * max(1, frows * fanin // devices)
    myself = lax.axis_index("gx") * along_y + lax.axis_index("gy")
    entries = intersection_devices.reshape(devices, frows * fanin)
    slots = ranks(entries)
    lat_all = intersection_rows.reshape(devices, frows * fanin)
    hits = entries == myself
    slot_ids = jnp.arange(capacity, dtype=jnp.int32)
    matched = jnp.logical_and(hits[:, None, :], slots[:, None, :] == slot_ids[None, :, None])
    send_row = jnp.sum(jnp.where(matched, lat_all[:, None, :], 0), axis=2).reshape(
        devices * capacity
    )
    outgoing = jnp.take(source, send_row, axis=1)
    mine_entries = lax.dynamic_index_in_dim(entries, myself, 0, keepdims=False)
    mine_slots = lax.dynamic_index_in_dim(slots, myself, 0, keepdims=False)
    pick_slot = mine_entries * capacity + mine_slots
    incoming = lax.all_to_all(outgoing, ("gx", "gy"), split_axis=1, concat_axis=1, tiled=True)
    picked = jnp.take(incoming, pick_slot, axis=1).reshape(incoming.shape[0], frows, fanin, block)
    field = jnp.einsum("likc,ikcd->lid", picked, remap_weights, precision=lax.Precision.HIGHEST)
    for _ in range(PASSES):
        padded = padded_2(field, (("gx", 1), ("gy", 2)), 1)
        field = smooth_step(padded, smoothing)
    return field


def solution(mesh):
    return jax.shard_map(
        shards,
        mesh=mesh,
        in_specs=(P("lev", "gy", "gx"), P(("gx", "gy"), None, None, None), P(), P(), P("gx", "gy")),
        out_specs=P("lev", "gx", "gy"),
        check_vma=False,
    )
```

profile of v0, /device:TPU:27, one launch (start us, length us, event | category | flops | bytes accessed | tf_op | source)
XLA Modules:
  0.0 166.6 jit_solution(6088041380241219824)
XLA Ops:
  0.0 0.0 copy-start
  0.0 0.0 copy-start.2
  0.0 1.5 copy.16
  1.6 1.6 reshape.112
  3.2 5.1 %convert_reduce_fusion = s32[128,128]{1,0:T(8,128)S(1)} fusion(s32[128,128]{1,0:T(8,128)S(1)} %reshape.112, pred[128,128]{1,0:T(8,128)(4,1)S(1)} %iota_compare_fusion.1), kind=kLoop, calls=%fused_computation.2 | loop fusion | flops 8372224 | bytes 147456 | tf_op jit(solution)/shard_map/reduce_sum | solution.py:26
  8.4 0.0 copy-done.2
  8.4 0.6 copy.17
  9.0 1.6 broadcast_in_dim.44
  10.7 0.1 select_reduce_fusion
  10.8 0.1 copy.18
  10.9 0.1 reshape.114
  11.1 0.1 reshape.113
  11.2 0.0 copy-done
  11.2 5.0 %gather_fusion = f32[256,16,128]{2,0,1:T(8,128)S(1)} fusion(f32[16,32,128]{2,1,0:T(8,128)S(1)} %copy-done, s32[1024]{0:T(1024)S(1)} %pad_clamp_fusion.1), kind=kCustom, calls=%fused_computation | custom fusion | bytes 4195328 | tf_op jit(solution)/shard_map/jit(_take)/gather | solution.py:58
  16.2 0.3 select_bitcast_fusion
  16.5 2.6 %copy.20 = f32[16,256,128]{2,0,1:T(8,128)} copy(f32[16,256,128]{2,1,0:T(8,128)S(1)} %select_bitcast_fusion) | data formatting | bytes 4194304 | tf_op jit(solution)/shard_map/jit(_take)/select_n | solution.py:58
  19.1 13.1 %all-to-all-start = ((f32[16,256,128]{2,0,1:T(8,128)}), f32[16,256,128]{2,0,1:T(8,128)S(1)}, u32[]{:S(2)}, u32[]{:S(2)}) async-start(f32[16,256,128]{2,0,1:T(8,128)} %copy.20), calls=%async_computation | async-start | bytes 4194304 | tf_op jit(solution)/shard_map/all_to_all | solution.py:62
  32.2 0.5 broadcast.102
  32.7 0.7 fusion.24
  33.4 0.1 add.109
  33.5 47.8 %all-to-all-done = f32[16,256,128]{2,0,1:T(8,128)S(1)} async-done(((f32[16,256,128]{2,0,1:T(8,128)}), f32[16,256,128]{2,0,1:T(8,128)S(1)}, u32[]{:S(2)}, u32[]{:S(2)}) %all-to-all-start) | async-done | bytes 2097184 | tf_op jit(solution)/shard_map/all_to_all | solution.py:62
  81.3 0.8 gather_fusion.1
  82.1 0.0 copy-start.1
  82.1 6.6 %convolution_bitcast_fusion = f32[16,32,128]{2,0,1:T(8,128)S(1)} fusion(f32[32,4,128,128]{3,2,1,0:T(8,128)} %param.6, f32[16,32,4,128]{3,0,2,1:T(8,128)S(1)} %bitcast.16, pred[32,4]{1,0:T(8,128)(4,1)S(1)} %compare_and_fusion), kind=kOutput, calls=%fused_computation.4 | convolution fusion | flops 402915328 | bytes 9699456 | tf_op jit(solution)/shard_map/likc,ikcd->lid/dot_general | solution.py:64
  88.8 2.2 %collective-permute-start.1 = (f32[16,1,128]{2,0,1:T(8,128)S(1)}, f32[16,1,128]{2,0,1:T(8,128)S(1)}, u32[]{:S(2)}, u32[]{:S(2)}) collective-permute-start(f32[16,1,128]{2,0,1:T(8,128)S(1)} %get-tuple-element.17), channel_id=1, source_target_pairs={{0,32},{32,64},{64,96},{96,128},{128,160},{160,192},{192,224},{1,3... | collective-permute-start | bytes 24584 | tf_op jit(solution)/shard_map/ppermute | solution.py:14
  91.0 2.1 %collective-permute-start = (f32[16,1,128]{2,0,1:T(8,128)S(1)}, f32[16,1,128]{2,0,1:T(8,128)S(1)}, u32[]{:S(2)}, u32[]{:S(2)}) collective-permute-start(f32[16,1,128]{2,0,1:T(8,128)S(1)} %get-tuple-element.18), channel_id=1, source_target_pairs={{32,0},{64,32},{96,64},{128,96},{160,128},{192,160},{224,192},{33,... | collective-permute-start | bytes 24584 | tf_op jit(solution)/shard_map/ppermute | solution.py:17
  93.1 0.0 collective-permute-done.1
  93.1 2.8 %collective-permute-done = f32[16,1,128]{2,0,1:T(8,128)S(1)} collective-permute-done((f32[16,1,128]{2,0,1:T(8,128)S(1)}, f32[16,1,128]{2,0,1:T(8,128)S(1)}, u32[]{:S(2)}, u32[]{:S(2)}) %collective-permute-start) | collective-permute-done | bytes 8224 | tf_op jit(solution)/shard_map/ppermute | solution.py:17
  96.0 0.1 fusion.27
  96.1 3.0 %collective-permute-start.2 = (f32[16,34,1]{2,0,1:T(8,128)S(1)}, f32[16,34,1]{2,0,1:T(8,128)S(1)}, u32[]{:S(2)}, u32[]{:S(2)}) collective-permute-start(f32[16,34,1]{2,0,1:T(8,128)S(1)} %get-tuple-element.11), channel_id=1, source_target_pairs={{2,0},{4,2},{6,4},{8,6},{10,8},{12,10},{14,12},{16,14},{18,16},{20... | collective-permute-start | bytes 6536 | tf_op jit(solution)/shard_map/ppermute | solution.py:17
  99.1 2.3 %collective-permute-start.3 = (f32[16,34,1]{2,0,1:T(8,128)S(1)}, f32[16,34,1]{2,0,1:T(8,128)S(1)}, u32[]{:S(2)}, u32[]{:S(2)}) collective-permute-start(f32[16,34,1]{2,0,1:T(8,128)S(1)} %get-tuple-element.12), channel_id=1, source_target_pairs={{0,2},{2,4},{4,6},{6,8},{8,10},{10,12},{12,14},{14,16},{16,18},{18... | collective-permute-start | bytes 6536 | tf_op jit(solution)/shard_map/ppermute | solution.py:14
  101.4 4.9 %collective-permute-done.2 = f32[16,34,1]{2,0,1:T(8,128)S(1)} collective-permute-done((f32[16,34,1]{2,0,1:T(8,128)S(1)}, f32[16,34,1]{2,0,1:T(8,128)S(1)}, u32[]{:S(2)}, u32[]{:S(2)}) %collective-permute-start.2) | collective-permute-done | bytes 2208 | tf_op jit(solution)/shard_map/ppermute | solution.py:17
  106.3 6.0 %collective-permute-done.3 = f32[16,34,1]{2,0,1:T(8,128)S(1)} collective-permute-done((f32[16,34,1]{2,0,1:T(8,128)S(1)}, f32[16,34,1]{2,0,1:T(8,128)S(1)}, u32[]{:S(2)}, u32[]{:S(2)}) %collective-permute-start.3) | collective-permute-done | bytes 2208 | tf_op jit(solution)/shard_map/ppermute | solution.py:14
  112.3 0.0 copy-done.1
  112.3 0.3 fusion.18
  112.6 2.9 %collective-permute-start.5 = (f32[16,1,128]{2,0,1:T(8,128)S(1)}, f32[16,1,128]{2,0,1:T(8,128)S(1)}, u32[]{:S(2)}, u32[]{:S(2)}) collective-permute-start(f32[16,1,128]{2,0,1:T(8,128)S(1)} %get-tuple-element.15), channel_id=1, source_target_pairs={{0,32},{32,64},{64,96},{96,128},{128,160},{160,192},{192,224},{1,3... | collective-permute-start | bytes 24584 | tf_op jit(solution)/shard_map/ppermute | solution.py:14
  115.6 1.9 %collective-permute-start.4 = (f32[16,1,128]{2,0,1:T(8,128)S(1)}, f32[16,1,128]{2,0,1:T(8,128)S(1)}, u32[]{:S(2)}, u32[]{:S(2)}) collective-permute-start(f32[16,1,128]{2,0,1:T(8,128)S(1)} %get-tuple-element.16), channel_id=1, source_target_pairs={{32,0},{64,32},{96,64},{128,96},{160,128},{192,160},{224,192},{33,... | collective-permute-start | bytes 24584 | tf_op jit(solution)/shard_map/ppermute | solution.py:17
  117.5 0.0 collective-permute-done.5
  117.5 3.0 %collective-permute-done.4 = f32[16,1,128]{2,0,1:T(8,128)S(1)} collective-permute-done((f32[16,1,128]{2,0,1:T(8,128)S(1)}, f32[16,1,128]{2,0,1:T(8,128)S(1)}, u32[]{:S(2)}, u32[]{:S(2)}) %collective-permute-start.4) | collective-permute-done | bytes 8224 | tf_op jit(solution)/shard_map/ppermute | solution.py:17
  120.5 0.1 fusion.26
  120.7 5.7 %collective-permute-start.6 = (f32[16,34,1]{2,0,1:T(8,128)S(1)}, f32[16,34,1]{2,0,1:T(8,128)S(1)}, u32[]{:S(2)}, u32[]{:S(2)}) collective-permute-start(f32[16,34,1]{2,0,1:T(8,128)S(1)} %get-tuple-element.9), channel_id=1, source_target_pairs={{2,0},{4,2},{6,4},{8,6},{10,8},{12,10},{14,12},{16,14},{18,16},{20... | collective-permute-start | bytes 6536 | tf_op jit(solution)/shard_map/ppermute | solution.py:17
  126.4 1.9 %collective-permute-start.7 = (f32[16,34,1]{2,0,1:T(8,128)S(1)}, f32[16,34,1]{2,0,1:T(8,128)S(1)}, u32[]{:S(2)}, u32[]{:S(2)}) collective-permute-start(f32[16,34,1]{2,0,1:T(8,128)S(1)} %get-tuple-element.10), channel_id=1, source_target_pairs={{0,2},{2,4},{4,6},{6,8},{8,10},{10,12},{12,14},{14,16},{16,18},{18... | collective-permute-start | bytes 6536 | tf_op jit(solution)/shard_map/ppermute | solution.py:14
  128.3 4.6 %collective-permute-done.6 = f32[16,34,1]{2,0,1:T(8,128)S(1)} collective-permute-done((f32[16,34,1]{2,0,1:T(8,128)S(1)}, f32[16,34,1]{2,0,1:T(8,128)S(1)}, u32[]{:S(2)}, u32[]{:S(2)}) %collective-permute-start.6) | collective-permute-done | bytes 2208 | tf_op jit(solution)/shard_map/ppermute | solution.py:17
  132.9 7.1 %collective-permute-done.7 = f32[16,34,1]{2,0,1:T(8,128)S(1)} collective-permute-done((f32[16,34,1]{2,0,1:T(8,128)S(1)}, f32[16,34,1]{2,0,1:T(8,128)S(1)}, u32[]{:S(2)}, u32[]{:S(2)}) %collective-permute-start.7) | collective-permute-done | bytes 2208 | tf_op jit(solution)/shard_map/ppermute | solution.py:14
  140.0 0.3 fusion.12
  140.3 2.0 %collective-permute-start.9 = (f32[16,1,128]{2,0,1:T(8,128)S(1)}, f32[16,1,128]{2,0,1:T(8,128)S(1)}, u32[]{:S(2)}, u32[]{:S(2)}) collective-permute-start(f32[16,1,128]{2,0,1:T(8,128)S(1)} %get-tuple-element.13), channel_id=1, source_target_pairs={{0,32},{32,64},{64,96},{96,128},{128,160},{160,192},{192,224},{1,3... | collective-permute-start | bytes 24584 | tf_op jit(solution)/shard_map/ppermute | solution.py:14
  142.3 2.4 %collective-permute-start.8 = (f32[16,1,128]{2,0,1:T(8,128)S(1)}, f32[16,1,128]{2,0,1:T(8,128)S(1)}, u32[]{:S(2)}, u32[]{:S(2)}) collective-permute-start(f32[16,1,128]{2,0,1:T(8,128)S(1)} %get-tuple-element.14), channel_id=1, source_target_pairs={{32,0},{64,32},{96,64},{128,96},{160,128},{192,160},{224,192},{33,... | collective-permute-start | bytes 24584 | tf_op jit(solution)/shard_map/ppermute | solution.py:17
  144.7 0.0 collective-permute-done.9
  144.7 2.6 %collective-permute-done.8 = f32[16,1,128]{2,0,1:T(8,128)S(1)} collective-permute-done((f32[16,1,128]{2,0,1:T(8,128)S(1)}, f32[16,1,128]{2,0,1:T(8,128)S(1)}, u32[]{:S(2)}, u32[]{:S(2)}) %collective-permute-start.8) | collective-permute-done | bytes 8224 | tf_op jit(solution)/shard_map/ppermute | solution.py:17
  147.3 0.1 fusion.25
  147.4 4.8 %collective-permute-start.10 = (f32[16,34,1]{2,0,1:T(8,128)S(1)}, f32[16,34,1]{2,0,1:T(8,128)S(1)}, u32[]{:S(2)}, u32[]{:S(2)}) collective-permute-start(f32[16,34,1]{2,0,1:T(8,128)S(1)} %get-tuple-element.7), channel_id=1, source_target_pairs={{2,0},{4,2},{6,4},{8,6},{10,8},{12,10},{14,12},{16,14},{18,16},{20... | collective-permute-start | bytes 6536 | tf_op jit(solution)/shard_map/ppermute | solution.py:17
  152.3 1.9 %collective-permute-start.11 = (f32[16,34,1]{2,0,1:T(8,128)S(1)}, f32[16,34,1]{2,0,1:T(8,128)S(1)}, u32[]{:S(2)}, u32[]{:S(2)}) collective-permute-start(f32[16,34,1]{2,0,1:T(8,128)S(1)} %get-tuple-element.8), channel_id=1, source_target_pairs={{0,2},{2,4},{4,6},{6,8},{8,10},{10,12},{12,14},{14,16},{16,18},{18... | collective-permute-start | bytes 6536 | tf_op jit(solution)/shard_map/ppermute | solution.py:14
  154.2 4.5 %collective-permute-done.10 = f32[16,34,1]{2,0,1:T(8,128)S(1)} collective-permute-done((f32[16,34,1]{2,0,1:T(8,128)S(1)}, f32[16,34,1]{2,0,1:T(8,128)S(1)}, u32[]{:S(2)}, u32[]{:S(2)}) %collective-permute-start.10) | collective-permute-done | bytes 2208 | tf_op jit(solution)/shard_map/ppermute | solution.py:17
  158.7 6.8 %collective-permute-done.11 = f32[16,34,1]{2,0,1:T(8,128)S(1)} collective-permute-done((f32[16,34,1]{2,0,1:T(8,128)S(1)}, f32[16,34,1]{2,0,1:T(8,128)S(1)}, u32[]{:S(2)}, u32[]{:S(2)}) %collective-permute-start.11) | collective-permute-done | bytes 2208 | tf_op jit(solution)/shard_map/ppermute | solution.py:14
  165.5 0.3 fusion.6
  165.8 0.8 copy.21
  (14 shorter events, 0.1 us)
Async XLA Ops:
  0.0 11.2 %copy-start = (f32[16,32,128]{2,1,0:T(8,128)S(1)}, f32[16,32,128]{2,1,0:T(8,128)}, u32[]{:S(2)}) copy-start(f32[16,32,128]{2,1,0:T(8,128)} %param.5) | copy-start | bytes 786436
  0.0 8.3 %copy-start.2 = (s32[4096,4]{0,1:T(4,128)S(1)}, s32[4096,4]{0,1:T(4,128)}, u32[]{:S(2)}) copy-start(s32[4096,4]{0,1:T(4,128)} %param.8) | copy-start | bytes 196612
  19.1 62.2 %all-to-all-start = ((f32[16,256,128]{2,0,1:T(8,128)}), f32[16,256,128]{2,0,1:T(8,128)S(1)}, u32[]{:S(2)}, u32[]{:S(2)}) async-start(f32[16,256,128]{2,0,1:T(8,128)} %copy.20), calls=%async_computation | async-start | bytes 4194304 | tf_op jit(solution)/shard_map/all_to_all | solution.py:62
  82.1 30.2 %copy-start.1 = (f32[32,128]{1,0:T(8,128)S(1)}, f32[32,128]{1,0:T(8,128)}, u32[]{:S(2)}) copy-start(f32[32,128]{1,0:T(8,128)} %param.9) | copy-start | bytes 49156
  88.8 4.3 %collective-permute-start.1 = (f32[16,1,128]{2,0,1:T(8,128)S(1)}, f32[16,1,128]{2,0,1:T(8,128)S(1)}, u32[]{:S(2)}, u32[]{:S(2)}) collective-permute-start(f32[16,1,128]{2,0,1:T(8,128)S(1)} %get-tuple-element.17), channel_id=1, source_target_pairs={{0,32},{32,64},{64,96},{96,128},{128,160},{160,192},{192,224},{1,3... | collective-permute-start | bytes 24584 | tf_op jit(solution)/shard_map/ppermute | solution.py:14
  91.0 5.0 %collective-permute-start = (f32[16,1,128]{2,0,1:T(8,128)S(1)}, f32[16,1,128]{2,0,1:T(8,128)S(1)}, u32[]{:S(2)}, u32[]{:S(2)}) collective-permute-start(f32[16,1,128]{2,0,1:T(8,128)S(1)} %get-tuple-element.18), channel_id=1, source_target_pairs={{32,0},{64,32},{96,64},{128,96},{160,128},{192,160},{224,192},{33,... | collective-permute-start | bytes 24584 | tf_op jit(solution)/shard_map/ppermute | solution.py:17
  96.1 10.2 %collective-permute-start.2 = (f32[16,34,1]{2,0,1:T(8,128)S(1)}, f32[16,34,1]{2,0,1:T(8,128)S(1)}, u32[]{:S(2)}, u32[]{:S(2)}) collective-permute-start(f32[16,34,1]{2,0,1:T(8,128)S(1)} %get-tuple-element.11), channel_id=1, source_target_pairs={{2,0},{4,2},{6,4},{8,6},{10,8},{12,10},{14,12},{16,14},{18,16},{20... | collective-permute-start | bytes 6536 | tf_op jit(solution)/shard_map/ppermute | solution.py:17
  99.1 13.2 %collective-permute-start.3 = (f32[16,34,1]{2,0,1:T(8,128)S(1)}, f32[16,34,1]{2,0,1:T(8,128)S(1)}, u32[]{:S(2)}, u32[]{:S(2)}) collective-permute-start(f32[16,34,1]{2,0,1:T(8,128)S(1)} %get-tuple-element.12), channel_id=1, source_target_pairs={{0,2},{2,4},{4,6},{6,8},{8,10},{10,12},{12,14},{14,16},{16,18},{18... | collective-permute-start | bytes 6536 | tf_op jit(solution)/shard_map/ppermute | solution.py:14
  112.6 4.9 %collective-permute-start.5 = (f32[16,1,128]{2,0,1:T(8,128)S(1)}, f32[16,1,128]{2,0,1:T(8,128)S(1)}, u32[]{:S(2)}, u32[]{:S(2)}) collective-permute-start(f32[16,1,128]{2,0,1:T(8,128)S(1)} %get-tuple-element.15), channel_id=1, source_target_pairs={{0,32},{32,64},{64,96},{96,128},{128,160},{160,192},{192,224},{1,3... | collective-permute-start | bytes 24584 | tf_op jit(solution)/shard_map/ppermute | solution.py:14
  115.6 5.0 %collective-permute-start.4 = (f32[16,1,128]{2,0,1:T(8,128)S(1)}, f32[16,1,128]{2,0,1:T(8,128)S(1)}, u32[]{:S(2)}, u32[]{:S(2)}) collective-permute-start(f32[16,1,128]{2,0,1:T(8,128)S(1)} %get-tuple-element.16), channel_id=1, source_target_pairs={{32,0},{64,32},{96,64},{128,96},{160,128},{192,160},{224,192},{33,... | collective-permute-start | bytes 24584 | tf_op jit(solution)/shard_map/ppermute | solution.py:17
  120.7 12.2 %collective-permute-start.6 = (f32[16,34,1]{2,0,1:T(8,128)S(1)}, f32[16,34,1]{2,0,1:T(8,128)S(1)}, u32[]{:S(2)}, u32[]{:S(2)}) collective-permute-start(f32[16,34,1]{2,0,1:T(8,128)S(1)} %get-tuple-element.9), channel_id=1, source_target_pairs={{2,0},{4,2},{6,4},{8,6},{10,8},{12,10},{14,12},{16,14},{18,16},{20... | collective-permute-start | bytes 6536 | tf_op jit(solution)/shard_map/ppermute | solution.py:17
  126.4 13.6 %collective-permute-start.7 = (f32[16,34,1]{2,0,1:T(8,128)S(1)}, f32[16,34,1]{2,0,1:T(8,128)S(1)}, u32[]{:S(2)}, u32[]{:S(2)}) collective-permute-start(f32[16,34,1]{2,0,1:T(8,128)S(1)} %get-tuple-element.10), channel_id=1, source_target_pairs={{0,2},{2,4},{4,6},{6,8},{8,10},{10,12},{12,14},{14,16},{16,18},{18... | collective-permute-start | bytes 6536 | tf_op jit(solution)/shard_map/ppermute | solution.py:14
  140.3 4.3 %collective-permute-start.9 = (f32[16,1,128]{2,0,1:T(8,128)S(1)}, f32[16,1,128]{2,0,1:T(8,128)S(1)}, u32[]{:S(2)}, u32[]{:S(2)}) collective-permute-start(f32[16,1,128]{2,0,1:T(8,128)S(1)} %get-tuple-element.13), channel_id=1, source_target_pairs={{0,32},{32,64},{64,96},{96,128},{128,160},{160,192},{192,224},{1,3... | collective-permute-start | bytes 24584 | tf_op jit(solution)/shard_map/ppermute | solution.py:14
  142.3 5.0 %collective-permute-start.8 = (f32[16,1,128]{2,0,1:T(8,128)S(1)}, f32[16,1,128]{2,0,1:T(8,128)S(1)}, u32[]{:S(2)}, u32[]{:S(2)}) collective-permute-start(f32[16,1,128]{2,0,1:T(8,128)S(1)} %get-tuple-element.14), channel_id=1, source_target_pairs={{32,0},{64,32},{96,64},{128,96},{160,128},{192,160},{224,192},{33,... | collective-permute-start | bytes 24584 | tf_op jit(solution)/shard_map/ppermute | solution.py:17
  147.4 11.3 %collective-permute-start.10 = (f32[16,34,1]{2,0,1:T(8,128)S(1)}, f32[16,34,1]{2,0,1:T(8,128)S(1)}, u32[]{:S(2)}, u32[]{:S(2)}) collective-permute-start(f32[16,34,1]{2,0,1:T(8,128)S(1)} %get-tuple-element.7), channel_id=1, source_target_pairs={{2,0},{4,2},{6,4},{8,6},{10,8},{12,10},{14,12},{16,14},{18,16},{20... | collective-permute-start | bytes 6536 | tf_op jit(solution)/shard_map/ppermute | solution.py:17
  152.3 13.2 %collective-permute-start.11 = (f32[16,34,1]{2,0,1:T(8,128)S(1)}, f32[16,34,1]{2,0,1:T(8,128)S(1)}, u32[]{:S(2)}, u32[]{:S(2)}) collective-permute-start(f32[16,34,1]{2,0,1:T(8,128)S(1)} %get-tuple-element.8), channel_id=1, source_target_pairs={{0,2},{2,4},{4,6},{6,8},{8,10},{10,12},{12,14},{14,16},{16,18},{18... | collective-permute-start | bytes 6536 | tf_op jit(solution)/shard_map/ppermute | solution.py:14
where the time goes:
time: 167 us
  waiting for transfers between devices  90.2 us (54%)
  starting transfers between devices  46.3 us (28%)
  local copies, waits for them, and re-layouts  16 us (10%)
  other arithmetic  7.16 us (4%)
  matrix products  6.64 us (4%)
    all_to_all x1, waiting for transfers between devices, shards(): lax.all_to_all(outgoing, ('gx', 'gy'), split_axis=1, concat_axis=1, tiled...  47.8 us
    ppermute x6, waiting for transfers between devices, padded_2(): lax.ppermute(lax.slice_in_dim(block, 0, width, axis=dim), axis, backward)  22.5 us
    ppermute x6, waiting for transfers between devices, padded_2(): lax.ppermute(lax.slice_in_dim(block, block.shape[dim] - width, None, axis...  20 us
    ppermute x6, starting transfers between devices, padded_2(): lax.ppermute(lax.slice_in_dim(block, 0, width, axis=dim), axis, backward)  19.9 us
    ppermute x6, starting transfers between devices, padded_2(): lax.ppermute(lax.slice_in_dim(block, block.shape[dim] - width, None, axis...  13.3 us
    all_to_all x1, starting transfers between devices, shards(): lax.all_to_all(outgoing, ('gx', 'gy'), split_axis=1, concat_axis=1, tiled...  13.1 us
    dot_general x1, matrix products, shards(): jnp.einsum('likc,ikcd->lid', picked, remap_weights, precision=lax.Precisi...  6.64 us
    reduce_sum x1, other arithmetic, ranks(): return jnp.sum(jnp.logical_and(same, before[None]), axis=2)  5.12 us
  transfers between devices with their start and end apart: 13, of which 10 were waited for; matrix products, arithmetic and copies ran while one was open for 1% of the time, Pallas kernels for 0%

commit v1 on v0

v1 whole, which is shorter than its diff:
```python
import jax
import jax.numpy as jnp
from jax import lax
from jax.sharding import PartitionSpec as P

PASSES = 3
CAP = 2


def with_halo(block, axis, dim, width):
    count = lax.axis_size(axis)
    forward = [(i, i + 1) for i in range(count - 1)]
    backward = [(target, source) for source, target in forward]
    low = lax.ppermute(
        lax.slice_in_dim(block, block.shape[dim] - width, None, axis=dim), axis, forward
    )
    high = lax.ppermute(lax.slice_in_dim(block, 0, width, axis=dim), axis, backward)
    return jnp.concatenate([low, block, high], axis=dim)


def smooth_step(values, gained):
    laplace = (
        values[:, 2:, 1:-1]
        + values[:, :-2, 1:-1]
        + values[:, 1:-1, 2:]
        + values[:, 1:-1, :-2]
        - 4.0 * values[:, 1:-1, 1:-1]
    )
    return values[:, 1:-1, 1:-1] + gained * laplace


def shards(source, remap_weights, intersection_devices, intersection_rows, smoothing):
    along_x = lax.axis_size("gx")
    along_y = lax.axis_size("gy")
    devices = along_x * along_y
    frows, fanin, block = remap_weights.shape[:3]
    levels = source.shape[0]
    myself = lax.axis_index("gx") * along_y + lax.axis_index("gy")

    entries = intersection_devices.reshape(devices, frows * fanin)
    lat_all = intersection_rows.reshape(devices, frows * fanin)
    hits = (entries == myself).astype(jnp.int32)
    slot = jnp.cumsum(hits, axis=1) - hits
    slot_ids = jnp.arange(CAP, dtype=jnp.int32)
    chosen = jnp.logical_and(hits[:, None, :] > 0, slot[:, None, :] == slot_ids[None, :, None])
    send_row = jnp.sum(jnp.where(chosen, lat_all[:, None, :], 0), axis=2).reshape(devices * CAP)
    rows_first = jnp.transpose(source, (1, 0, 2))
    outgoing = jnp.take(rows_first, send_row, axis=0)
    incoming = lax.all_to_all(outgoing, ("gx", "gy"), 0, 0, tiled=True)

    mine = lax.dynamic_index_in_dim(entries, myself, 0, keepdims=False)
    order = jnp.arange(frows * fanin)
    earlier = jnp.logical_and(mine[:, None] == mine[None, :], order[None, :] < order[:, None])
    mine_slot = jnp.sum(earlier.astype(jnp.int32), axis=1)
    picked = jnp.take(incoming, mine * CAP + mine_slot, axis=0)
    picked = picked.reshape(frows, fanin, levels, block)
    field = jnp.einsum(
        "iklc,ikcd->lid", picked, remap_weights, precision=lax.Precision.HIGHEST
    )

    carried = jnp.concatenate([field, smoothing[None]], axis=0)
    carried = with_halo(carried, "gx", 1, PASSES)
    carried = with_halo(carried, "gy", 2, PASSES)
    field, gain = carried[:levels], carried[levels:]
    for _ in range(PASSES):
        gain = gain[:, 1:-1, 1:-1]
        field = smooth_step(field, gain)
    return field


def solution(mesh):
    return jax.shard_map(
        shards,
        mesh=mesh,
        in_specs=(P("lev", "gy", "gx"), P(("gx", "gy"), None, None, None), P(), P(), P("gx", "gy")),
        out_specs=P("lev", "gx", "gy"),
        check_vma=False,
    )
```

time: 167 us -> 120 us (0.72)
  the two profiles are of different devices: /device:TPU:27 before, /device:TPU:1 now
where the time goes in v1:
time: 120 us; the launch traced here: 119 us
  waiting for transfers between devices  76.1 us (63%)
  starting transfers between devices  22.1 us (18%)
  local copies, waits for them, and re-layouts  9.53 us (8%)
  matrix products  6.64 us (6%)
  other arithmetic  4.81 us (4%)
    all_to_all x1, waiting for transfers between devices, shards(): incoming = lax.all_to_all(outgoing, ('gx', 'gy'), 0, 0, tiled=True)  50.7 us
    ppermute x2, waiting for transfers between devices, with_halo(): lax.ppermute(lax.slice_in_dim(block, 0, width, axis=dim), axis, backward)  17.6 us
    all_to_all x1, starting transfers between devices, shards(): incoming = lax.all_to_all(outgoing, ('gx', 'gy'), 0, 0, tiled=True)  13.8 us
    ppermute x2, waiting for transfers between devices, with_halo(): lax.ppermute(lax.slice_in_dim(block, block.shape[dim] - width, None, axis...  7.76 us
    dot_general x1, matrix products, shards(): jnp.einsum('iklc,ikcd->lid', picked, remap_weights, precision=lax.Precisi...  6.64 us
    ppermute x2, starting transfers between devices, with_halo(): lax.ppermute(lax.slice_in_dim(block, block.shape[dim] - width, None, axis...  5.02 us
    ppermute x2, starting transfers between devices, with_halo(): lax.ppermute(lax.slice_in_dim(block, 0, width, axis=dim), axis, backward)  3.21 us
  transfers between devices with their start and end apart: 5, of which 4 were waited for; matrix products, arithmetic and copies ran while one was open for 1% of the time, Pallas kernels for 0%

profile of v1, /device:TPU:1, one launch (start us, length us, event | category | flops | bytes accessed | tf_op | source)
XLA Modules:
  0.0 119.4 jit_solution(7541101746654603855)
XLA Ops:
  0.0 0.0 copy-start.2
  0.0 1.5 %copy.26 = s32[4096,4]{1,0:T(8,128)S(1)} copy(s32[4096,4]{0,1:T(4,128)} %param.7) | data formatting | bytes 131072 | tf_op args[2]
  1.5 1.6 %reshape.111 = s32[128,128]{1,0:T(8,128)S(1)} reshape(s32[4096,4]{1,0:T(8,128)S(1)} %copy.26) | data formatting | bytes 131072 | tf_op jit(solution)/shard_map/reshape | solution.py:40
  3.2 0.1 copy.30
  3.3 0.1 copy.31
  3.4 0.2 reduce_window_sum.11
  3.6 0.1 copy.32
  3.7 0.0 copy-done.2
  3.7 0.0 copy-start.1
  3.7 0.6 copy.33
  4.4 1.6 %broadcast_in_dim.45 = s32[128,128]{1,0:T(8,128)S(1)} reshape(s32[4096,4]{1,0:T(8,128)S(1)} %copy.33) | data formatting | bytes 131072 | tf_op jit(solution)/shard_map/jit(_where)/broadcast_in_dim | solution.py:46
  6.0 0.1 select_reduce_fusion
  6.1 0.1 copy.34
  6.2 0.1 reshape.113
  6.4 0.1 reshape.112
  6.5 0.0 copy-done.1
  6.5 0.2 copy.44
  6.8 1.0 gather_fusion
  7.8 1.7 %broadcast_select_fusion = f32[256,16,128]{2,1,0:T(8,128)} fusion(f32[256,16,128]{2,1,0:T(8,128)S(1)} %gather_fusion, pred[256]{0:T(512)(128)(4,1)S(1)} %compare_and_fusion), kind=kLoop, calls=%fused_computation.4 | loop fusion | flops 524288 | bytes 4194560 | tf_op jit(solution)/shard_map/jit(_take)/select_n | solution.py:48
  9.5 13.8 %all-to-all-start = ((f32[256,16,128]{2,1,0:T(8,128)}), f32[256,16,128]{2,1,0:T(8,128)S(1)}, u32[]{:S(2)}, u32[]{:S(2)}) async-start(f32[256,16,128]{2,1,0:T(8,128)} %broadcast_select_fusion), calls=%async_computation | async-start | bytes 4194304 | tf_op jit(solution)/shard_map/all_to_all | solution.py:49
  23.3 0.2 convert_reduce_fusion
  23.5 0.1 reduce_sum.23
  23.6 0.1 copy.28
  23.7 0.1 mul.74
  23.8 0.1 copy.27
  23.9 0.1 copy.29
  24.0 50.7 %all-to-all-done = f32[256,16,128]{2,1,0:T(8,128)S(1)} async-done(((f32[256,16,128]{2,1,0:T(8,128)}), f32[256,16,128]{2,1,0:T(8,128)S(1)}, u32[]{:S(2)}, u32[]{:S(2)}) %all-to-all-start) | async-done | bytes 2097184 | tf_op jit(solution)/shard_map/all_to_all | solution.py:49
  74.8 0.8 gather_fusion.1
  75.5 0.0 copy-start
  75.5 6.6 %convolution_bitcast_fusion = f32[16,32,128]{2,0,1:T(8,128)S(1)} fusion(f32[32,4,128,128]{3,2,1,0:T(8,128)} %param.6, f32[32,4,16,128]{3,2,1,0:T(8,128)S(1)} %bitcast.29, pred[32,4]{1,0:T(8,128)(4,1)S(1)} %copy.29), kind=kOutput, calls=%fused_computation.2 | convolution fusion | flops 402915328 | bytes 9699456 | tf_op jit(solution)/shard_map/iklc,ikcd->lid/dot_general | solution.py:57
  82.2 0.0 copy-done
  82.2 3.7 %collective-permute-start = (f32[17,3,128]{2,0,1:T(8,128)S(1)}, f32[17,3,128]{2,0,1:T(8,128)S(1)}, u32[]{:S(2)}, u32[]{:S(2)}) collective-permute-start(f32[17,3,128]{2,0,1:T(8,128)S(1)} %get-tuple-element.9), channel_id=1, source_target_pairs={{0,32},{32,64},{64,96},{96,128},{128,160},{160,192},{192,224},{1,3... | collective-permute-start | bytes 78344 | tf_op jit(solution)/shard_map/ppermute | solution.py:14
  85.9 1.9 %collective-permute-start.1 = (f32[17,3,128]{2,0,1:T(8,128)S(1)}, f32[17,3,128]{2,0,1:T(8,128)S(1)}, u32[]{:S(2)}, u32[]{:S(2)}) collective-permute-start(f32[17,3,128]{2,0,1:T(8,128)S(1)} %get-tuple-element.10), channel_id=1, source_target_pairs={{32,0},{64,32},{96,64},{128,96},{160,128},{192,160},{224,192},{33,... | collective-permute-start | bytes 78344 | tf_op jit(solution)/shard_map/ppermute | solution.py:17
  87.9 0.0 collective-permute-done
  87.9 3.3 %collective-permute-done.1 = f32[17,3,128]{2,0,1:T(8,128)S(1)} collective-permute-done((f32[17,3,128]{2,0,1:T(8,128)S(1)}, f32[17,3,128]{2,0,1:T(8,128)S(1)}, u32[]{:S(2)}, u32[]{:S(2)}) %collective-permute-start.1) | collective-permute-done | bytes 26144 | tf_op jit(solution)/shard_map/ppermute | solution.py:17
  91.2 0.2 fusion.17
  91.4 1.3 %collective-permute-start.2 = (f32[17,38,3]{2,0,1:T(8,128)S(1)}, f32[17,38,3]{2,0,1:T(8,128)S(1)}, u32[]{:S(2)}, u32[]{:S(2)}) collective-permute-start(f32[17,38,3]{2,0,1:T(8,128)S(1)} %get-tuple-element.7), channel_id=1, source_target_pairs={{0,2},{2,4},{4,6},{6,8},{8,10},{10,12},{12,14},{14,16},{16,18},{18... | collective-permute-start | bytes 23264 | tf_op jit(solution)/shard_map/ppermute | solution.py:14
  92.8 1.3 %collective-permute-start.3 = (f32[17,38,3]{2,0,1:T(8,128)S(1)}, f32[17,38,3]{2,0,1:T(8,128)S(1)}, u32[]{:S(2)}, u32[]{:S(2)}) collective-permute-start(f32[17,38,3]{2,0,1:T(8,128)S(1)} %get-tuple-element.8), channel_id=1, source_target_pairs={{2,0},{4,2},{6,4},{8,6},{10,8},{12,10},{14,12},{16,14},{18,16},{20... | collective-permute-start | bytes 23264 | tf_op jit(solution)/shard_map/ppermute | solution.py:17
  94.1 7.8 %collective-permute-done.2 = f32[17,38,3]{2,0,1:T(8,128)S(1)} collective-permute-done((f32[17,38,3]{2,0,1:T(8,128)S(1)}, f32[17,38,3]{2,0,1:T(8,128)S(1)}, u32[]{:S(2)}, u32[]{:S(2)}) %collective-permute-start.2) | collective-permute-done | bytes 7784 | tf_op jit(solution)/shard_map/ppermute | solution.py:14
  101.8 14.3 %collective-permute-done.3 = f32[17,38,3]{2,0,1:T(8,128)S(1)} collective-permute-done((f32[17,38,3]{2,0,1:T(8,128)S(1)}, f32[17,38,3]{2,0,1:T(8,128)S(1)}, u32[]{:S(2)}, u32[]{:S(2)}) %collective-permute-start.3) | collective-permute-done | bytes 7784 | tf_op jit(solution)/shard_map/ppermute | solution.py:17
  116.1 0.2 pad_maximum_fusion.5
  116.3 0.2 pad_maximum_fusion.2
  116.5 0.4 pad_maximum_fusion
  117.0 0.7 fusion.3
  117.7 0.7 fusion.6
  118.3 0.3 fusion.11
  118.7 0.8 copy.37
  (13 shorter events, 0.2 us)
Async XLA Ops:
  0.0 3.7 %copy-start.2 = (s32[4096,4]{0,1:T(4,128)S(1)}, s32[4096,4]{0,1:T(4,128)}, u32[]{:S(2)}) copy-start(s32[4096,4]{0,1:T(4,128)} %param.8) | copy-start | bytes 196612
  3.7 2.8 %copy-start.1 = (f32[16,32,128]{2,1,0:T(8,128)S(1)}, f32[16,32,128]{2,1,0:T(8,128)}, u32[]{:S(2)}) copy-start(f32[16,32,128]{2,1,0:T(8,128)} %param.5) | copy-start | bytes 786436
  9.5 65.3 %all-to-all-start = ((f32[256,16,128]{2,1,0:T(8,128)}), f32[256,16,128]{2,1,0:T(8,128)S(1)}, u32[]{:S(2)}, u32[]{:S(2)}) async-start(f32[256,16,128]{2,1,0:T(8,128)} %broadcast_select_fusion), calls=%async_computation | async-start | bytes 4194304 | tf_op jit(solution)/shard_map/all_to_all | solution.py:49
  75.5 6.7 %copy-start = (f32[32,128]{1,0:T(8,128)S(1)}, f32[32,128]{1,0:T(8,128)}, u32[]{:S(2)}) copy-start(f32[32,128]{1,0:T(8,128)} %param.9) | copy-start | bytes 49156
  82.2 5.6 %collective-permute-start = (f32[17,3,128]{2,0,1:T(8,128)S(1)}, f32[17,3,128]{2,0,1:T(8,128)S(1)}, u32[]{:S(2)}, u32[]{:S(2)}) collective-permute-start(f32[17,3,128]{2,0,1:T(8,128)S(1)} %get-tuple-element.9), channel_id=1, source_target_pairs={{0,32},{32,64},{64,96},{96,128},{128,160},{160,192},{192,224},{1,3... | collective-permute-start | bytes 78344 | tf_op jit(solution)/shard_map/ppermute | solution.py:14
  85.9 5.3 %collective-permute-start.1 = (f32[17,3,128]{2,0,1:T(8,128)S(1)}, f32[17,3,128]{2,0,1:T(8,128)S(1)}, u32[]{:S(2)}, u32[]{:S(2)}) collective-permute-start(f32[17,3,128]{2,0,1:T(8,128)S(1)} %get-tuple-element.10), channel_id=1, source_target_pairs={{32,0},{64,32},{96,64},{128,96},{160,128},{192,160},{224,192},{33,... | collective-permute-start | bytes 78344 | tf_op jit(solution)/shard_map/ppermute | solution.py:17
  91.4 10.4 %collective-permute-start.2 = (f32[17,38,3]{2,0,1:T(8,128)S(1)}, f32[17,38,3]{2,0,1:T(8,128)S(1)}, u32[]{:S(2)}, u32[]{:S(2)}) collective-permute-start(f32[17,38,3]{2,0,1:T(8,128)S(1)} %get-tuple-element.7), channel_id=1, source_target_pairs={{0,2},{2,4},{4,6},{6,8},{8,10},{10,12},{12,14},{14,16},{16,18},{18... | collective-permute-start | bytes 23264 | tf_op jit(solution)/shard_map/ppermute | solution.py:14
  92.8 23.3 %collective-permute-start.3 = (f32[17,38,3]{2,0,1:T(8,128)S(1)}, f32[17,38,3]{2,0,1:T(8,128)S(1)}, u32[]{:S(2)}, u32[]{:S(2)}) collective-permute-start(f32[17,38,3]{2,0,1:T(8,128)S(1)} %get-tuple-element.8), channel_id=1, source_target_pairs={{2,0},{4,2},{6,4},{8,6},{10,8},{12,10},{14,12},{16,14},{18,16},{20... | collective-permute-start | bytes 23264 | tf_op jit(solution)/shard_map/ppermute | solution.py:17

commit v2 on v1

--- a/solution.py
+++ b/solution.py
@@ -16,6 +16,27 @@
     )
     high = lax.ppermute(lax.slice_in_dim(block, 0, width, axis=dim), axis, backward)
     return jnp.concatenate([low, block, high], axis=dim)
+
+
+def packed_halo(block, axis, width):
+    count = lax.axis_size(axis)
+    forward = [(i, i + 1) for i in range(count - 1)]
+    backward = [(target, source) for source, target in forward]
+    channels, rows, cols = block.shape
+    size = channels * rows * width
+    padded = -(-size // 1024) * 1024
+
+    def pack(part):
+        flat = jnp.transpose(part, (2, 0, 1)).reshape(size)
+        return jnp.pad(flat, (0, padded - size)).reshape(padded // 128, 128)
+
+    def unpack(tile):
+        flat = tile.reshape(padded)[:size]
+        return jnp.transpose(flat.reshape(width, channels, rows), (1, 2, 0))
+
+    low = unpack(lax.ppermute(pack(block[:, :, cols - width:]), axis, forward))
+    high = unpack(lax.ppermute(pack(block[:, :, :width]), axis, backward))
+    return jnp.concatenate([low, block, high], axis=2)
 
 
 def smooth_step(values, gained):
@@ -60,7 +81,7 @@
 
     carried = jnp.concatenate([field, smoothing[None]], axis=0)
     carried = with_halo(carried, "gx", 1, PASSES)
-    carried = with_halo(carried, "gy", 2, PASSES)
+    carried = packed_halo(carried, "gy", PASSES)
     field, gain = carried[:levels], carried[levels:]
     for _ in range(PASSES):
         gain = gain[:, 1:-1, 1:-1]

time: 120 us -> 104 us (0.87)
  the two profiles are of different devices: /device:TPU:1 before, /device:TPU:10 now
where the time goes in v2:
time: 104 us; the launch traced here: 103 us
  waiting for transfers between devices  52.5 us (50%)
  starting transfers between devices  27.2 us (26%)
  local copies, waits for them, and re-layouts  11.2 us (11%)
  matrix products  6.6 us (6%)
  other arithmetic  4.82 us (5%)
    all_to_all x1, waiting for transfers between devices, shards(): incoming = lax.all_to_all(outgoing, ('gx', 'gy'), 0, 0, tiled=True)  49.9 us
    all_to_all x1, starting transfers between devices, shards(): incoming = lax.all_to_all(outgoing, ('gx', 'gy'), 0, 0, tiled=True)  12.9 us
    ppermute x1, starting transfers between devices, packed_halo(): high = unpack(lax.ppermute(pack(block[:, :, :width]), axis, backward))  6.8 us
    dot_general x1, matrix products, shards(): jnp.einsum('iklc,ikcd->lid', picked, remap_weights, precision=lax.Precisi...  6.6 us
    ppermute x1, starting transfers between devices, with_halo(): lax.ppermute(lax.slice_in_dim(block, 0, width, axis=dim), axis, backward)  3.64 us
    unnamed x11, local copies, waits for them, and re-layouts  2.32 us
  transfers between devices with their start and end apart: 5, of which 3 were waited for; matrix products, arithmetic and copies ran while one was open for 1% of the time, Pallas kernels for 0%

profile of v2, /device:TPU:10, one launch (start us, length us, event | category | flops | bytes accessed | tf_op | source)
XLA Modules:
  0.0 102.6 jit_solution(8090711861584892398)
XLA Ops:
  0.0 0.0 copy-start.2
  0.0 1.5 %copy.34 = s32[4096,4]{1,0:T(8,128)S(1)} copy(s32[4096,4]{0,1:T(4,128)} %param.7) | data formatting | bytes 131072 | tf_op args[2]
  1.5 1.6 %reshape.135 = s32[128,128]{1,0:T(8,128)S(1)} reshape(s32[4096,4]{1,0:T(8,128)S(1)} %copy.34) | data formatting | bytes 131072 | tf_op jit(solution)/shard_map/reshape | solution.py:61
  3.2 0.1 copy.38
  3.3 0.1 copy.39
  3.4 0.2 reduce_window_sum.11
  3.6 0.1 copy.40
  3.7 0.0 copy-done.2
  3.7 0.0 copy-start.1
  3.7 0.6 copy.41
  4.4 1.6 %broadcast_in_dim.45 = s32[128,128]{1,0:T(8,128)S(1)} reshape(s32[4096,4]{1,0:T(8,128)S(1)} %copy.41) | data formatting | bytes 131072 | tf_op jit(solution)/shard_map/jit(_where)/broadcast_in_dim | solution.py:67
  6.0 0.1 select_reduce_fusion
  6.1 0.1 copy.42
  6.2 0.1 reshape.137
  6.4 0.1 reshape.136
  6.5 0.0 copy-done.1
  6.5 0.2 copy.56
  6.8 1.0 gather_fusion
  7.8 1.7 %broadcast_select_fusion = f32[256,16,128]{2,1,0:T(8,128)} fusion(f32[256,16,128]{2,1,0:T(8,128)S(1)} %gather_fusion, pred[256]{0:T(512)(128)(4,1)S(1)} %compare_and_fusion), kind=kLoop, calls=%fused_computation.4 | loop fusion | flops 524288 | bytes 4194560 | tf_op jit(solution)/shard_map/jit(_take)/select_n | solution.py:69
  9.5 12.9 %all-to-all-start = ((f32[256,16,128]{2,1,0:T(8,128)}), f32[256,16,128]{2,1,0:T(8,128)S(1)}, u32[]{:S(2)}, u32[]{:S(2)}) async-start(f32[256,16,128]{2,1,0:T(8,128)} %broadcast_select_fusion), calls=%async_computation | async-start | bytes 4194304 | tf_op jit(solution)/shard_map/all_to_all | solution.py:70
  22.4 0.2 convert_reduce_fusion
  22.5 0.1 reduce_sum.23
  22.7 0.1 copy.36
  22.7 0.1 mul.74
  22.9 0.1 copy.35
  22.9 0.1 copy.37
  23.1 49.9 %all-to-all-done = f32[256,16,128]{2,1,0:T(8,128)S(1)} async-done(((f32[256,16,128]{2,1,0:T(8,128)}), f32[256,16,128]{2,1,0:T(8,128)S(1)}, u32[]{:S(2)}, u32[]{:S(2)}) %all-to-all-start) | async-done | bytes 2097184 | tf_op jit(solution)/shard_map/all_to_all | solution.py:70
  73.0 0.8 gather_fusion.1
  73.7 0.0 copy-start
  73.8 6.6 %convolution_bitcast_fusion = f32[16,32,128]{2,0,1:T(8,128)S(1)} fusion(f32[32,4,128,128]{3,2,1,0:T(8,128)} %param.6, f32[32,4,16,128]{3,2,1,0:T(8,128)S(1)} %bitcast.49, pred[32,4]{1,0:T(8,128)(4,1)S(1)} %copy.37), kind=kOutput, calls=%fused_computation.2 | convolution fusion | flops 402915328 | bytes 9699456 | tf_op jit(solution)/shard_map/iklc,ikcd->lid/dot_general | solution.py:78
  80.4 0.0 copy-done
  80.4 1.9 %collective-permute-start = (f32[17,3,128]{2,0,1:T(8,128)S(1)}, f32[17,3,128]{2,0,1:T(8,128)S(1)}, u32[]{:S(2)}, u32[]{:S(2)}) collective-permute-start(f32[17,3,128]{2,0,1:T(8,128)S(1)} %get-tuple-element.9), channel_id=1, source_target_pairs={{0,32},{32,64},{64,96},{96,128},{128,160},{160,192},{192,224},{1,3... | collective-permute-start | bytes 78344 | tf_op jit(solution)/shard_map/ppermute | solution.py:14
  82.3 3.6 %collective-permute-start.1 = (f32[17,3,128]{2,0,1:T(8,128)S(1)}, f32[17,3,128]{2,0,1:T(8,128)S(1)}, u32[]{:S(2)}, u32[]{:S(2)}) collective-permute-start(f32[17,3,128]{2,0,1:T(8,128)S(1)} %get-tuple-element.10), channel_id=1, source_target_pairs={{32,0},{64,32},{96,64},{128,96},{160,128},{192,160},{224,192},{33,... | collective-permute-start | bytes 78344 | tf_op jit(solution)/shard_map/ppermute | solution.py:17
  86.0 0.0 collective-permute-done
  86.0 1.6 %collective-permute-done.1 = f32[17,3,128]{2,0,1:T(8,128)S(1)} collective-permute-done((f32[17,3,128]{2,0,1:T(8,128)S(1)}, f32[17,3,128]{2,0,1:T(8,128)S(1)}, u32[]{:S(2)}, u32[]{:S(2)}) %collective-permute-start.1) | collective-permute-done | bytes 26144 | tf_op jit(solution)/shard_map/ppermute | solution.py:17
  87.6 0.2 slice_bitcast_fusion.1
  87.8 0.3 copy.45
  88.1 0.1 reshape.138
  88.2 1.9 %collective-permute-start.2 = (f32[16,128]{1,0:T(8,128)S(1)}, f32[16,128]{1,0:T(8,128)S(1)}, u32[]{:S(2)}, u32[]{:S(2)}) collective-permute-start(f32[16,128]{1,0:T(8,128)S(1)} %pad_bitcast_fusion.1), channel_id=1, source_target_pairs={{0,2},{2,4},{4,6},{6,8},{8,10},{10,12},{12,14},{14,16},{16,18},{18... | collective-permute-start | bytes 24584 | tf_op jit(solution)/shard_map/ppermute | solution.py:37
  90.2 0.3 copy.47
  90.4 0.1 reshape.142
  90.6 6.8 %collective-permute-start.3 = (f32[16,128]{1,0:T(8,128)S(1)}, f32[16,128]{1,0:T(8,128)S(1)}, u32[]{:S(2)}, u32[]{:S(2)}) collective-permute-start(f32[16,128]{1,0:T(8,128)S(1)} %pad_bitcast_fusion), channel_id=1, source_target_pairs={{2,0},{4,2},{6,4},{8,6},{10,8},{12,10},{14,12},{16,14},{18,16},{20... | collective-permute-start | bytes 24584 | tf_op jit(solution)/shard_map/ppermute | solution.py:38
  97.4 0.0 collective-permute-done.2
  97.4 0.1 reshape.141
  97.5 1.0 %collective-permute-done.3 = f32[16,128]{1,0:T(8,128)S(1)} collective-permute-done((f32[16,128]{1,0:T(8,128)S(1)}, f32[16,128]{1,0:T(8,128)S(1)}, u32[]{:S(2)}, u32[]{:S(2)}) %collective-permute-start.3) | collective-permute-done | bytes 8224 | tf_op jit(solution)/shard_map/ppermute | solution.py:38
  98.5 0.1 reshape.145
  98.7 0.3 copy.48
  99.0 0.3 copy.46
  99.3 0.2 pad_maximum_fusion.5
  99.5 0.2 pad_maximum_fusion.2
  99.7 0.4 pad_maximum_fusion
  100.2 0.7 fusion.3
  100.9 0.7 fusion.6
  101.5 0.3 fusion.11
  101.9 0.8 copy.49
  (15 shorter events, 0.2 us)
Async XLA Ops:
  0.0 3.7 %copy-start.2 = (s32[4096,4]{0,1:T(4,128)S(1)}, s32[4096,4]{0,1:T(4,128)}, u32[]{:S(2)}) copy-start(s32[4096,4]{0,1:T(4,128)} %param.8) | copy-start | bytes 196612
  3.7 2.8 %copy-start.1 = (f32[16,32,128]{2,1,0:T(8,128)S(1)}, f32[16,32,128]{2,1,0:T(8,128)}, u32[]{:S(2)}) copy-start(f32[16,32,128]{2,1,0:T(8,128)} %param.5) | copy-start | bytes 786436
  9.5 63.5 %all-to-all-start = ((f32[256,16,128]{2,1,0:T(8,128)}), f32[256,16,128]{2,1,0:T(8,128)S(1)}, u32[]{:S(2)}, u32[]{:S(2)}) async-start(f32[256,16,128]{2,1,0:T(8,128)} %broadcast_select_fusion), calls=%async_computation | async-start | bytes 4194304 | tf_op jit(solution)/shard_map/all_to_all | solution.py:70
  73.7 6.6 %copy-start = (f32[32,128]{1,0:T(8,128)S(1)}, f32[32,128]{1,0:T(8,128)}, u32[]{:S(2)}) copy-start(f32[32,128]{1,0:T(8,128)} %param.9) | copy-start | bytes 49156
  80.4 5.6 %collective-permute-start = (f32[17,3,128]{2,0,1:T(8,128)S(1)}, f32[17,3,128]{2,0,1:T(8,128)S(1)}, u32[]{:S(2)}, u32[]{:S(2)}) collective-permute-start(f32[17,3,128]{2,0,1:T(8,128)S(1)} %get-tuple-element.9), channel_id=1, source_target_pairs={{0,32},{32,64},{64,96},{96,128},{128,160},{160,192},{192,224},{1,3... | collective-permute-start | bytes 78344 | tf_op jit(solution)/shard_map/ppermute | solution.py:14
  82.3 5.3 %collective-permute-start.1 = (f32[17,3,128]{2,0,1:T(8,128)S(1)}, f32[17,3,128]{2,0,1:T(8,128)S(1)}, u32[]{:S(2)}, u32[]{:S(2)}) collective-permute-start(f32[17,3,128]{2,0,1:T(8,128)S(1)} %get-tuple-element.10), channel_id=1, source_target_pairs={{32,0},{64,32},{96,64},{128,96},{160,128},{192,160},{224,192},{33,... | collective-permute-start | bytes 78344 | tf_op jit(solution)/shard_map/ppermute | solution.py:17
  88.2 9.2 %collective-permute-start.2 = (f32[16,128]{1,0:T(8,128)S(1)}, f32[16,128]{1,0:T(8,128)S(1)}, u32[]{:S(2)}, u32[]{:S(2)}) collective-permute-start(f32[16,128]{1,0:T(8,128)S(1)} %pad_bitcast_fusion.1), channel_id=1, source_target_pairs={{0,2},{2,4},{4,6},{6,8},{8,10},{10,12},{12,14},{14,16},{16,18},{18... | collective-permute-start | bytes 24584 | tf_op jit(solution)/shard_map/ppermute | solution.py:37
  90.6 8.0 %collective-permute-start.3 = (f32[16,128]{1,0:T(8,128)S(1)}, f32[16,128]{1,0:T(8,128)S(1)}, u32[]{:S(2)}, u32[]{:S(2)}) collective-permute-start(f32[16,128]{1,0:T(8,128)S(1)} %pad_bitcast_fusion), channel_id=1, source_target_pairs={{2,0},{4,2},{6,4},{8,6},{10,8},{12,10},{14,12},{16,14},{18,16},{20... | collective-permute-start | bytes 24584 | tf_op jit(solution)/shard_map/ppermute | solution.py:38

commit v3 on v2

--- a/solution.py
+++ b/solution.py
@@ -58,25 +58,27 @@
     levels = source.shape[0]
     myself = lax.axis_index("gx") * along_y + lax.axis_index("gy")
 
-    entries = intersection_devices.reshape(devices, frows * fanin)
-    lat_all = intersection_rows.reshape(devices, frows * fanin)
-    hits = (entries == myself).astype(jnp.int32)
-    slot = jnp.cumsum(hits, axis=1) - hits
+    ids_t = intersection_devices.T
+    rows_t = intersection_rows.T
+    hit_k = ids_t == myself
+    hit = jnp.any(hit_k, axis=0).astype(jnp.int32).reshape(devices, frows)
+    lat = jnp.sum(jnp.where(hit_k, rows_t, 0), axis=0).reshape(devices, frows)
+    slot = jnp.cumsum(hit, axis=1) - hit
     slot_ids = jnp.arange(CAP, dtype=jnp.int32)
-    chosen = jnp.logical_and(hits[:, None, :] > 0, slot[:, None, :] == slot_ids[None, :, None])
-    send_row = jnp.sum(jnp.where(chosen, lat_all[:, None, :], 0), axis=2).reshape(devices * CAP)
+    chosen = jnp.logical_and(hit[:, None, :] > 0, slot[:, None, :] == slot_ids[None, :, None])
+    send_row = jnp.sum(jnp.where(chosen, lat[:, None, :], 0), axis=2).reshape(devices * CAP)
     rows_first = jnp.transpose(source, (1, 0, 2))
-    outgoing = jnp.take(rows_first, send_row, axis=0)
+    outgoing = jnp.take(rows_first, send_row, axis=0, mode="clip")
     incoming = lax.all_to_all(outgoing, ("gx", "gy"), 0, 0, tiled=True)
 
-    mine = lax.dynamic_index_in_dim(entries, myself, 0, keepdims=False)
+    mine = lax.dynamic_slice_in_dim(ids_t, myself * frows, frows, axis=1).T.reshape(frows * fanin)
     order = jnp.arange(frows * fanin)
     earlier = jnp.logical_and(mine[:, None] == mine[None, :], order[None, :] < order[:, None])
     mine_slot = jnp.sum(earlier.astype(jnp.int32), axis=1)
-    picked = jnp.take(incoming, mine * CAP + mine_slot, axis=0)
+    picked = jnp.take(incoming, mine * CAP + mine_slot, axis=0, mode="clip")
     picked = picked.reshape(frows, fanin, levels, block)
     field = jnp.einsum(
-        "iklc,ikcd->lid", picked, remap_weights, precision=lax.Precision.HIGHEST
+        "iklc,ikcd->lid", picked, remap_weights, precision=lax.Precision.HIGH
     )
 
     carried = jnp.concatenate([field, smoothing[None]], axis=0)

time: 104 us -> 101 us (0.971); the launches traced: 103 us -> 101 us
  waiting for transfers between devices: 52.5 us -> 58.5 us
  local copies, waits for them, and re-layouts: 11.2 us -> 7.84 us
  starting transfers between devices: 27.2 us -> 24.1 us
  matrix products: 6.6 us -> 4.71 us
    ppermute x1, waiting for transfers between devices: 0.01 us -> 5.88 us  [packed_halo(): low = unpack(lax.ppermute(pack(block[:, :, cols - width:]), axis, forward))]
    ppermute x1, waiting for transfers between devices: 0.01 us -> 3.34 us  [with_halo(): lax.ppermute(lax.slice_in_dim(block, block.shape[dim] - width, None, axis...]
    ppermute x1, starting transfers between devices: 6.8 us -> 4.65 us  [packed_halo(): high = unpack(lax.ppermute(pack(block[:, :, :width]), axis, backward))]
    reshape x4 -> x0, local copies, waits for them, and re-layouts: 2.02 us -> none  [the longest x2 1.74 us: shards(): entries = intersection_devices.reshape(devices, frows * fanin)]
    dot_general x1, matrix products: 6.6 us -> 4.71 us  [shards(): jnp.einsum('iklc,ikcd->lid', picked, remap_weights, precision=lax.Precisi...]
    select_n x3 -> x0, other arithmetic: 1.7 us -> none  [the longest x2 1.69 us: shards(): outgoing = jnp.take(rows_first, send_row, axis=0)]
    ppermute x1, waiting for transfers between devices: 1.6 us -> 0.01 us  [with_halo(): lax.ppermute(lax.slice_in_dim(block, 0, width, axis=dim), axis, backward)]
    broadcast_in_dim x1 -> x3, local copies, waits for them, and re-layouts: 1.65 us -> 0.28 us  [the longest x1 0.14 us: shards(): outgoing = jnp.take(rows_first, send_row, axis=0, mode='clip')]
  transfers between devices with their start and end apart: 5 -> 5, of which waited for: 3 -> 3; matrix products, arithmetic and copies ran while one was open for 1% -> 2% of each run, Pallas kernels for 0% -> 0%
where the time goes in v3:
time: 101 us
  waiting for transfers between devices  58.5 us (58%)
  starting transfers between devices  24.1 us (24%)
  local copies, waits for them, and re-layouts  7.84 us (8%)
  other arithmetic  5.49 us (5%)
  matrix products  4.71 us (5%)
    all_to_all x1, waiting for transfers between devices, shards(): incoming = lax.all_to_all(outgoing, ('gx', 'gy'), 0, 0, tiled=True)  49.3 us
    all_to_all x1, starting transfers between devices, shards(): incoming = lax.all_to_all(outgoing, ('gx', 'gy'), 0, 0, tiled=True)  12.9 us
    ppermute x1, waiting for transfers between devices, packed_halo(): low = unpack(lax.ppermute(pack(block[:, :, cols - width:]), axis, forward))  5.88 us
    dot_general x1, matrix products, shards(): jnp.einsum('iklc,ikcd->lid', picked, remap_weights, precision=lax.Precisi...  4.71 us
    ppermute x1, starting transfers between devices, packed_halo(): high = unpack(lax.ppermute(pack(block[:, :, :width]), axis, backward))  4.65 us
    ppermute x1, waiting for transfers between devices, with_halo(): lax.ppermute(lax.slice_in_dim(block, block.shape[dim] - width, None, axis...  3.34 us
    ppermute x1, starting transfers between devices, with_halo(): lax.ppermute(lax.slice_in_dim(block, 0, width, axis=dim), axis, backward)  2.76 us
    gather x1, local copies, waits for them, and re-layouts, shards(): outgoing = jnp.take(rows_first, send_row, axis=0, mode='clip')  2.36 us
  transfers between devices with their start and end apart: 5, of which 3 were waited for; matrix products, arithmetic and copies ran while one was open for 2% of the time, Pallas kernels for 0%

profile of v3, /device:TPU:10, one launch (start us, length us, event | category | flops | bytes accessed | tf_op | source)
XLA Modules:
  0.0 100.9 jit_solution(7345740456670956110)
XLA Ops:
  0.0 0.9 fusion.12
  0.9 0.1 reshape.89
  1.0 0.1 copy.25
  1.1 1.1 %copy.42 = f32[16,32,128]{2,0,1:T(8,128)S(1)} copy(f32[16,32,128]{2,1,0:T(8,128)} %param.5) | data formatting | bytes 524288 | tf_op args[0]
  2.2 0.9 select_reduce_fusion
  3.1 0.1 broadcast_in_dim.32
  3.2 0.1 copy.27
  3.2 0.1 reduce_window_sum.11
  3.3 0.1 copy.24
  3.4 0.1 copy.28
  3.6 0.1 reshape.92
  3.7 2.4 %gather_fusion = f32[256,16,128]{2,1,0:T(8,128)} fusion(f32[32,16,128]{2,1,0:T(8,128)S(1)} %bitcast.38, s32[1024]{0:T(1024)S(1)} %pad_clamp_fusion.1), kind=kCustom, calls=%fused_computation | custom fusion | bytes 4195328 | tf_op jit(solution)/shard_map/jit(_take)/gather | solution.py:71
  6.1 12.9 %all-to-all-start = ((f32[256,16,128]{2,1,0:T(8,128)}), f32[256,16,128]{2,1,0:T(8,128)S(1)}, u32[]{:S(2)}, u32[]{:S(2)}) async-start(f32[256,16,128]{2,1,0:T(8,128)} %gather_fusion), calls=%async_computation | async-start | bytes 4194304 | tf_op jit(solution)/shard_map/all_to_all | solution.py:72
  19.0 0.8 broadcast_multiply_fusion
  19.7 0.1 copy.29
  19.8 0.1 mul.72
  19.9 0.1 copy.30
  20.0 0.1 eq.40
  20.1 0.2 convert_reduce_fusion
  20.3 49.3 %all-to-all-done = f32[256,16,128]{2,1,0:T(8,128)S(1)} async-done(((f32[256,16,128]{2,1,0:T(8,128)}), f32[256,16,128]{2,1,0:T(8,128)S(1)}, u32[]{:S(2)}, u32[]{:S(2)}) %all-to-all-start) | async-done | bytes 2097184 | tf_op jit(solution)/shard_map/all_to_all | solution.py:72
  69.6 0.8 gather_fusion.1
  70.4 0.0 copy-start
  70.4 4.7 %convolution_bitcast_fusion = f32[16,32,128]{2,0,1:T(8,128)S(1)} fusion(f32[32,4,16,128]{3,2,1,0:T(8,128)S(1)} %bitcast.45, f32[32,4,128,128]{3,2,1,0:T(8,128)} %param.6), kind=kOutput, calls=%fused_computation.2 | convolution fusion | flops 201326592 | bytes 9699328 | tf_op jit(solution)/shard_map/iklc,ikcd->lid/dot_general | solution.py:80
  75.1 0.0 copy-done
  75.1 2.8 %collective-permute-start.1 = (f32[17,3,128]{2,0,1:T(8,128)S(1)}, f32[17,3,128]{2,0,1:T(8,128)S(1)}, u32[]{:S(2)}, u32[]{:S(2)}) collective-permute-start(f32[17,3,128]{2,0,1:T(8,128)S(1)} %get-tuple-element.12), channel_id=1, source_target_pairs={{32,0},{64,32},{96,64},{128,96},{160,128},{192,160},{224,192},{33,... | collective-permute-start | bytes 78344 | tf_op jit(solution)/shard_map/ppermute | solution.py:17
  77.9 1.9 %collective-permute-start = (f32[17,3,128]{2,0,1:T(8,128)S(1)}, f32[17,3,128]{2,0,1:T(8,128)S(1)}, u32[]{:S(2)}, u32[]{:S(2)}) collective-permute-start(f32[17,3,128]{2,0,1:T(8,128)S(1)} %get-tuple-element.11), channel_id=1, source_target_pairs={{0,32},{32,64},{64,96},{96,128},{128,160},{160,192},{192,224},{1,3... | collective-permute-start | bytes 78344 | tf_op jit(solution)/shard_map/ppermute | solution.py:14
  79.8 0.0 collective-permute-done.1
  79.8 3.3 %collective-permute-done = f32[17,3,128]{2,0,1:T(8,128)S(1)} collective-permute-done((f32[17,3,128]{2,0,1:T(8,128)S(1)}, f32[17,3,128]{2,0,1:T(8,128)S(1)}, u32[]{:S(2)}, u32[]{:S(2)}) %collective-permute-start) | collective-permute-done | bytes 26144 | tf_op jit(solution)/shard_map/ppermute | solution.py:14
  83.2 0.2 slice_bitcast_fusion.1
  83.4 0.3 copy.33
  83.7 0.1 reshape.85
  83.8 4.7 %collective-permute-start.3 = (f32[16,128]{1,0:T(8,128)S(1)}, f32[16,128]{1,0:T(8,128)S(1)}, u32[]{:S(2)}, u32[]{:S(2)}) collective-permute-start(f32[16,128]{1,0:T(8,128)S(1)} %pad_bitcast_fusion), channel_id=1, source_target_pairs={{2,0},{4,2},{6,4},{8,6},{10,8},{12,10},{14,12},{16,14},{18,16},{20... | collective-permute-start | bytes 24584 | tf_op jit(solution)/shard_map/ppermute | solution.py:38
  88.5 0.3 copy.31
  88.7 0.1 reshape.81
  88.9 1.9 %collective-permute-start.2 = (f32[16,128]{1,0:T(8,128)S(1)}, f32[16,128]{1,0:T(8,128)S(1)}, u32[]{:S(2)}, u32[]{:S(2)}) collective-permute-start(f32[16,128]{1,0:T(8,128)S(1)} %pad_bitcast_fusion.1), channel_id=1, source_target_pairs={{0,2},{2,4},{4,6},{6,8},{8,10},{10,12},{12,14},{14,16},{16,18},{18... | collective-permute-start | bytes 24584 | tf_op jit(solution)/shard_map/ppermute | solution.py:37
  90.8 0.0 collective-permute-done.3
  90.8 0.1 reshape.88
  90.9 0.3 copy.34
  91.2 5.9 %collective-permute-done.2 = f32[16,128]{1,0:T(8,128)S(1)} collective-permute-done((f32[16,128]{1,0:T(8,128)S(1)}, f32[16,128]{1,0:T(8,128)S(1)}, u32[]{:S(2)}, u32[]{:S(2)}) %collective-permute-start.2) | collective-permute-done | bytes 8224 | tf_op jit(solution)/shard_map/ppermute | solution.py:37
  97.1 0.1 reshape.84
  97.2 0.3 copy.32
  97.5 0.2 pad_maximum_fusion.2
  97.8 0.2 pad_maximum_fusion.5
  98.0 0.4 pad_maximum_fusion
  98.4 0.7 fusion.2
  99.1 0.7 fusion.5
  99.8 0.3 fusion.8
  100.1 0.8 copy.35
  (13 shorter events, 0.2 us)
Async XLA Ops:
  6.1 63.5 %all-to-all-start = ((f32[256,16,128]{2,1,0:T(8,128)}), f32[256,16,128]{2,1,0:T(8,128)S(1)}, u32[]{:S(2)}, u32[]{:S(2)}) async-start(f32[256,16,128]{2,1,0:T(8,128)} %gather_fusion), calls=%async_computation | async-start | bytes 4194304 | tf_op jit(solution)/shard_map/all_to_all | solution.py:72
  70.4 4.7 %copy-start = (f32[32,128]{1,0:T(8,128)S(1)}, f32[32,128]{1,0:T(8,128)}, u32[]{:S(2)}) copy-start(f32[32,128]{1,0:T(8,128)} %param.9) | copy-start | bytes 49156
  75.1 4.7 %collective-permute-start.1 = (f32[17,3,128]{2,0,1:T(8,128)S(1)}, f32[17,3,128]{2,0,1:T(8,128)S(1)}, u32[]{:S(2)}, u32[]{:S(2)}) collective-permute-start(f32[17,3,128]{2,0,1:T(8,128)S(1)} %get-tuple-element.12), channel_id=1, source_target_pairs={{32,0},{64,32},{96,64},{128,96},{160,128},{192,160},{224,192},{33,... | collective-permute-start | bytes 78344 | tf_op jit(solution)/shard_map/ppermute | solution.py:17
  77.9 5.3 %collective-permute-start = (f32[17,3,128]{2,0,1:T(8,128)S(1)}, f32[17,3,128]{2,0,1:T(8,128)S(1)}, u32[]{:S(2)}, u32[]{:S(2)}) collective-permute-start(f32[17,3,128]{2,0,1:T(8,128)S(1)} %get-tuple-element.11), channel_id=1, source_target_pairs={{0,32},{32,64},{64,96},{96,128},{128,160},{160,192},{192,224},{1,3... | collective-permute-start | bytes 78344 | tf_op jit(solution)/shard_map/ppermute | solution.py:14
  83.8 7.0 %collective-permute-start.3 = (f32[16,128]{1,0:T(8,128)S(1)}, f32[16,128]{1,0:T(8,128)S(1)}, u32[]{:S(2)}, u32[]{:S(2)}) collective-permute-start(f32[16,128]{1,0:T(8,128)S(1)} %pad_bitcast_fusion), channel_id=1, source_target_pairs={{2,0},{4,2},{6,4},{8,6},{10,8},{12,10},{14,12},{16,14},{18,16},{20... | collective-permute-start | bytes 24584 | tf_op jit(solution)/shard_map/ppermute | solution.py:38
  88.9 8.2 %collective-permute-start.2 = (f32[16,128]{1,0:T(8,128)S(1)}, f32[16,128]{1,0:T(8,128)S(1)}, u32[]{:S(2)}, u32[]{:S(2)}) collective-permute-start(f32[16,128]{1,0:T(8,128)S(1)} %pad_bitcast_fusion.1), channel_id=1, source_target_pairs={{0,2},{2,4},{4,6},{6,8},{8,10},{10,12},{12,14},{14,16},{16,18},{18... | collective-permute-start | bytes 24584 | tf_op jit(solution)/shard_map/ppermute | solution.py:37

commit v4 on v3

--- a/solution.py
+++ b/solution.py
@@ -77,12 +77,26 @@
     mine_slot = jnp.sum(earlier.astype(jnp.int32), axis=1)
     picked = jnp.take(incoming, mine * CAP + mine_slot, axis=0, mode="clip")
     picked = picked.reshape(frows, fanin, levels, block)
-    field = jnp.einsum(
-        "iklc,ikcd->lid", picked, remap_weights, precision=lax.Precision.HIGH
+
+    def remap(lo, hi):
+        return jnp.einsum(
+            "iklc,ikcd->lid", picked[lo:hi], remap_weights[lo:hi], precision=lax.Precision.HIGH
+        )
+
+    count = lax.axis_size("gx")
+    forward = [(i, i + 1) for i in range(count - 1)]
+    backward = [(target, source) for source, target in forward]
+    top = jnp.concatenate([remap(0, PASSES), smoothing[None, :PASSES]], axis=0)
+    bottom = jnp.concatenate(
+        [remap(frows - PASSES, frows), smoothing[None, frows - PASSES:]], axis=0
     )
-
-    carried = jnp.concatenate([field, smoothing[None]], axis=0)
-    carried = with_halo(carried, "gx", 1, PASSES)
+    top, bottom = lax.optimization_barrier((top, bottom))
+    low = lax.ppermute(bottom, "gx", forward)
+    high = lax.ppermute(top, "gx", backward)
+    middle = jnp.concatenate(
+        [remap(PASSES, frows - PASSES), smoothing[None, PASSES:frows - PASSES]], axis=0
+    )
+    carried = jnp.concatenate([low, top, middle, bottom, high], axis=1)
     carried = packed_halo(carried, "gy", PASSES)
     field, gain = carried[:levels], carried[levels:]
     for _ in range(PASSES):

time: 101 us -> 101 us (level); the launches traced: 101 us -> 99.3 us
  waiting for transfers between devices: 58.5 us -> 51.6 us
  starting transfers between devices: 24.1 us -> 27 us
  matrix products: 4.71 us -> 6.9 us
    ppermute x1, waiting for transfers between devices: 5.88 us -> 0.01 us  [packed_halo(): low = unpack(lax.ppermute(pack(block[:, :, cols - width:]), axis, forward))]
    dot_general x1 -> x3, matrix products: 4.71 us -> 6.9 us  [remap(): jnp.einsum('iklc,ikcd->lid', picked[lo:hi], remap_weights[lo:hi], precisi...]
    ppermute x1, starting transfers between devices: 4.65 us -> 6.62 us  [packed_halo(): high = unpack(lax.ppermute(pack(block[:, :, :width]), axis, backward))]
    ppermute x2, waiting for transfers between devices: 3.34 us -> 1.53 us  [the longest x1 1.53 us: shards(): high = lax.ppermute(top, 'gx', backward)]
  transfers between devices with their start and end apart: 5 -> 5, of which waited for: 3 -> 3; matrix products, arithmetic and copies ran while one was open for 2% -> 6% of each run, Pallas kernels for 0% -> 0%
where the time goes in v4:
time: 101 us; the launch traced here: 99.3 us
  waiting for transfers between devices  51.6 us (51%)
  starting transfers between devices  27 us (27%)
  local copies, waits for them, and re-layouts  7.95 us (8%)
  matrix products  6.9 us (7%)
  other arithmetic  5.51 us (5%)
    all_to_all x1, waiting for transfers between devices, shards(): incoming = lax.all_to_all(outgoing, ('gx', 'gy'), 0, 0, tiled=True)  49.2 us
    all_to_all x1, starting transfers between devices, shards(): incoming = lax.all_to_all(outgoing, ('gx', 'gy'), 0, 0, tiled=True)  12.9 us
    dot_general x3, matrix products, remap(): jnp.einsum('iklc,ikcd->lid', picked[lo:hi], remap_weights[lo:hi], precisi...  6.9 us
    ppermute x1, starting transfers between devices, packed_halo(): high = unpack(lax.ppermute(pack(block[:, :, :width]), axis, backward))  6.62 us
    ppermute x1, starting transfers between devices, shards(): high = lax.ppermute(top, 'gx', backward)  3.64 us
    gather x1, local copies, waits for them, and re-layouts, shards(): outgoing = jnp.take(rows_first, send_row, axis=0, mode='clip')  2.36 us
  transfers between devices with their start and end apart: 5, of which 3 were waited for; matrix products, arithmetic and copies ran while one was open for 6% of the time, Pallas kernels for 0%

profile of v4, /device:TPU:10, one launch (start us, length us, event | category | flops | bytes accessed | tf_op | source)
XLA Modules:
  0.0 99.3 jit_solution(7515594927989826046)
XLA Ops:
  0.0 0.0 copy-start
  0.0 0.9 fusion.19
  0.9 0.1 reshape.88
  1.0 0.1 copy.27
  1.1 0.1 reduce_window_sum.11
  1.2 0.1 copy.26
  1.2 0.9 select_reduce_fusion
  2.2 0.1 broadcast_in_dim.38
  2.2 0.1 copy.29
  2.3 0.1 copy.30
  2.5 0.1 reshape.91
  2.6 1.1 %copy.46 = f32[16,32,128]{2,0,1:T(8,128)S(1)} copy(f32[16,32,128]{2,1,0:T(8,128)} %param.5) | data formatting | bytes 524288 | tf_op args[0]
  3.7 2.4 %gather_fusion = f32[256,16,128]{2,1,0:T(8,128)} fusion(f32[32,16,128]{2,1,0:T(8,128)S(1)} %bitcast.51, s32[1024]{0:T(1024)S(1)} %pad_clamp_fusion.1), kind=kCustom, calls=%fused_computation | custom fusion | bytes 4195328 | tf_op jit(solution)/shard_map/jit(_take)/gather | solution.py:71
  6.1 12.9 %all-to-all-start = ((f32[256,16,128]{2,1,0:T(8,128)}), f32[256,16,128]{2,1,0:T(8,128)S(1)}, u32[]{:S(2)}, u32[]{:S(2)}) async-start(f32[256,16,128]{2,1,0:T(8,128)} %gather_fusion), calls=%async_computation | async-start | bytes 4194304 | tf_op jit(solution)/shard_map/all_to_all | solution.py:72
  19.0 0.8 broadcast_multiply_fusion
  19.7 0.1 copy.32
  19.8 0.1 eq.40
  19.9 0.1 copy.31
  20.0 0.1 mul.74
  20.1 0.0 copy-done
  20.2 0.2 convert_reduce_fusion
  20.4 49.2 %all-to-all-done = f32[256,16,128]{2,1,0:T(8,128)S(1)} async-done(((f32[256,16,128]{2,1,0:T(8,128)}), f32[256,16,128]{2,1,0:T(8,128)S(1)}, u32[]{:S(2)}, u32[]{:S(2)}) %all-to-all-start) | async-done | bytes 2097184 | tf_op jit(solution)/shard_map/all_to_all | solution.py:72
  69.6 0.8 gather_fusion.1
  70.4 0.1 slice.157
  70.5 1.4 %convolution_bitcast_fusion = f32[16,3,128]{2,0,1:T(8,128)S(1)} fusion(f32[3,4,16,128]{3,2,1,0:T(8,128)S(1)} %bitcast.60, f32[32,4,128,128]{3,2,1,0:T(8,128)} %param.6), kind=kOutput, calls=%fused_computation.5 | convolution fusion | flops 18874368 | bytes 909312 | tf_op jit(solution)/shard_map/iklc,ikcd->lid/dot_general | solution.py:82
  71.9 1.4 %convolution_bitcast_fusion.1 = f32[16,3,128]{2,0,1:T(8,128)S(1)} fusion(f32[3,4,16,128]{3,2,1,0:T(8,128)S(1)} %bitcast.59, f32[32,4,128,128]{3,2,1,0:T(8,128)} %param.6), kind=kOutput, calls=%fused_computation.6 | convolution fusion | flops 18874368 | bytes 909312 | tf_op jit(solution)/shard_map/iklc,ikcd->lid/dot_general | solution.py:82
  73.4 1.9 %collective-permute-start = (f32[17,3,128]{2,0,1:T(8,128)S(1)}, f32[17,3,128]{2,0,1:T(8,128)S(1)}, u32[]{:S(2)}, u32[]{:S(2)}) collective-permute-start(f32[17,3,128]{2,0,1:T(8,128)S(1)} %get-tuple-element.7), channel_id=1, source_target_pairs={{0,32},{32,64},{64,96},{96,128},{128,160},{160,192},{192,224},{1,3... | collective-permute-start | bytes 78344 | tf_op jit(solution)/shard_map/ppermute | solution.py:94
  75.3 4.0 %fusion.2 = f32[16,26,128]{2,0,1:T(8,128)S(1)} fusion(f32[26,4,16,128]{3,2,1,0:T(8,128)S(1)} %bitcast.58, f32[32,4,128,128]{3,2,1,0:T(8,128)} %param.6), kind=kOutput, calls=%fused_computation.4 | convolution fusion | flops 163577856 | bytes 7880704 | tf_op jit(solution)/shard_map/iklc,ikcd->lid/dot_general | solution.py:82
  79.3 3.6 %collective-permute-start.1 = (f32[17,3,128]{2,0,1:T(8,128)S(1)}, f32[17,3,128]{2,0,1:T(8,128)S(1)}, u32[]{:S(2)}, u32[]{:S(2)}) collective-permute-start(f32[17,3,128]{2,0,1:T(8,128)S(1)} %get-tuple-element.8), channel_id=1, source_target_pairs={{32,0},{64,32},{96,64},{128,96},{160,128},{192,160},{224,192},{33,... | collective-permute-start | bytes 78344 | tf_op jit(solution)/shard_map/ppermute | solution.py:95
  83.0 0.0 collective-permute-done
  83.1 1.5 %collective-permute-done.1 = f32[17,3,128]{2,0,1:T(8,128)S(1)} collective-permute-done((f32[17,3,128]{2,0,1:T(8,128)S(1)}, f32[17,3,128]{2,0,1:T(8,128)S(1)}, u32[]{:S(2)}, u32[]{:S(2)}) %collective-permute-start.1) | collective-permute-done | bytes 26144 | tf_op jit(solution)/shard_map/ppermute | solution.py:95
  84.6 0.2 slice_bitcast_fusion.1
  84.8 0.3 copy.33
  85.1 0.1 reshape.80
  85.2 1.9 %collective-permute-start.2 = (f32[16,128]{1,0:T(8,128)S(1)}, f32[16,128]{1,0:T(8,128)S(1)}, u32[]{:S(2)}, u32[]{:S(2)}) collective-permute-start(f32[16,128]{1,0:T(8,128)S(1)} %pad_bitcast_fusion.1), channel_id=1, source_target_pairs={{0,2},{2,4},{4,6},{6,8},{8,10},{10,12},{12,14},{14,16},{16,18},{18... | collective-permute-start | bytes 24584 | tf_op jit(solution)/shard_map/ppermute | solution.py:37
  87.1 0.3 copy.35
  87.4 0.1 reshape.84
  87.5 6.6 %collective-permute-start.3 = (f32[16,128]{1,0:T(8,128)S(1)}, f32[16,128]{1,0:T(8,128)S(1)}, u32[]{:S(2)}, u32[]{:S(2)}) collective-permute-start(f32[16,128]{1,0:T(8,128)S(1)} %pad_bitcast_fusion), channel_id=1, source_target_pairs={{2,0},{4,2},{6,4},{8,6},{10,8},{12,10},{14,12},{16,14},{18,16},{20... | collective-permute-start | bytes 24584 | tf_op jit(solution)/shard_map/ppermute | solution.py:38
  94.2 0.0 collective-permute-done.2
  94.2 0.1 reshape.83
  94.3 0.3 copy.34
  94.6 0.9 collective-permute-done.3
  95.5 0.1 reshape.87
  95.6 0.3 copy.36
  95.9 0.2 pad_maximum_fusion.4
  96.2 0.2 pad_maximum_fusion.1
  96.4 0.4 pad_maximum_fusion
  96.8 0.7 fusion.9
  97.5 0.7 fusion.12
  98.2 0.3 fusion.15
  98.5 0.8 copy.37
  (24 shorter events, 0.2 us)
Async XLA Ops:
  0.0 20.1 %copy-start = (f32[32,128]{1,0:T(8,128)S(1)}, f32[32,128]{1,0:T(8,128)}, u32[]{:S(2)}) copy-start(f32[32,128]{1,0:T(8,128)} %param.9) | copy-start | bytes 49156
  6.1 63.5 %all-to-all-start = ((f32[256,16,128]{2,1,0:T(8,128)}), f32[256,16,128]{2,1,0:T(8,128)S(1)}, u32[]{:S(2)}, u32[]{:S(2)}) async-start(f32[256,16,128]{2,1,0:T(8,128)} %gather_fusion), calls=%async_computation | async-start | bytes 4194304 | tf_op jit(solution)/shard_map/all_to_all | solution.py:72
  73.4 9.6 %collective-permute-start = (f32[17,3,128]{2,0,1:T(8,128)S(1)}, f32[17,3,128]{2,0,1:T(8,128)S(1)}, u32[]{:S(2)}, u32[]{:S(2)}) collective-permute-start(f32[17,3,128]{2,0,1:T(8,128)S(1)} %get-tuple-element.7), channel_id=1, source_target_pairs={{0,32},{32,64},{64,96},{96,128},{128,160},{160,192},{192,224},{1,3... | collective-permute-start | bytes 78344 | tf_op jit(solution)/shard_map/ppermute | solution.py:94
  79.3 5.3 %collective-permute-start.1 = (f32[17,3,128]{2,0,1:T(8,128)S(1)}, f32[17,3,128]{2,0,1:T(8,128)S(1)}, u32[]{:S(2)}, u32[]{:S(2)}) collective-permute-start(f32[17,3,128]{2,0,1:T(8,128)S(1)} %get-tuple-element.8), channel_id=1, source_target_pairs={{32,0},{64,32},{96,64},{128,96},{160,128},{192,160},{224,192},{33,... | collective-permute-start | bytes 78344 | tf_op jit(solution)/shard_map/ppermute | solution.py:95
  85.2 9.0 %collective-permute-start.2 = (f32[16,128]{1,0:T(8,128)S(1)}, f32[16,128]{1,0:T(8,128)S(1)}, u32[]{:S(2)}, u32[]{:S(2)}) collective-permute-start(f32[16,128]{1,0:T(8,128)S(1)} %pad_bitcast_fusion.1), channel_id=1, source_target_pairs={{0,2},{2,4},{4,6},{6,8},{8,10},{10,12},{12,14},{14,16},{16,18},{18... | collective-permute-start | bytes 24584 | tf_op jit(solution)/shard_map/ppermute | solution.py:37
  87.5 8.0 %collective-permute-start.3 = (f32[16,128]{1,0:T(8,128)S(1)}, f32[16,128]{1,0:T(8,128)S(1)}, u32[]{:S(2)}, u32[]{:S(2)}) collective-permute-start(f32[16,128]{1,0:T(8,128)S(1)} %pad_bitcast_fusion), channel_id=1, source_target_pairs={{2,0},{4,2},{6,4},{8,6},{10,8},{12,10},{14,12},{16,14},{18,16},{20... | collective-permute-start | bytes 24584 | tf_op jit(solution)/shard_map/ppermute | solution.py:38

commit v5 on v3

--- a/solution.py
+++ b/solution.py
@@ -7,36 +7,48 @@
 CAP = 2
 
 
-def with_halo(block, axis, dim, width):
-    count = lax.axis_size(axis)
-    forward = [(i, i + 1) for i in range(count - 1)]
-    backward = [(target, source) for source, target in forward]
-    low = lax.ppermute(
-        lax.slice_in_dim(block, block.shape[dim] - width, None, axis=dim), axis, forward
-    )
-    high = lax.ppermute(lax.slice_in_dim(block, 0, width, axis=dim), axis, backward)
-    return jnp.concatenate([low, block, high], axis=dim)
+def chain(count, step):
+    return [(i, i + step) for i in range(count) if 0 <= i + step < count]
 
 
-def packed_halo(block, axis, width):
-    count = lax.axis_size(axis)
-    forward = [(i, i + 1) for i in range(count - 1)]
-    backward = [(target, source) for source, target in forward]
+def pack(part):
+    size = part.size
+    padded = -(-size // 1024) * 1024
+    flat = jnp.transpose(part, (2, 0, 1)).reshape(size)
+    return jnp.pad(flat, (0, padded - size)).reshape(padded // 128, 128)
+
+
+def unpack(tile, shape):
+    channels, rows, cols = shape
+    flat = tile.reshape(tile.size)[: channels * rows * cols]
+    return jnp.transpose(flat.reshape(cols, channels, rows), (1, 2, 0))
+
+
+def with_halo(block, width):
+    nx, ny = lax.axis_size("gx"), lax.axis_size("gy")
     channels, rows, cols = block.shape
-    size = channels * rows * width
-    padded = -(-size // 1024) * 1024
+    w = width
+    low_r = lax.ppermute(block[:, rows - w:], "gx", chain(nx, 1))
+    high_r = lax.ppermute(block[:, :w], "gx", chain(nx, -1))
+    side = (channels, rows, w)
+    low_c = unpack(lax.ppermute(pack(block[:, :, cols - w:]), "gy", chain(ny, 1)), side)
+    high_c = unpack(lax.ppermute(pack(block[:, :, :w]), "gy", chain(ny, -1)), side)
 
-    def pack(part):
-        flat = jnp.transpose(part, (2, 0, 1)).reshape(size)
-        return jnp.pad(flat, (0, padded - size)).reshape(padded // 128, 128)
+    def corner(dx, dy):
+        part = block[:, rows - w:] if dx > 0 else block[:, :w]
+        part = part[:, :, cols - w:] if dy > 0 else part[:, :, :w]
+        pairs = [
+            (a * ny + b, (a + dx) * ny + b + dy)
+            for a in range(nx)
+            for b in range(ny)
+            if 0 <= a + dx < nx and 0 <= b + dy < ny
+        ]
+        return unpack(lax.ppermute(pack(part), ("gx", "gy"), pairs), (channels, w, w))
 
-    def unpack(tile):
-        flat = tile.reshape(padded)[:size]
-        return jnp.transpose(flat.reshape(width, channels, rows), (1, 2, 0))
-
-    low = unpack(lax.ppermute(pack(block[:, :, cols - width:]), axis, forward))
-    high = unpack(lax.ppermute(pack(block[:, :, :width]), axis, backward))
-    return jnp.concatenate([low, block, high], axis=2)
+    upper = jnp.concatenate([corner(1, 1), low_r, corner(1, -1)], axis=2)
+    centre = jnp.concatenate([low_c, block, high_c], axis=2)
+    lower = jnp.concatenate([corner(-1, 1), high_r, corner(-1, -1)], axis=2)
+    return jnp.concatenate([upper, centre, lower], axis=1)
 
 
 def smooth_step(values, gained):
@@ -77,13 +89,12 @@
     mine_slot = jnp.sum(earlier.astype(jnp.int32), axis=1)
     picked = jnp.take(incoming, mine * CAP + mine_slot, axis=0, mode="clip")
     picked = picked.reshape(frows, fanin, levels, block)
+
     field = jnp.einsum(
         "iklc,ikcd->lid", picked, remap_weights, precision=lax.Precision.HIGH
     )
 
-    carried = jnp.concatenate([field, smoothing[None]], axis=0)
-    carried = with_halo(carried, "gx", 1, PASSES)
-    carried = packed_halo(carried, "gy", PASSES)
+    carried = with_halo(jnp.concatenate([field, smoothing[None]], axis=0), PASSES)
     field, gain = carried[:levels], carried[levels:]
     for _ in range(PASSES):
         gain = gain[:, 1:-1, 1:-1]

time: 101 us -> 118 us (1.17)
  starting transfers between devices: 24.1 us -> 41.8 us
  waiting for transfers between devices: 58.5 us -> 54.7 us
  local copies, waits for them, and re-layouts: 7.84 us -> 10.3 us
    ppermute x4 -> x8, starting transfers between devices: 11.2 us -> 28.9 us  [the longest x4 15.1 us: corner(): lax.ppermute(pack(part), ('gx', 'gy'), pairs)]
    ppermute x4 -> x8, waiting for transfers between devices: 9.23 us -> 5.44 us  [the longest x4 5.43 us: corner(): lax.ppermute(pack(part), ('gx', 'gy'), pairs)]
    reshape x4 -> x12, local copies, waits for them, and re-layouts: 0.83 us -> 2.16 us  [unpack(): return jnp.transpose(flat.reshape(cols, channels, rows), (1, 2, 0))]
  transfers between devices with their start and end apart: 5 -> 9, of which waited for: 3 -> 2; matrix products, arithmetic and copies ran while one was open for 2% -> 4% of each run, Pallas kernels for 0% -> 0%
where the time goes in v5:
time: 118 us
  waiting for transfers between devices  54.7 us (46%)
  starting transfers between devices  41.8 us (35%)
  local copies, waits for them, and re-layouts  10.3 us (9%)
  other arithmetic  5.71 us (5%)
  matrix products  4.71 us (4%)
    all_to_all x1, waiting for transfers between devices, shards(): incoming = lax.all_to_all(outgoing, ('gx', 'gy'), 0, 0, tiled=True)  49.3 us
    ppermute x4, starting transfers between devices, corner(): lax.ppermute(pack(part), ('gx', 'gy'), pairs)  15.1 us
    all_to_all x1, starting transfers between devices, shards(): incoming = lax.all_to_all(outgoing, ('gx', 'gy'), 0, 0, tiled=True)  12.9 us
    ppermute x1, starting transfers between devices, with_halo(): lax.ppermute(pack(block[:, :, :w]), 'gy', chain(ny, -1))  6.07 us
    ppermute x4, waiting for transfers between devices, corner(): lax.ppermute(pack(part), ('gx', 'gy'), pairs)  5.43 us
    dot_general x1, matrix products, shards(): jnp.einsum('iklc,ikcd->lid', picked, remap_weights, precision=lax.Precisi...  4.71 us
    ppermute x1, starting transfers between devices, with_halo(): low_r = lax.ppermute(block[:, rows - w:], 'gx', chain(nx, 1))  3.31 us
    ppermute x1, starting transfers between devices, with_halo(): high_r = lax.ppermute(block[:, :w], 'gx', chain(nx, -1))  2.47 us
  transfers between devices with their start and end apart: 9, of which 2 were waited for; matrix products, arithmetic and copies ran while one was open for 4% of the time, Pallas kernels for 0%

profile of v5, /device:TPU:10, one launch (start us, length us, event | category | flops | bytes accessed | tf_op | source)
XLA Modules:
  0.0 117.6 jit_solution(8557072656417688642)
XLA Ops:
  0.0 0.9 fusion.20
  0.9 0.1 reshape.153
  1.0 0.1 copy.33
  1.1 1.1 copy.58
  2.2 0.9 select_reduce_fusion
  3.1 0.1 broadcast_in_dim.32
  3.2 0.1 copy.35
  3.2 0.1 reduce_window_sum.11
  3.3 0.1 copy.32
  3.4 0.1 copy.36
  3.6 0.1 reshape.156
  3.7 2.4 %gather_fusion = f32[256,16,128]{2,1,0:T(8,128)} fusion(f32[32,16,128]{2,1,0:T(8,128)S(1)} %bitcast.62, s32[1024]{0:T(1024)S(1)} %pad_clamp_fusion.1), kind=kCustom, calls=%fused_computation | custom fusion | bytes 4195328 | tf_op jit(solution)/shard_map/jit(_take)/gather | solution.py:83
  6.1 12.9 %all-to-all-start = ((f32[256,16,128]{2,1,0:T(8,128)}), f32[256,16,128]{2,1,0:T(8,128)S(1)}, u32[]{:S(2)}, u32[]{:S(2)}) async-start(f32[256,16,128]{2,1,0:T(8,128)} %gather_fusion), calls=%async_computation | async-start | bytes 4194304 | tf_op jit(solution)/shard_map/all_to_all | solution.py:84
  19.0 0.8 broadcast_multiply_fusion
  19.7 0.1 copy.37
  19.8 0.1 mul.72
  19.9 0.1 copy.38
  20.0 0.1 eq.40
  20.1 0.2 convert_reduce_fusion
  20.3 49.3 %all-to-all-done = f32[256,16,128]{2,1,0:T(8,128)S(1)} async-done(((f32[256,16,128]{2,1,0:T(8,128)}), f32[256,16,128]{2,1,0:T(8,128)S(1)}, u32[]{:S(2)}, u32[]{:S(2)}) %all-to-all-start) | async-done | bytes 2097184 | tf_op jit(solution)/shard_map/all_to_all | solution.py:84
  69.6 0.8 gather_fusion.1
  70.4 4.7 %convolution_bitcast_fusion = f32[16,32,128]{2,0,1:T(8,128)S(1)} fusion(f32[32,4,16,128]{3,2,1,0:T(8,128)S(1)} %bitcast.69, f32[32,4,128,128]{3,2,1,0:T(8,128)} %param.6), kind=kOutput, calls=%fused_computation.2 | convolution fusion | flops 201326592 | bytes 9699328 | tf_op jit(solution)/shard_map/iklc,ikcd->lid/dot_general | solution.py:93
  75.1 0.1 maximum_bitcast_fusion.1
  75.2 0.2 fusion.7
  75.4 0.3 copy.49
  75.6 0.1 reshape.149
  75.8 4.9 %collective-permute-start.7 = (f32[8,128]{1,0:T(8,128)S(1)}, f32[8,128]{1,0:T(8,128)S(1)}, u32[]{:S(2)}, u32[]{:S(2)}) collective-permute-start(f32[8,128]{1,0:T(8,128)S(1)} %pad_bitcast_fusion.2), channel_id=1, source_target_pairs={{34,0},{36,2},{38,4},{40,6},{42,8},{44,10},{46,12},{48,14},{50,16}... | collective-permute-start | bytes 12296 | tf_op jit(solution)/shard_map/ppermute | solution.py:46
  80.7 2.5 %collective-permute-start.6 = (f32[17,3,128]{2,0,1:T(8,128)S(1)}, f32[17,3,128]{2,0,1:T(8,128)S(1)}, u32[]{:S(2)}, u32[]{:S(2)}) collective-permute-start(f32[17,3,128]{2,0,1:T(8,128)S(1)} %get-tuple-element.14), channel_id=1, source_target_pairs={{32,0},{64,32},{96,64},{128,96},{160,128},{192,160},{224,192},{33,... | collective-permute-start | bytes 78344 | tf_op jit(solution)/shard_map/ppermute | solution.py:32
  83.2 0.3 copy.47
  83.4 0.1 reshape.145
  83.6 1.9 %collective-permute-start.5 = (f32[8,128]{1,0:T(8,128)S(1)}, f32[8,128]{1,0:T(8,128)S(1)}, u32[]{:S(2)}, u32[]{:S(2)}) collective-permute-start(f32[8,128]{1,0:T(8,128)S(1)} %pad_bitcast_fusion.3), channel_id=1, source_target_pairs={{32,2},{34,4},{36,6},{38,8},{40,10},{42,12},{44,14},{46,16},{48,18... | collective-permute-start | bytes 12296 | tf_op jit(solution)/shard_map/ppermute | solution.py:46
  85.5 0.2 copy.45
  85.7 0.1 reshape.141
  85.8 6.1 %collective-permute-start.4 = (f32[16,128]{1,0:T(8,128)S(1)}, f32[16,128]{1,0:T(8,128)S(1)}, u32[]{:S(2)}, u32[]{:S(2)}) collective-permute-start(f32[16,128]{1,0:T(8,128)S(1)} %pad_bitcast_fusion), channel_id=1, source_target_pairs={{2,0},{4,2},{6,4},{8,6},{10,8},{12,10},{14,12},{16,14},{18,16},{20... | collective-permute-start | bytes 24584 | tf_op jit(solution)/shard_map/ppermute | solution.py:35
  91.9 0.2 copy.43
  92.1 0.1 reshape.137
  92.2 1.9 %collective-permute-start.3 = (f32[16,128]{1,0:T(8,128)S(1)}, f32[16,128]{1,0:T(8,128)S(1)}, u32[]{:S(2)}, u32[]{:S(2)}) collective-permute-start(f32[16,128]{1,0:T(8,128)S(1)} %pad_bitcast_fusion.1), channel_id=1, source_target_pairs={{0,2},{2,4},{4,6},{6,8},{8,10},{10,12},{12,14},{14,16},{16,18},{18... | collective-permute-start | bytes 24584 | tf_op jit(solution)/shard_map/ppermute | solution.py:34
  94.1 0.3 copy.41
  94.4 0.1 reshape.133
  94.5 0.3 copy.39
  94.8 0.1 reshape.129
  94.9 6.3 %collective-permute-start.2 = (f32[8,128]{1,0:T(8,128)S(1)}, f32[8,128]{1,0:T(8,128)S(1)}, u32[]{:S(2)}, u32[]{:S(2)}) collective-permute-start(f32[8,128]{1,0:T(8,128)S(1)} %pad_bitcast_fusion.4), channel_id=1, source_target_pairs={{2,32},{4,34},{6,36},{8,38},{10,40},{12,42},{14,44},{16,46},{18,48... | collective-permute-start | bytes 12296 | tf_op jit(solution)/shard_map/ppermute | solution.py:46
  101.3 3.3 %collective-permute-start.1 = (f32[17,3,128]{2,0,1:T(8,128)S(1)}, f32[17,3,128]{2,0,1:T(8,128)S(1)}, u32[]{:S(2)}, u32[]{:S(2)}) collective-permute-start(f32[17,3,128]{2,0,1:T(8,128)S(1)} %get-tuple-element.13), channel_id=1, source_target_pairs={{0,32},{32,64},{64,96},{96,128},{128,160},{160,192},{192,224},{1,3... | collective-permute-start | bytes 78344 | tf_op jit(solution)/shard_map/ppermute | solution.py:31
  104.6 1.9 %collective-permute-start = (f32[8,128]{1,0:T(8,128)S(1)}, f32[8,128]{1,0:T(8,128)S(1)}, u32[]{:S(2)}, u32[]{:S(2)}) collective-permute-start(f32[8,128]{1,0:T(8,128)S(1)} %pad_bitcast_fusion.5), channel_id=1, source_target_pairs={{0,34},{2,36},{4,38},{6,40},{8,42},{10,44},{12,46},{14,48},{16,50}... | collective-permute-start | bytes 12296 | tf_op jit(solution)/shard_map/ppermute | solution.py:46
  106.6 0.1 reshape.152
  106.7 0.3 copy.50
  106.9 0.1 reshape.148
  107.1 0.3 copy.48
  107.3 0.1 reshape.136
  107.5 0.3 copy.42
  107.7 5.4 %collective-permute-done = f32[8,128]{1,0:T(8,128)S(1)} collective-permute-done((f32[8,128]{1,0:T(8,128)S(1)}, f32[8,128]{1,0:T(8,128)S(1)}, u32[]{:S(2)}, u32[]{:S(2)}) %collective-permute-start) | collective-permute-done | bytes 4128 | tf_op jit(solution)/shard_map/ppermute | solution.py:46
  113.1 0.1 reshape.132
  113.3 0.3 copy.40
  113.5 0.1 reshape.144
  113.6 0.2 copy.46
  113.9 0.1 reshape.140
  113.9 0.2 copy.44
  114.2 0.2 maximum_maximum_fusion.1
  114.5 0.2 maximum_maximum_fusion.2
  114.7 0.4 maximum_maximum_fusion
  115.1 0.7 fusion.2
  115.8 0.7 fusion.5
  116.5 0.3 fusion.12
  116.8 0.8 copy.51
  (29 shorter events, 0.2 us)
Async XLA Ops:
  6.1 63.5 %all-to-all-start = ((f32[256,16,128]{2,1,0:T(8,128)}), f32[256,16,128]{2,1,0:T(8,128)S(1)}, u32[]{:S(2)}, u32[]{:S(2)}) async-start(f32[256,16,128]{2,1,0:T(8,128)} %gather_fusion), calls=%async_computation | async-start | bytes 4194304 | tf_op jit(solution)/shard_map/all_to_all | solution.py:84
  70.4 4.7 %copy-start = (f32[32,128]{1,0:T(8,128)S(1)}, f32[32,128]{1,0:T(8,128)}, u32[]{:S(2)}) copy-start(f32[32,128]{1,0:T(8,128)} %param.9) | copy-start | bytes 49156
  75.8 19.2 %collective-permute-start.7 = (f32[8,128]{1,0:T(8,128)S(1)}, f32[8,128]{1,0:T(8,128)S(1)}, u32[]{:S(2)}, u32[]{:S(2)}) collective-permute-start(f32[8,128]{1,0:T(8,128)S(1)} %pad_bitcast_fusion.2), channel_id=1, source_target_pairs={{34,0},{36,2},{38,4},{40,6},{42,8},{44,10},{46,12},{48,14},{50,16}... | collective-permute-start | bytes 12296 | tf_op jit(solution)/shard_map/ppermute | solution.py:46
  80.7 33.5 %collective-permute-start.6 = (f32[17,3,128]{2,0,1:T(8,128)S(1)}, f32[17,3,128]{2,0,1:T(8,128)S(1)}, u32[]{:S(2)}, u32[]{:S(2)}) collective-permute-start(f32[17,3,128]{2,0,1:T(8,128)S(1)} %get-tuple-element.14), channel_id=1, source_target_pairs={{32,0},{64,32},{96,64},{128,96},{160,128},{192,160},{224,192},{33,... | collective-permute-start | bytes 78344 | tf_op jit(solution)/shard_map/ppermute | solution.py:32
  83.6 17.7 %collective-permute-start.5 = (f32[8,128]{1,0:T(8,128)S(1)}, f32[8,128]{1,0:T(8,128)S(1)}, u32[]{:S(2)}, u32[]{:S(2)}) collective-permute-start(f32[8,128]{1,0:T(8,128)S(1)} %pad_bitcast_fusion.3), channel_id=1, source_target_pairs={{32,2},{34,4},{36,6},{38,8},{40,10},{42,12},{44,14},{46,16},{48,18... | collective-permute-start | bytes 12296 | tf_op jit(solution)/shard_map/ppermute | solution.py:46
  85.8 27.7 %collective-permute-start.4 = (f32[16,128]{1,0:T(8,128)S(1)}, f32[16,128]{1,0:T(8,128)S(1)}, u32[]{:S(2)}, u32[]{:S(2)}) collective-permute-start(f32[16,128]{1,0:T(8,128)S(1)} %pad_bitcast_fusion), channel_id=1, source_target_pairs={{2,0},{4,2},{6,4},{8,6},{10,8},{12,10},{14,12},{16,14},{18,16},{20... | collective-permute-start | bytes 24584 | tf_op jit(solution)/shard_map/ppermute | solution.py:35
  92.2 21.7 %collective-permute-start.3 = (f32[16,128]{1,0:T(8,128)S(1)}, f32[16,128]{1,0:T(8,128)S(1)}, u32[]{:S(2)}, u32[]{:S(2)}) collective-permute-start(f32[16,128]{1,0:T(8,128)S(1)} %pad_bitcast_fusion.1), channel_id=1, source_target_pairs={{0,2},{2,4},{4,6},{6,8},{8,10},{10,12},{12,14},{14,16},{16,18},{18... | collective-permute-start | bytes 24584 | tf_op jit(solution)/shard_map/ppermute | solution.py:34
  94.9 9.7 %collective-permute-start.2 = (f32[8,128]{1,0:T(8,128)S(1)}, f32[8,128]{1,0:T(8,128)S(1)}, u32[]{:S(2)}, u32[]{:S(2)}) collective-permute-start(f32[8,128]{1,0:T(8,128)S(1)} %pad_bitcast_fusion.4), channel_id=1, source_target_pairs={{2,32},{4,34},{6,36},{8,38},{10,40},{12,42},{14,44},{16,46},{18,48... | collective-permute-start | bytes 12296 | tf_op jit(solution)/shard_map/ppermute | solution.py:46
  101.3 12.9 %collective-permute-start.1 = (f32[17,3,128]{2,0,1:T(8,128)S(1)}, f32[17,3,128]{2,0,1:T(8,128)S(1)}, u32[]{:S(2)}, u32[]{:S(2)}) collective-permute-start(f32[17,3,128]{2,0,1:T(8,128)S(1)} %get-tuple-element.13), channel_id=1, source_target_pairs={{0,32},{32,64},{64,96},{96,128},{128,160},{160,192},{192,224},{1,3... | collective-permute-start | bytes 78344 | tf_op jit(solution)/shard_map/ppermute | solution.py:31
  104.6 8.5 %collective-permute-start = (f32[8,128]{1,0:T(8,128)S(1)}, f32[8,128]{1,0:T(8,128)S(1)}, u32[]{:S(2)}, u32[]{:S(2)}) collective-permute-start(f32[8,128]{1,0:T(8,128)S(1)} %pad_bitcast_fusion.5), channel_id=1, source_target_pairs={{0,34},{2,36},{4,38},{6,40},{8,42},{10,44},{12,46},{14,48},{16,50}... | collective-permute-start | bytes 12296 | tf_op jit(solution)/shard_map/ppermute | solution.py:46

commit v6 on v4

--- a/solution.py
+++ b/solution.py
@@ -67,8 +67,8 @@
     slot_ids = jnp.arange(CAP, dtype=jnp.int32)
     chosen = jnp.logical_and(hit[:, None, :] > 0, slot[:, None, :] == slot_ids[None, :, None])
     send_row = jnp.sum(jnp.where(chosen, lat[:, None, :], 0), axis=2).reshape(devices * CAP)
-    rows_first = jnp.transpose(source, (1, 0, 2))
-    outgoing = jnp.take(rows_first, send_row, axis=0, mode="clip")
+    onehot = (send_row[:, None] == jnp.arange(source.shape[1])[None, :]).astype(source.dtype)
+    outgoing = jnp.einsum("jr,lrc->jlc", onehot, source, precision=lax.Precision.HIGHEST)
     incoming = lax.all_to_all(outgoing, ("gx", "gy"), 0, 0, tiled=True)
 
     mine = lax.dynamic_slice_in_dim(ids_t, myself * frows, frows, axis=1).T.reshape(frows * fanin)

time: 101 us -> 101 us (level)
  matrix products: 6.9 us -> 7.93 us
    dot_general x0 -> x1, local copies, waits for them, and re-layouts: none -> 2.57 us  [shards(): jnp.einsum('jr,lrc->jlc', onehot, source, precision=lax.Precision.HIGHEST)]
    gather x1 -> x0, local copies, waits for them, and re-layouts: 2.36 us -> none  [shards(): outgoing = jnp.take(rows_first, send_row, axis=0, mode='clip')]
    unnamed x8 -> x9, local copies, waits for them, and re-layouts: 1.14 us -> 0.03 us
    dot_general x0 -> x1, matrix products: none -> 1.03 us  [shards(): jnp.einsum('jr,lrc->jlc', onehot, source, precision=lax.Precision.HIGHEST)]
where the time goes in v6:
time: 101 us; the launch traced here: 99.5 us
  waiting for transfers between devices  51.6 us (51%)
  starting transfers between devices  27 us (27%)
  matrix products  7.93 us (8%)
  local copies, waits for them, and re-layouts  7.05 us (7%)
  other arithmetic  5.54 us (5%)
    all_to_all x1, waiting for transfers between devices, shards(): incoming = lax.all_to_all(outgoing, ('gx', 'gy'), 0, 0, tiled=True)  49.2 us
    all_to_all x1, starting transfers between devices, shards(): incoming = lax.all_to_all(outgoing, ('gx', 'gy'), 0, 0, tiled=True)  12.9 us
    dot_general x3, matrix products, remap(): jnp.einsum('iklc,ikcd->lid', picked[lo:hi], remap_weights[lo:hi], precisi...  6.9 us
    ppermute x1, starting transfers between devices, packed_halo(): high = unpack(lax.ppermute(pack(block[:, :, :width]), axis, backward))  6.62 us
    ppermute x1, starting transfers between devices, shards(): high = lax.ppermute(top, 'gx', backward)  3.64 us
    dot_general x1, local copies, waits for them, and re-layouts, shards(): jnp.einsum('jr,lrc->jlc', onehot, source, precision=lax.Precision.HIGHEST)  2.57 us
  transfers between devices with their start and end apart: 5, of which 3 were waited for; matrix products, arithmetic and copies ran while one was open for 6% of the time, Pallas kernels for 0%

profile of v6, /device:TPU:10, one launch (start us, length us, event | category | flops | bytes accessed | tf_op | source)
XLA Modules:
  0.0 99.5 jit_solution(17953918235519311847)
XLA Ops:
  0.0 0.0 copy-start
  0.0 0.0 copy-start.1
  0.0 0.9 fusion.23
  1.0 0.1 reshape.87
  1.0 0.1 copy.37
  1.1 0.1 reduce_window_sum.11
  1.2 0.1 copy.36
  1.3 0.9 select_reduce_fusion
  2.2 0.1 broadcast_in_dim.35
  2.3 0.1 copy.39
  2.4 0.1 copy.40
  2.5 0.1 eq.55
  2.6 0.0 copy-done
  2.6 1.0 %fusion.19 = f32[256,16,128]{2,0,1:T(8,128)S(1)} fusion(f32[16,32,128]{2,1,0:T(8,128)S(1)} %copy-done, s32[256]{0:T(256)S(1)} %eq.55), kind=kOutput, calls=%fused_computation.47 | convolution fusion | flops 201334784 | bytes 2360320 | tf_op jit(solution)/shard_map/jr,lrc->jlc/dot_general | solution.py:71
  3.7 2.6 %copy.41 = f32[256,16,128]{2,1,0:T(8,128)} copy(f32[256,16,128]{2,0,1:T(8,128)S(1)} %fusion.19) | data formatting | bytes 4194304 | tf_op jit(solution)/shard_map/jr,lrc->jlc/dot_general | solution.py:71
  6.2 12.9 %all-to-all-start = ((f32[256,16,128]{2,1,0:T(8,128)}), f32[256,16,128]{2,1,0:T(8,128)S(1)}, u32[]{:S(2)}, u32[]{:S(2)}) async-start(f32[256,16,128]{2,1,0:T(8,128)} %copy.41), calls=%async_computation | async-start | bytes 4194304 | tf_op jit(solution)/shard_map/all_to_all | solution.py:72
  19.1 0.8 broadcast_multiply_fusion
  19.9 0.1 copy.43
  20.0 0.1 eq.59
  20.1 0.1 copy.42
  20.2 0.1 mul.74
  20.3 0.0 copy-done.1
  20.4 0.2 convert_reduce_fusion
  20.6 49.2 %all-to-all-done = f32[256,16,128]{2,1,0:T(8,128)S(1)} async-done(((f32[256,16,128]{2,1,0:T(8,128)}), f32[256,16,128]{2,1,0:T(8,128)S(1)}, u32[]{:S(2)}, u32[]{:S(2)}) %all-to-all-start) | async-done | bytes 2097184 | tf_op jit(solution)/shard_map/all_to_all | solution.py:72
  69.8 0.8 gather_fusion
  70.6 0.1 slice.155
  70.6 1.4 %convolution_bitcast_fusion = f32[16,3,128]{2,0,1:T(8,128)S(1)} fusion(f32[3,4,16,128]{3,2,1,0:T(8,128)S(1)} %bitcast.60, f32[32,4,128,128]{3,2,1,0:T(8,128)} %param.6), kind=kOutput, calls=%fused_computation.4 | convolution fusion | flops 18874368 | bytes 909312 | tf_op jit(solution)/shard_map/iklc,ikcd->lid/dot_general | solution.py:82
  72.1 1.4 %convolution_bitcast_fusion.1 = f32[16,3,128]{2,0,1:T(8,128)S(1)} fusion(f32[3,4,16,128]{3,2,1,0:T(8,128)S(1)} %bitcast.59, f32[32,4,128,128]{3,2,1,0:T(8,128)} %param.6), kind=kOutput, calls=%fused_computation.5 | convolution fusion | flops 18874368 | bytes 909312 | tf_op jit(solution)/shard_map/iklc,ikcd->lid/dot_general | solution.py:82
  73.5 1.9 %collective-permute-start = (f32[17,3,128]{2,0,1:T(8,128)S(1)}, f32[17,3,128]{2,0,1:T(8,128)S(1)}, u32[]{:S(2)}, u32[]{:S(2)}) collective-permute-start(f32[17,3,128]{2,0,1:T(8,128)S(1)} %get-tuple-element.7), channel_id=1, source_target_pairs={{0,32},{32,64},{64,96},{96,128},{128,160},{160,192},{192,224},{1,3... | collective-permute-start | bytes 78344 | tf_op jit(solution)/shard_map/ppermute | solution.py:94
  75.4 4.0 %fusion.2 = f32[16,26,128]{2,0,1:T(8,128)S(1)} fusion(f32[26,4,16,128]{3,2,1,0:T(8,128)S(1)} %bitcast.58, f32[32,4,128,128]{3,2,1,0:T(8,128)} %param.6), kind=kOutput, calls=%fused_computation.3 | convolution fusion | flops 163577856 | bytes 7880704 | tf_op jit(solution)/shard_map/iklc,ikcd->lid/dot_general | solution.py:82
  79.5 3.6 %collective-permute-start.1 = (f32[17,3,128]{2,0,1:T(8,128)S(1)}, f32[17,3,128]{2,0,1:T(8,128)S(1)}, u32[]{:S(2)}, u32[]{:S(2)}) collective-permute-start(f32[17,3,128]{2,0,1:T(8,128)S(1)} %get-tuple-element.8), channel_id=1, source_target_pairs={{32,0},{64,32},{96,64},{128,96},{160,128},{192,160},{224,192},{33,... | collective-permute-start | bytes 78344 | tf_op jit(solution)/shard_map/ppermute | solution.py:95
  83.1 0.0 collective-permute-done
  83.2 1.5 %collective-permute-done.1 = f32[17,3,128]{2,0,1:T(8,128)S(1)} collective-permute-done((f32[17,3,128]{2,0,1:T(8,128)S(1)}, f32[17,3,128]{2,0,1:T(8,128)S(1)}, u32[]{:S(2)}, u32[]{:S(2)}) %collective-permute-start.1) | collective-permute-done | bytes 26144 | tf_op jit(solution)/shard_map/ppermute | solution.py:95
  84.8 0.2 slice_bitcast_fusion.1
  84.9 0.3 copy.44
  85.2 0.1 reshape.79
  85.4 1.9 %collective-permute-start.2 = (f32[16,128]{1,0:T(8,128)S(1)}, f32[16,128]{1,0:T(8,128)S(1)}, u32[]{:S(2)}, u32[]{:S(2)}) collective-permute-start(f32[16,128]{1,0:T(8,128)S(1)} %pad_bitcast_fusion.1), channel_id=1, source_target_pairs={{0,2},{2,4},{4,6},{6,8},{8,10},{10,12},{12,14},{14,16},{16,18},{18... | collective-permute-start | bytes 24584 | tf_op jit(solution)/shard_map/ppermute | solution.py:37
  87.3 0.3 copy.46
  87.6 0.1 reshape.83
  87.7 6.6 %collective-permute-start.3 = (f32[16,128]{1,0:T(8,128)S(1)}, f32[16,128]{1,0:T(8,128)S(1)}, u32[]{:S(2)}, u32[]{:S(2)}) collective-permute-start(f32[16,128]{1,0:T(8,128)S(1)} %pad_bitcast_fusion), channel_id=1, source_target_pairs={{2,0},{4,2},{6,4},{8,6},{10,8},{12,10},{14,12},{16,14},{18,16},{20... | collective-permute-start | bytes 24584 | tf_op jit(solution)/shard_map/ppermute | solution.py:38
  94.4 0.0 collective-permute-done.2
  94.4 0.1 reshape.82
  94.5 0.3 copy.45
  94.8 0.9 collective-permute-done.3
  95.7 0.1 reshape.86
  95.8 0.3 copy.47
  96.1 0.2 pad_maximum_fusion.4
  96.3 0.2 pad_maximum_fusion.1
  96.5 0.4 pad_maximum_fusion
  97.0 0.7 fusion.9
  97.7 0.7 fusion.12
  98.3 0.3 fusion.15
  98.7 0.8 copy.48
  (23 shorter events, 0.2 us)
Async XLA Ops:
  0.0 2.6 %copy-start = (f32[16,32,128]{2,1,0:T(8,128)S(1)}, f32[16,32,128]{2,1,0:T(8,128)}, u32[]{:S(2)}) copy-start(f32[16,32,128]{2,1,0:T(8,128)} %param.5) | copy-start | bytes 786436
  0.0 20.3 %copy-start.1 = (f32[32,128]{1,0:T(8,128)S(1)}, f32[32,128]{1,0:T(8,128)}, u32[]{:S(2)}) copy-start(f32[32,128]{1,0:T(8,128)} %param.9) | copy-start | bytes 49156
  6.2 63.5 %all-to-all-start = ((f32[256,16,128]{2,1,0:T(8,128)}), f32[256,16,128]{2,1,0:T(8,128)S(1)}, u32[]{:S(2)}, u32[]{:S(2)}) async-start(f32[256,16,128]{2,1,0:T(8,128)} %copy.41), calls=%async_computation | async-start | bytes 4194304 | tf_op jit(solution)/shard_map/all_to_all | solution.py:72
  73.5 9.6 %collective-permute-start = (f32[17,3,128]{2,0,1:T(8,128)S(1)}, f32[17,3,128]{2,0,1:T(8,128)S(1)}, u32[]{:S(2)}, u32[]{:S(2)}) collective-permute-start(f32[17,3,128]{2,0,1:T(8,128)S(1)} %get-tuple-element.7), channel_id=1, source_target_pairs={{0,32},{32,64},{64,96},{96,128},{128,160},{160,192},{192,224},{1,3... | collective-permute-start | bytes 78344 | tf_op jit(solution)/shard_map/ppermute | solution.py:94
  79.5 5.3 %collective-permute-start.1 = (f32[17,3,128]{2,0,1:T(8,128)S(1)}, f32[17,3,128]{2,0,1:T(8,128)S(1)}, u32[]{:S(2)}, u32[]{:S(2)}) collective-permute-start(f32[17,3,128]{2,0,1:T(8,128)S(1)} %get-tuple-element.8), channel_id=1, source_target_pairs={{32,0},{64,32},{96,64},{128,96},{160,128},{192,160},{224,192},{33,... | collective-permute-start | bytes 78344 | tf_op jit(solution)/shard_map/ppermute | solution.py:95
  85.4 9.0 %collective-permute-start.2 = (f32[16,128]{1,0:T(8,128)S(1)}, f32[16,128]{1,0:T(8,128)S(1)}, u32[]{:S(2)}, u32[]{:S(2)}) collective-permute-start(f32[16,128]{1,0:T(8,128)S(1)} %pad_bitcast_fusion.1), channel_id=1, source_target_pairs={{0,2},{2,4},{4,6},{6,8},{8,10},{10,12},{12,14},{14,16},{16,18},{18... | collective-permute-start | bytes 24584 | tf_op jit(solution)/shard_map/ppermute | solution.py:37
  87.7 8.0 %collective-permute-start.3 = (f32[16,128]{1,0:T(8,128)S(1)}, f32[16,128]{1,0:T(8,128)S(1)}, u32[]{:S(2)}, u32[]{:S(2)}) collective-permute-start(f32[16,128]{1,0:T(8,128)S(1)} %pad_bitcast_fusion), channel_id=1, source_target_pairs={{2,0},{4,2},{6,4},{8,6},{10,8},{12,10},{14,12},{16,14},{18,16},{20... | collective-permute-start | bytes 24584 | tf_op jit(solution)/shard_map/ppermute | solution.py:38

commit v7 on v4

--- a/solution.py
+++ b/solution.py
@@ -60,9 +60,9 @@
 
     ids_t = intersection_devices.T
     rows_t = intersection_rows.T
-    hit_k = ids_t == myself
-    hit = jnp.any(hit_k, axis=0).astype(jnp.int32).reshape(devices, frows)
-    lat = jnp.sum(jnp.where(hit_k, rows_t, 0), axis=0).reshape(devices, frows)
+    code = jnp.sum(jnp.where(ids_t == myself, rows_t + 1, 0), axis=0).reshape(devices, frows)
+    hit = (code > 0).astype(jnp.int32)
+    lat = code - 1
     slot = jnp.cumsum(hit, axis=1) - hit
     slot_ids = jnp.arange(CAP, dtype=jnp.int32)
     chosen = jnp.logical_and(hit[:, None, :] > 0, slot[:, None, :] == slot_ids[None, :, None])

time: 101 us -> 99.7 us (0.987)
  no operation moved by 1% of the time
where the time goes in v7:
time: 99.7 us; the launch traced here: 98.5 us
  waiting for transfers between devices  51.6 us (52%)
  starting transfers between devices  27 us (27%)
  local copies, waits for them, and re-layouts  7.96 us (8%)
  matrix products  6.9 us (7%)
  other arithmetic  4.63 us (5%)
    all_to_all x1, waiting for transfers between devices, shards(): incoming = lax.all_to_all(outgoing, ('gx', 'gy'), 0, 0, tiled=True)  49.2 us
    all_to_all x1, starting transfers between devices, shards(): incoming = lax.all_to_all(outgoing, ('gx', 'gy'), 0, 0, tiled=True)  12.9 us
    dot_general x3, matrix products, remap(): jnp.einsum('iklc,ikcd->lid', picked[lo:hi], remap_weights[lo:hi], precisi...  6.9 us
    ppermute x1, starting transfers between devices, packed_halo(): high = unpack(lax.ppermute(pack(block[:, :, :width]), axis, backward))  6.62 us
    ppermute x1, starting transfers between devices, shards(): high = lax.ppermute(top, 'gx', backward)  3.64 us
    gather x1, local copies, waits for them, and re-layouts, shards(): outgoing = jnp.take(rows_first, send_row, axis=0, mode='clip')  2.36 us
  transfers between devices with their start and end apart: 5, of which 3 were waited for; matrix products, arithmetic and copies ran while one was open for 6% of the time, Pallas kernels for 0%

profile of v7, /device:TPU:10, one launch (start us, length us, event | category | flops | bytes accessed | tf_op | source)
XLA Modules:
  0.0 98.5 jit_solution(2475704541589017478)
XLA Ops:
  0.0 0.0 copy-start
  0.0 0.9 select_reduce_fusion
  1.0 0.1 reshape.95
  1.0 0.1 copy.27
  1.1 0.1 reduce_window_sum.11
  1.2 0.1 copy.26
  1.3 0.1 sub.24
  1.4 0.1 copy.29
  1.5 0.1 copy.30
  1.6 0.1 reshape.98
  1.8 1.1 %copy.46 = f32[16,32,128]{2,0,1:T(8,128)S(1)} copy(f32[16,32,128]{2,1,0:T(8,128)} %param.5) | data formatting | bytes 524288 | tf_op args[0]
  2.9 2.4 %gather_fusion = f32[256,16,128]{2,1,0:T(8,128)} fusion(f32[32,16,128]{2,1,0:T(8,128)S(1)} %bitcast.51, s32[1024]{0:T(1024)S(1)} %pad_clamp_fusion.1), kind=kCustom, calls=%fused_computation | custom fusion | bytes 4195328 | tf_op jit(solution)/shard_map/jit(_take)/gather | solution.py:71
  5.2 12.9 %all-to-all-start = ((f32[256,16,128]{2,1,0:T(8,128)}), f32[256,16,128]{2,1,0:T(8,128)S(1)}, u32[]{:S(2)}, u32[]{:S(2)}) async-start(f32[256,16,128]{2,1,0:T(8,128)} %gather_fusion), calls=%async_computation | async-start | bytes 4194304 | tf_op jit(solution)/shard_map/all_to_all | solution.py:72
  18.1 0.8 broadcast_multiply_fusion
  18.9 0.1 copy.32
  19.0 0.1 eq.40
  19.1 0.1 copy.31
  19.2 0.1 mul.74
  19.3 0.0 copy-done
  19.3 0.2 convert_reduce_fusion
  19.5 49.2 %all-to-all-done = f32[256,16,128]{2,1,0:T(8,128)S(1)} async-done(((f32[256,16,128]{2,1,0:T(8,128)}), f32[256,16,128]{2,1,0:T(8,128)S(1)}, u32[]{:S(2)}, u32[]{:S(2)}) %all-to-all-start) | async-done | bytes 2097184 | tf_op jit(solution)/shard_map/all_to_all | solution.py:72
  68.7 0.8 gather_fusion.1
  69.5 0.1 slice.157
  69.6 1.4 %convolution_bitcast_fusion = f32[16,3,128]{2,0,1:T(8,128)S(1)} fusion(f32[3,4,16,128]{3,2,1,0:T(8,128)S(1)} %bitcast.60, f32[32,4,128,128]{3,2,1,0:T(8,128)} %param.6), kind=kOutput, calls=%fused_computation.5 | convolution fusion | flops 18874368 | bytes 909312 | tf_op jit(solution)/shard_map/iklc,ikcd->lid/dot_general | solution.py:82
  71.0 1.4 %convolution_bitcast_fusion.1 = f32[16,3,128]{2,0,1:T(8,128)S(1)} fusion(f32[3,4,16,128]{3,2,1,0:T(8,128)S(1)} %bitcast.59, f32[32,4,128,128]{3,2,1,0:T(8,128)} %param.6), kind=kOutput, calls=%fused_computation.6 | convolution fusion | flops 18874368 | bytes 909312 | tf_op jit(solution)/shard_map/iklc,ikcd->lid/dot_general | solution.py:82
  72.5 1.9 %collective-permute-start = (f32[17,3,128]{2,0,1:T(8,128)S(1)}, f32[17,3,128]{2,0,1:T(8,128)S(1)}, u32[]{:S(2)}, u32[]{:S(2)}) collective-permute-start(f32[17,3,128]{2,0,1:T(8,128)S(1)} %get-tuple-element.7), channel_id=1, source_target_pairs={{0,32},{32,64},{64,96},{96,128},{128,160},{160,192},{192,224},{1,3... | collective-permute-start | bytes 78344 | tf_op jit(solution)/shard_map/ppermute | solution.py:94
  74.4 4.0 %fusion.2 = f32[16,26,128]{2,0,1:T(8,128)S(1)} fusion(f32[26,4,16,128]{3,2,1,0:T(8,128)S(1)} %bitcast.58, f32[32,4,128,128]{3,2,1,0:T(8,128)} %param.6), kind=kOutput, calls=%fused_computation.4 | convolution fusion | flops 163577856 | bytes 7880704 | tf_op jit(solution)/shard_map/iklc,ikcd->lid/dot_general | solution.py:82
  78.5 3.6 %collective-permute-start.1 = (f32[17,3,128]{2,0,1:T(8,128)S(1)}, f32[17,3,128]{2,0,1:T(8,128)S(1)}, u32[]{:S(2)}, u32[]{:S(2)}) collective-permute-start(f32[17,3,128]{2,0,1:T(8,128)S(1)} %get-tuple-element.8), channel_id=1, source_target_pairs={{32,0},{64,32},{96,64},{128,96},{160,128},{192,160},{224,192},{33,... | collective-permute-start | bytes 78344 | tf_op jit(solution)/shard_map/ppermute | solution.py:95
  82.1 0.0 collective-permute-done
  82.2 1.5 %collective-permute-done.1 = f32[17,3,128]{2,0,1:T(8,128)S(1)} collective-permute-done((f32[17,3,128]{2,0,1:T(8,128)S(1)}, f32[17,3,128]{2,0,1:T(8,128)S(1)}, u32[]{:S(2)}, u32[]{:S(2)}) %collective-permute-start.1) | collective-permute-done | bytes 26144 | tf_op jit(solution)/shard_map/ppermute | solution.py:95
  83.7 0.2 slice_bitcast_fusion.1
  83.9 0.3 copy.33
  84.2 0.1 reshape.87
  84.3 1.9 %collective-permute-start.2 = (f32[16,128]{1,0:T(8,128)S(1)}, f32[16,128]{1,0:T(8,128)S(1)}, u32[]{:S(2)}, u32[]{:S(2)}) collective-permute-start(f32[16,128]{1,0:T(8,128)S(1)} %pad_bitcast_fusion.1), channel_id=1, source_target_pairs={{0,2},{2,4},{4,6},{6,8},{8,10},{10,12},{12,14},{14,16},{16,18},{18... | collective-permute-start | bytes 24584 | tf_op jit(solution)/shard_map/ppermute | solution.py:37
  86.3 0.3 copy.35
  86.5 0.1 reshape.91
  86.7 6.6 %collective-permute-start.3 = (f32[16,128]{1,0:T(8,128)S(1)}, f32[16,128]{1,0:T(8,128)S(1)}, u32[]{:S(2)}, u32[]{:S(2)}) collective-permute-start(f32[16,128]{1,0:T(8,128)S(1)} %pad_bitcast_fusion), channel_id=1, source_target_pairs={{2,0},{4,2},{6,4},{8,6},{10,8},{12,10},{14,12},{16,14},{18,16},{20... | collective-permute-start | bytes 24584 | tf_op jit(solution)/shard_map/ppermute | solution.py:38
  93.3 0.0 collective-permute-done.2
  93.3 0.1 reshape.90
  93.5 0.3 copy.34
  93.8 0.9 collective-permute-done.3
  94.7 0.1 reshape.94
  94.8 0.3 copy.36
  95.1 0.2 pad_maximum_fusion.4
  95.3 0.2 pad_maximum_fusion.1
  95.5 0.4 pad_maximum_fusion
  96.0 0.7 fusion.9
  96.7 0.7 fusion.12
  97.3 0.3 fusion.15
  97.7 0.8 copy.37
  (25 shorter events, 0.2 us)
Async XLA Ops:
  0.0 19.3 %copy-start = (f32[32,128]{1,0:T(8,128)S(1)}, f32[32,128]{1,0:T(8,128)}, u32[]{:S(2)}) copy-start(f32[32,128]{1,0:T(8,128)} %param.9) | copy-start | bytes 49156
  5.2 63.5 %all-to-all-start = ((f32[256,16,128]{2,1,0:T(8,128)}), f32[256,16,128]{2,1,0:T(8,128)S(1)}, u32[]{:S(2)}, u32[]{:S(2)}) async-start(f32[256,16,128]{2,1,0:T(8,128)} %gather_fusion), calls=%async_computation | async-start | bytes 4194304 | tf_op jit(solution)/shard_map/all_to_all | solution.py:72
  72.5 9.6 %collective-permute-start = (f32[17,3,128]{2,0,1:T(8,128)S(1)}, f32[17,3,128]{2,0,1:T(8,128)S(1)}, u32[]{:S(2)}, u32[]{:S(2)}) collective-permute-start(f32[17,3,128]{2,0,1:T(8,128)S(1)} %get-tuple-element.7), channel_id=1, source_target_pairs={{0,32},{32,64},{64,96},{96,128},{128,160},{160,192},{192,224},{1,3... | collective-permute-start | bytes 78344 | tf_op jit(solution)/shard_map/ppermute | solution.py:94
  78.5 5.3 %collective-permute-start.1 = (f32[17,3,128]{2,0,1:T(8,128)S(1)}, f32[17,3,128]{2,0,1:T(8,128)S(1)}, u32[]{:S(2)}, u32[]{:S(2)}) collective-permute-start(f32[17,3,128]{2,0,1:T(8,128)S(1)} %get-tuple-element.8), channel_id=1, source_target_pairs={{32,0},{64,32},{96,64},{128,96},{160,128},{192,160},{224,192},{33,... | collective-permute-start | bytes 78344 | tf_op jit(solution)/shard_map/ppermute | solution.py:95
  84.3 9.0 %collective-permute-start.2 = (f32[16,128]{1,0:T(8,128)S(1)}, f32[16,128]{1,0:T(8,128)S(1)}, u32[]{:S(2)}, u32[]{:S(2)}) collective-permute-start(f32[16,128]{1,0:T(8,128)S(1)} %pad_bitcast_fusion.1), channel_id=1, source_target_pairs={{0,2},{2,4},{4,6},{6,8},{8,10},{10,12},{12,14},{14,16},{16,18},{18... | collective-permute-start | bytes 24584 | tf_op jit(solution)/shard_map/ppermute | solution.py:37
  86.7 8.0 %collective-permute-start.3 = (f32[16,128]{1,0:T(8,128)S(1)}, f32[16,128]{1,0:T(8,128)S(1)}, u32[]{:S(2)}, u32[]{:S(2)}) collective-permute-start(f32[16,128]{1,0:T(8,128)S(1)} %pad_bitcast_fusion), channel_id=1, source_target_pairs={{2,0},{4,2},{6,4},{8,6},{10,8},{12,10},{14,12},{16,14},{18,16},{20... | collective-permute-start | bytes 24584 | tf_op jit(solution)/shard_map/ppermute | solution.py:38

commit v8 on v7

--- a/solution.py
+++ b/solution.py
@@ -86,10 +86,15 @@
     count = lax.axis_size("gx")
     forward = [(i, i + 1) for i in range(count - 1)]
     backward = [(target, source) for source, target in forward]
-    top = jnp.concatenate([remap(0, PASSES), smoothing[None, :PASSES]], axis=0)
-    bottom = jnp.concatenate(
-        [remap(frows - PASSES, frows), smoothing[None, frows - PASSES:]], axis=0
+    edge_rows = lambda a: jnp.concatenate([a[:PASSES], a[frows - PASSES:]], axis=0)
+    edges = jnp.einsum(
+        "iklc,ikcd->lid",
+        edge_rows(picked),
+        edge_rows(remap_weights),
+        precision=lax.Precision.HIGH,
     )
+    top = jnp.concatenate([edges[:, :PASSES], smoothing[None, :PASSES]], axis=0)
+    bottom = jnp.concatenate([edges[:, PASSES:], smoothing[None, frows - PASSES:]], axis=0)
     top, bottom = lax.optimization_barrier((top, bottom))
     low = lax.ppermute(bottom, "gx", forward)
     high = lax.ppermute(top, "gx", backward)

time: 99.7 us -> 98.7 us (0.990)
  local copies, waits for them, and re-layouts: 7.96 us -> 11.9 us
  waiting for transfers between devices: 51.6 us -> 49 us
  matrix products: 6.9 us -> 4.52 us
    dot_general x3 -> x1, matrix products: 6.9 us -> 4.04 us  [remap(): jnp.einsum('iklc,ikcd->lid', picked[lo:hi], remap_weights[lo:hi], precisi...]
    slice x0 -> x3, local copies, waits for them, and re-layouts: none -> 2.69 us  [the longest x2 2.68 us: shards(): a[:PASSES]]
    all_to_all x1, waiting for transfers between devices: 49.2 us -> 46.5 us  [shards(): incoming = lax.all_to_all(outgoing, ('gx', 'gy'), 0, 0, tiled=True)]
    unnamed x8 -> x12, local copies, waits for them, and re-layouts: 1.14 us -> 2.41 us
  transfers between devices with their start and end apart: 5 -> 5, of which waited for: 3 -> 3; matrix products, arithmetic and copies ran while one was open for 6% -> 9% of each run, Pallas kernels for 0% -> 0%
where the time goes in v8:
time: 98.7 us; the launch traced here: 97.5 us
  waiting for transfers between devices  49 us (50%)
  starting transfers between devices  27.1 us (27%)
  local copies, waits for them, and re-layouts  11.9 us (12%)
  other arithmetic  4.62 us (5%)
  matrix products  4.52 us (5%)
    all_to_all x1, waiting for transfers between devices, shards(): incoming = lax.all_to_all(outgoing, ('gx', 'gy'), 0, 0, tiled=True)  46.5 us
    all_to_all x1, starting transfers between devices, shards(): incoming = lax.all_to_all(outgoing, ('gx', 'gy'), 0, 0, tiled=True)  13 us
    ppermute x1, starting transfers between devices, packed_halo(): high = unpack(lax.ppermute(pack(block[:, :, :width]), axis, backward))  6.62 us
    dot_general x1, matrix products, remap(): jnp.einsum('iklc,ikcd->lid', picked[lo:hi], remap_weights[lo:hi], precisi...  4.04 us
    ppermute x1, starting transfers between devices, shards(): high = lax.ppermute(top, 'gx', backward)  3.64 us
    slice x2, local copies, waits for them, and re-layouts, shards(): a[:PASSES]  2.68 us
    unnamed x12, local copies, waits for them, and re-layouts  2.41 us
    gather x1, local copies, waits for them, and re-layouts, shards(): outgoing = jnp.take(rows_first, send_row, axis=0, mode='clip')  2.34 us
  transfers between devices with their start and end apart: 5, of which 3 were waited for; matrix products, arithmetic and copies ran while one was open for 9% of the time, Pallas kernels for 0%

profile of v8, /device:TPU:10, one launch (start us, length us, event | category | flops | bytes accessed | tf_op | source)
XLA Modules:
  0.0 97.5 jit_solution(6478735289652128989)
XLA Ops:
  0.0 0.9 select_reduce_fusion
  0.9 0.1 reshape.95
  1.0 0.1 copy.27
  1.1 0.1 reduce_window_sum.11
  1.2 0.1 copy.26
  1.3 0.1 sub.24
  1.4 0.1 copy.29
  1.5 0.1 copy.30
  1.6 0.1 reshape.98
  1.7 1.1 %copy.45 = f32[16,32,128]{2,0,1:T(8,128)S(1)} copy(f32[16,32,128]{2,1,0:T(8,128)} %param.5) | data formatting | bytes 524288 | tf_op args[0]
  2.9 2.3 %gather_fusion = f32[256,16,128]{2,1,0:T(8,128)} fusion(f32[32,16,128]{2,1,0:T(8,128)S(1)} %bitcast.44, s32[1024]{0:T(1024)S(1)} %pad_clamp_fusion.1), kind=kCustom, calls=%fused_computation | custom fusion | bytes 4195328 | tf_op jit(solution)/shard_map/jit(_take)/gather | solution.py:71
  5.2 0.0 copy-start.2
  5.2 13.0 %all-to-all-start = ((f32[256,16,128]{2,1,0:T(8,128)}), f32[256,16,128]{2,1,0:T(8,128)S(1)}, u32[]{:S(2)}, u32[]{:S(2)}) async-start(f32[256,16,128]{2,1,0:T(8,128)} %gather_fusion), calls=%async_computation | async-start | bytes 4194304 | tf_op jit(solution)/shard_map/all_to_all | solution.py:72
  18.2 0.8 broadcast_multiply_fusion
  19.0 0.1 copy.32
  19.1 0.1 eq.40
  19.2 0.1 copy.31
  19.3 0.1 mul.74
  19.4 0.0 copy-done.2
  19.4 0.2 convert_reduce_fusion
  19.6 2.7 %fusion.28 = (f32[3,4,128,128]{3,2,1,0:T(8,128)}, f32[3,4,128,128]{3,2,1,0:T(8,128)}) fusion(f32[32,4,128,128]{3,2,1,0:T(8,128)} %param.6), kind=kLoop, calls=%fused_computation.68 | loop fusion | bytes 3145728 | tf_op jit(solution)/shard_map/slice | solution.py:89
  22.3 46.5 %all-to-all-done = f32[256,16,128]{2,1,0:T(8,128)S(1)} async-done(((f32[256,16,128]{2,1,0:T(8,128)}), f32[256,16,128]{2,1,0:T(8,128)S(1)}, u32[]{:S(2)}, u32[]{:S(2)}) %all-to-all-start) | async-done | bytes 2097184 | tf_op jit(solution)/shard_map/all_to_all | solution.py:72
  68.8 0.8 gather_fusion.1
  69.6 0.0 copy-start
  69.6 0.0 copy-start.1
  69.7 0.1 slice.167
  69.7 1.0 %copy-done = f32[3,4,128,128]{3,2,1,0:T(8,128)S(1)} copy-done((f32[3,4,128,128]{3,2,1,0:T(8,128)S(1)}, f32[3,4,128,128]{3,2,1,0:T(8,128)}, u32[]{:S(2)}) %copy-start) | copy-done | bytes 786456
  70.7 0.2 copy-done.1
  71.0 0.5 fusion.9
  71.5 1.9 %collective-permute-start = (f32[17,3,128]{2,0,1:T(8,128)S(1)}, f32[17,3,128]{2,0,1:T(8,128)S(1)}, u32[]{:S(2)}, u32[]{:S(2)}) collective-permute-start(f32[17,3,128]{2,0,1:T(8,128)S(1)} %get-tuple-element.7), channel_id=1, source_target_pairs={{0,32},{32,64},{64,96},{96,128},{128,160},{160,192},{192,224},{1,3... | collective-permute-start | bytes 78344 | tf_op jit(solution)/shard_map/ppermute | solution.py:99
  73.4 4.0 %fusion.6 = f32[16,26,128]{2,0,1:T(8,128)S(1)} fusion(f32[26,4,16,128]{3,2,1,0:T(8,128)S(1)} %bitcast.51, f32[32,4,128,128]{3,2,1,0:T(8,128)} %param.6), kind=kOutput, calls=%fused_computation.8 | convolution fusion | flops 163577856 | bytes 7880704 | tf_op jit(solution)/shard_map/iklc,ikcd->lid/dot_general | solution.py:82
  77.5 3.6 %collective-permute-start.1 = (f32[17,3,128]{2,0,1:T(8,128)S(1)}, f32[17,3,128]{2,0,1:T(8,128)S(1)}, u32[]{:S(2)}, u32[]{:S(2)}) collective-permute-start(f32[17,3,128]{2,0,1:T(8,128)S(1)} %get-tuple-element.8), channel_id=1, source_target_pairs={{32,0},{64,32},{96,64},{128,96},{160,128},{192,160},{224,192},{33,... | collective-permute-start | bytes 78344 | tf_op jit(solution)/shard_map/ppermute | solution.py:100
  81.1 0.0 collective-permute-done
  81.2 1.5 %collective-permute-done.1 = f32[17,3,128]{2,0,1:T(8,128)S(1)} collective-permute-done((f32[17,3,128]{2,0,1:T(8,128)S(1)}, f32[17,3,128]{2,0,1:T(8,128)S(1)}, u32[]{:S(2)}, u32[]{:S(2)}) %collective-permute-start.1) | collective-permute-done | bytes 26144 | tf_op jit(solution)/shard_map/ppermute | solution.py:100
  82.8 0.2 slice_bitcast_fusion.1
  82.9 0.3 copy.33
  83.2 0.1 reshape.87
  83.4 1.9 %collective-permute-start.2 = (f32[16,128]{1,0:T(8,128)S(1)}, f32[16,128]{1,0:T(8,128)S(1)}, u32[]{:S(2)}, u32[]{:S(2)}) collective-permute-start(f32[16,128]{1,0:T(8,128)S(1)} %pad_bitcast_fusion.1), channel_id=1, source_target_pairs={{0,2},{2,4},{4,6},{6,8},{8,10},{10,12},{12,14},{14,16},{16,18},{18... | collective-permute-start | bytes 24584 | tf_op jit(solution)/shard_map/ppermute | solution.py:37
  85.3 0.3 copy.35
  85.6 0.1 reshape.91
  85.7 6.6 %collective-permute-start.3 = (f32[16,128]{1,0:T(8,128)S(1)}, f32[16,128]{1,0:T(8,128)S(1)}, u32[]{:S(2)}, u32[]{:S(2)}) collective-permute-start(f32[16,128]{1,0:T(8,128)S(1)} %pad_bitcast_fusion), channel_id=1, source_target_pairs={{2,0},{4,2},{6,4},{8,6},{10,8},{12,10},{14,12},{16,14},{18,16},{20... | collective-permute-start | bytes 24584 | tf_op jit(solution)/shard_map/ppermute | solution.py:38
  92.3 0.0 collective-permute-done.2
  92.4 0.1 reshape.90
  92.5 0.3 copy.34
  92.8 0.9 collective-permute-done.3
  93.7 0.1 reshape.94
  93.8 0.3 copy.36
  94.1 0.2 pad_maximum_fusion.4
  94.3 0.2 pad_maximum_fusion.1
  94.5 0.4 pad_maximum_fusion
  95.0 0.7 fusion.14
  95.7 0.7 fusion.17
  96.3 0.3 fusion.20
  96.7 0.8 copy.37
  (26 shorter events, 0.3 us)
Async XLA Ops:
  5.2 14.2 %copy-start.2 = (f32[32,128]{1,0:T(8,128)S(1)}, f32[32,128]{1,0:T(8,128)}, u32[]{:S(2)}) copy-start(f32[32,128]{1,0:T(8,128)} %param.9) | copy-start | bytes 49156
  5.2 63.7 %all-to-all-start = ((f32[256,16,128]{2,1,0:T(8,128)}), f32[256,16,128]{2,1,0:T(8,128)S(1)}, u32[]{:S(2)}, u32[]{:S(2)}) async-start(f32[256,16,128]{2,1,0:T(8,128)} %gather_fusion), calls=%async_computation | async-start | bytes 4194304 | tf_op jit(solution)/shard_map/all_to_all | solution.py:72
  69.6 1.1 %copy-start = (f32[3,4,128,128]{3,2,1,0:T(8,128)S(1)}, f32[3,4,128,128]{3,2,1,0:T(8,128)}, u32[]{:S(2)}) copy-start(f32[3,4,128,128]{3,2,1,0:T(8,128)} %get-tuple-element.11) | copy-start | bytes 2359300
  69.6 1.4 %copy-start.1 = (f32[3,4,128,128]{3,2,1,0:T(8,128)S(1)}, f32[3,4,128,128]{3,2,1,0:T(8,128)}, u32[]{:S(2)}) copy-start(f32[3,4,128,128]{3,2,1,0:T(8,128)} %get-tuple-element.12) | copy-start | bytes 2359300
  71.5 9.6 %collective-permute-start = (f32[17,3,128]{2,0,1:T(8,128)S(1)}, f32[17,3,128]{2,0,1:T(8,128)S(1)}, u32[]{:S(2)}, u32[]{:S(2)}) collective-permute-start(f32[17,3,128]{2,0,1:T(8,128)S(1)} %get-tuple-element.7), channel_id=1, source_target_pairs={{0,32},{32,64},{64,96},{96,128},{128,160},{160,192},{192,224},{1,3... | collective-permute-start | bytes 78344 | tf_op jit(solution)/shard_map/ppermute | solution.py:99
  77.5 5.3 %collective-permute-start.1 = (f32[17,3,128]{2,0,1:T(8,128)S(1)}, f32[17,3,128]{2,0,1:T(8,128)S(1)}, u32[]{:S(2)}, u32[]{:S(2)}) collective-permute-start(f32[17,3,128]{2,0,1:T(8,128)S(1)} %get-tuple-element.8), channel_id=1, source_target_pairs={{32,0},{64,32},{96,64},{128,96},{160,128},{192,160},{224,192},{33,... | collective-permute-start | bytes 78344 | tf_op jit(solution)/shard_map/ppermute | solution.py:100
  83.4 9.0 %collective-permute-start.2 = (f32[16,128]{1,0:T(8,128)S(1)}, f32[16,128]{1,0:T(8,128)S(1)}, u32[]{:S(2)}, u32[]{:S(2)}) collective-permute-start(f32[16,128]{1,0:T(8,128)S(1)} %pad_bitcast_fusion.1), channel_id=1, source_target_pairs={{0,2},{2,4},{4,6},{6,8},{8,10},{10,12},{12,14},{14,16},{16,18},{18... | collective-permute-start | bytes 24584 | tf_op jit(solution)/shard_map/ppermute | solution.py:37
  85.7 8.0 %collective-permute-start.3 = (f32[16,128]{1,0:T(8,128)S(1)}, f32[16,128]{1,0:T(8,128)S(1)}, u32[]{:S(2)}, u32[]{:S(2)}) collective-permute-start(f32[16,128]{1,0:T(8,128)S(1)} %pad_bitcast_fusion), channel_id=1, source_target_pairs={{2,0},{4,2},{6,4},{8,6},{10,8},{12,10},{14,12},{16,14},{18,16},{20... | collective-permute-start | bytes 24584 | tf_op jit(solution)/shard_map/ppermute | solution.py:38

commit v9 on v8

--- a/solution.py
+++ b/solution.py
@@ -86,6 +86,7 @@
     count = lax.axis_size("gx")
     forward = [(i, i + 1) for i in range(count - 1)]
     backward = [(target, source) for source, target in forward]
+    gain = packed_halo(with_halo(smoothing[None], "gx", 1, PASSES), "gy", PASSES)
     edge_rows = lambda a: jnp.concatenate([a[:PASSES], a[frows - PASSES:]], axis=0)
     edges = jnp.einsum(
         "iklc,ikcd->lid",
@@ -93,17 +94,12 @@
         edge_rows(remap_weights),
         precision=lax.Precision.HIGH,
     )
-    top = jnp.concatenate([edges[:, :PASSES], smoothing[None, :PASSES]], axis=0)
-    bottom = jnp.concatenate([edges[:, PASSES:], smoothing[None, frows - PASSES:]], axis=0)
-    top, bottom = lax.optimization_barrier((top, bottom))
+    top, bottom = lax.optimization_barrier((edges[:, :PASSES], edges[:, PASSES:]))
     low = lax.ppermute(bottom, "gx", forward)
     high = lax.ppermute(top, "gx", backward)
-    middle = jnp.concatenate(
-        [remap(PASSES, frows - PASSES), smoothing[None, PASSES:frows - PASSES]], axis=0
-    )
+    middle = remap(PASSES, frows - PASSES)
     carried = jnp.concatenate([low, top, middle, bottom, high], axis=1)
-    carried = packed_halo(carried, "gy", PASSES)
-    field, gain = carried[:levels], carried[levels:]
+    field = packed_halo(carried, "gy", PASSES)
     for _ in range(PASSES):
         gain = gain[:, 1:-1, 1:-1]
         field = smooth_step(field, gain)

time: 98.7 us -> 96.3 us (0.976)
  waiting for transfers between devices: 49 us -> 32.4 us
  starting transfers between devices: 27.1 us -> 41.3 us
  matrix products: 4.52 us -> 5.9 us
    all_to_all x1, waiting for transfers between devices: 46.5 us -> 12.6 us  [shards(): incoming = lax.all_to_all(outgoing, ('gx', 'gy'), 0, 0, tiled=True)]
    ppermute x1 -> x2, waiting for transfers between devices: 0.01 us -> 18.3 us  [packed_halo(): low = unpack(lax.ppermute(pack(block[:, :, cols - width:]), axis, forward))]
    ppermute x1 -> x2, starting transfers between devices: 6.62 us -> 12.3 us  [packed_halo(): high = unpack(lax.ppermute(pack(block[:, :, :width]), axis, backward))]
    ppermute x0 -> x2, starting transfers between devices: none -> 5.56 us  [the longest x1 3.43 us: with_halo(): lax.ppermute(lax.slice_in_dim(block, 0, width, axis=dim), axis, backward)]
    ppermute x1 -> x2, starting transfers between devices: 1.92 us -> 4.8 us  [packed_halo(): low = unpack(lax.ppermute(pack(block[:, :, cols - width:]), axis, forward))]
    ppermute x1, waiting for transfers between devices: 1.53 us -> 0.01 us  [shards(): high = lax.ppermute(top, 'gx', backward)]
    dot_general x1, matrix products: 0.49 us -> 1.86 us  [shards(): jnp.einsum('iklc,ikcd->lid', edge_rows(picked), edge_rows(remap_weights),...]
    unnamed x12 -> x6, local copies, waits for them, and re-layouts: 2.41 us -> 1.13 us
  transfers between devices with their start and end apart: 5 -> 9, of which waited for: 3 -> 4; matrix products, arithmetic and copies ran while one was open for 9% -> 10% of each run, Pallas kernels for 0% -> 0%
where the time goes in v9:
time: 96.3 us; the launch traced here: 95.3 us
  starting transfers between devices  41.3 us (43%)
  waiting for transfers between devices  32.4 us (34%)
  local copies, waits for them, and re-layouts  11.3 us (12%)
  matrix products  5.9 us (6%)
  other arithmetic  4.1 us (4%)
    ppermute x2, waiting for transfers between devices, packed_halo(): low = unpack(lax.ppermute(pack(block[:, :, cols - width:]), axis, forward))  18.3 us
    all_to_all x1, starting transfers between devices, shards(): incoming = lax.all_to_all(outgoing, ('gx', 'gy'), 0, 0, tiled=True)  13 us
    all_to_all x1, waiting for transfers between devices, shards(): incoming = lax.all_to_all(outgoing, ('gx', 'gy'), 0, 0, tiled=True)  12.6 us
    ppermute x2, starting transfers between devices, packed_halo(): high = unpack(lax.ppermute(pack(block[:, :, :width]), axis, backward))  12.3 us
    ppermute x2, starting transfers between devices, packed_halo(): low = unpack(lax.ppermute(pack(block[:, :, cols - width:]), axis, forward))  4.8 us
    dot_general x1, matrix products, remap(): jnp.einsum('iklc,ikcd->lid', picked[lo:hi], remap_weights[lo:hi], precisi...  4.04 us
    ppermute x1, starting transfers between devices, shards(): high = lax.ppermute(top, 'gx', backward)  3.64 us
    ppermute x1, starting transfers between devices, with_halo(): lax.ppermute(lax.slice_in_dim(block, 0, width, axis=dim), axis, backward)  3.43 us
  transfers between devices with their start and end apart: 9, of which 4 were waited for; matrix products, arithmetic and copies ran while one was open for 10% of the time, Pallas kernels for 0%

profile of v9, /device:TPU:10, one launch (start us, length us, event | category | flops | bytes accessed | tf_op | source)
XLA Modules:
  0.0 95.3 jit_solution(11608142367783858206)
XLA Ops:
  0.0 0.9 select_reduce_fusion
  0.9 0.1 reshape.128
  1.0 0.1 copy.35
  1.1 0.1 reduce_window_sum.11
  1.2 0.1 copy.34
  1.3 0.1 sub.24
  1.4 0.1 copy.37
  1.5 0.1 copy.38
  1.6 0.1 reshape.131
  1.7 1.1 %copy.53 = f32[16,32,128]{2,0,1:T(8,128)S(1)} copy(f32[16,32,128]{2,1,0:T(8,128)} %param.5) | data formatting | bytes 524288 | tf_op args[0]
  2.9 2.4 %gather_fusion = f32[256,16,128]{2,1,0:T(8,128)} fusion(f32[32,16,128]{2,1,0:T(8,128)S(1)} %bitcast.60, s32[1024]{0:T(1024)S(1)} %pad_clamp_fusion.1), kind=kCustom, calls=%fused_computation | custom fusion | bytes 4195328 | tf_op jit(solution)/shard_map/jit(_take)/gather | solution.py:71
  5.2 13.0 %all-to-all-start = ((f32[256,16,128]{2,1,0:T(8,128)}), f32[256,16,128]{2,1,0:T(8,128)S(1)}, u32[]{:S(2)}, u32[]{:S(2)}) async-start(f32[256,16,128]{2,1,0:T(8,128)} %gather_fusion), calls=%async_computation | async-start | bytes 4194304 | tf_op jit(solution)/shard_map/all_to_all | solution.py:72
  18.3 2.1 %collective-permute-start.4 = (f32[1,3,128]{2,1,0:T(4,128)S(1)}, f32[1,3,128]{2,1,0:T(4,128)S(1)}, u32[]{:S(2)}, u32[]{:S(2)}) collective-permute-start(f32[1,3,128]{2,1,0:T(4,128)S(1)} %get-tuple-element.21), channel_id=1, source_target_pairs={{0,32},{32,64},{64,96},{96,128},{128,160},{160,192},{192,224},{1,3... | collective-permute-start | bytes 4616 | tf_op jit(solution)/shard_map/ppermute | solution.py:14
  20.4 3.4 %collective-permute-start.5 = (f32[1,3,128]{2,1,0:T(4,128)S(1)}, f32[1,3,128]{2,1,0:T(4,128)S(1)}, u32[]{:S(2)}, u32[]{:S(2)}) collective-permute-start(f32[1,3,128]{2,1,0:T(4,128)S(1)} %get-tuple-element.22), channel_id=1, source_target_pairs={{32,0},{64,32},{96,64},{128,96},{160,128},{192,160},{224,192},{33,... | collective-permute-start | bytes 4616 | tf_op jit(solution)/shard_map/ppermute | solution.py:17
  23.8 0.8 broadcast_multiply_fusion
  24.6 0.1 copy.40
  24.7 0.1 eq.40
  24.8 0.1 copy.39
  24.9 0.1 mul.72
  25.0 0.2 convert_reduce_fusion
  25.2 2.7 %fusion.31 = (f32[3,4,128,128]{3,2,1,0:T(8,128)}, f32[3,4,128,128]{3,2,1,0:T(8,128)}) fusion(f32[32,4,128,128]{3,2,1,0:T(8,128)} %param.6), kind=kLoop, calls=%fused_computation.67 | loop fusion | bytes 3145728 | tf_op jit(solution)/shard_map/slice | solution.py:90
  27.9 0.0 collective-permute-done.4
  27.9 0.5 collective-permute-done.5
  28.4 0.1 slice_bitcast_fusion.5
  28.4 0.1 copy.45
  28.5 0.1 reshape.120
  28.6 2.9 %collective-permute-start.6 = (f32[8,128]{1,0:T(8,128)S(1)}, f32[8,128]{1,0:T(8,128)S(1)}, u32[]{:S(2)}, u32[]{:S(2)}) collective-permute-start(f32[8,128]{1,0:T(8,128)S(1)} %pad_bitcast_fusion.3), channel_id=1, source_target_pairs={{0,2},{2,4},{4,6},{6,8},{8,10},{10,12},{12,14},{14,16},{16,18},{18... | collective-permute-start | bytes 12296 | tf_op jit(solution)/shard_map/ppermute | solution.py:37
  31.5 0.1 copy.46
  31.6 0.1 reshape.124
  31.7 5.7 %collective-permute-start.7 = (f32[8,128]{1,0:T(8,128)S(1)}, f32[8,128]{1,0:T(8,128)S(1)}, u32[]{:S(2)}, u32[]{:S(2)}) collective-permute-start(f32[8,128]{1,0:T(8,128)S(1)} %pad_bitcast_fusion.2), channel_id=1, source_target_pairs={{2,0},{4,2},{6,4},{8,6},{10,8},{12,10},{14,12},{16,14},{18,16},{20... | collective-permute-start | bytes 12296 | tf_op jit(solution)/shard_map/ppermute | solution.py:38
  37.4 18.3 %collective-permute-done.6 = f32[8,128]{1,0:T(8,128)S(1)} collective-permute-done((f32[8,128]{1,0:T(8,128)S(1)}, f32[8,128]{1,0:T(8,128)S(1)}, u32[]{:S(2)}, u32[]{:S(2)}) %collective-permute-start.6) | collective-permute-done | bytes 4128 | tf_op jit(solution)/shard_map/ppermute | solution.py:37
  55.7 0.1 reshape.123
  55.8 0.1 copy.47
  55.9 0.0 collective-permute-done.7
  55.9 0.1 reshape.127
  56.0 0.1 copy.48
  56.1 0.1 pad_maximum_fusion.1
  56.2 12.6 %all-to-all-done = f32[256,16,128]{2,1,0:T(8,128)S(1)} async-done(((f32[256,16,128]{2,1,0:T(8,128)}), f32[256,16,128]{2,1,0:T(8,128)S(1)}, u32[]{:S(2)}, u32[]{:S(2)}) %all-to-all-start) | async-done | bytes 2097184 | tf_op jit(solution)/shard_map/all_to_all | solution.py:72
  68.9 0.8 gather_fusion.1
  69.7 1.9 %fusion.12 = f32[16,6,128]{2,0,1:T(8,128)S(1)} fusion(f32[3,4,128,128]{3,2,1,0:T(8,128)} %get-tuple-element.12, f32[3,4,128,128]{3,2,1,0:T(8,128)} %get-tuple-element.11, f32[3,4,16,128]{3,2,1,0:T(8,128)S(1)} %bitcast.65, f32[3,4,16,128]{3,2,1,0:T(8,128)S(1)} %bitcast.64), kind=kOutput, calls=%fused_computation.10 | convolution fusion | flops 38191104 | bytes 1818624 | tf_op jit(solution)/shard_map/iklc,ikcd->lid/dot_general | solution.py:91
  71.5 1.9 %collective-permute-start = (f32[16,3,128]{2,0,1:T(8,128)S(1)}, f32[16,3,128]{2,0,1:T(8,128)S(1)}, u32[]{:S(2)}, u32[]{:S(2)}) collective-permute-start(f32[16,3,128]{2,0,1:T(8,128)S(1)} %get-tuple-element.7), channel_id=1, source_target_pairs={{0,32},{32,64},{64,96},{96,128},{128,160},{160,192},{192,224},{1,3... | collective-permute-start | bytes 73736 | tf_op jit(solution)/shard_map/ppermute | solution.py:98
  73.5 0.1 slice_bitcast_fusion.3
  73.5 0.1 slice.167
  73.6 3.6 %collective-permute-start.1 = (f32[16,3,128]{2,0,1:T(8,128)S(1)}, f32[16,3,128]{2,0,1:T(8,128)S(1)}, u32[]{:S(2)}, u32[]{:S(2)}) collective-permute-start(f32[16,3,128]{2,0,1:T(8,128)S(1)} %get-tuple-element.8), channel_id=1, source_target_pairs={{32,0},{64,32},{96,64},{128,96},{160,128},{192,160},{224,192},{33,... | collective-permute-start | bytes 73736 | tf_op jit(solution)/shard_map/ppermute | solution.py:99
  77.3 0.0 collective-permute-done
  77.3 4.0 %fusion.9 = f32[16,38,128]{2,0,1:T(8,128)S(1)} fusion(f32[16,38,128]{2,0,1:T(8,128)S(1)} %constant_dynamic-update-slice_fusion.2, f32[26,4,16,128]{3,2,1,0:T(8,128)S(1)} %bitcast.61, f32[32,4,128,128]{3,2,1,0:T(8,128)} %param.6), kind=kOutput, calls=%fused_computation.9 | convolution fusion | flops 163577856 | bytes 7880704 | tf_op jit(solution)/shard_map/iklc,ikcd->lid/dot_general | solution.py:82
  81.4 0.2 slice_bitcast_fusion.1
  81.5 0.2 copy.41
  81.8 0.1 reshape.112
  81.9 1.9 %collective-permute-start.2 = (f32[16,128]{1,0:T(8,128)S(1)}, f32[16,128]{1,0:T(8,128)S(1)}, u32[]{:S(2)}, u32[]{:S(2)}) collective-permute-start(f32[16,128]{1,0:T(8,128)S(1)} %pad_bitcast_fusion.1), channel_id=1, source_target_pairs={{0,2},{2,4},{4,6},{6,8},{8,10},{10,12},{12,14},{14,16},{16,18},{18... | collective-permute-start | bytes 24584 | tf_op jit(solution)/shard_map/ppermute | solution.py:37
  83.8 0.2 copy.43
  84.0 0.1 reshape.116
  84.2 6.6 %collective-permute-start.3 = (f32[16,128]{1,0:T(8,128)S(1)}, f32[16,128]{1,0:T(8,128)S(1)}, u32[]{:S(2)}, u32[]{:S(2)}) collective-permute-start(f32[16,128]{1,0:T(8,128)S(1)} %pad_bitcast_fusion), channel_id=1, source_target_pairs={{2,0},{4,2},{6,4},{8,6},{10,8},{12,10},{14,12},{16,14},{18,16},{20... | collective-permute-start | bytes 24584 | tf_op jit(solution)/shard_map/ppermute | solution.py:38
  90.8 0.1 slice_bitcast_fusion.2
  90.9 0.1 reshape.115
  91.0 0.3 copy.42
  91.3 0.9 collective-permute-done.3
  92.1 0.1 reshape.119
  92.3 0.3 copy.44
  92.5 0.3 pad_maximum_fusion
  92.8 0.7 fusion.17
  93.5 0.6 fusion.20
  94.2 0.3 fusion.23
  94.5 0.8 copy.49
  (26 shorter events, 0.2 us)
Async XLA Ops:
  5.2 13.0 %copy-start = (f32[32,128]{1,0:T(8,128)S(1)}, f32[32,128]{1,0:T(8,128)}, u32[]{:S(2)}) copy-start(f32[32,128]{1,0:T(8,128)} %param.9) | copy-start | bytes 49156
  5.2 63.7 %all-to-all-start = ((f32[256,16,128]{2,1,0:T(8,128)}), f32[256,16,128]{2,1,0:T(8,128)S(1)}, u32[]{:S(2)}, u32[]{:S(2)}) async-start(f32[256,16,128]{2,1,0:T(8,128)} %gather_fusion), calls=%async_computation | async-start | bytes 4194304 | tf_op jit(solution)/shard_map/all_to_all | solution.py:72
  18.3 9.6 %collective-permute-start.4 = (f32[1,3,128]{2,1,0:T(4,128)S(1)}, f32[1,3,128]{2,1,0:T(4,128)S(1)}, u32[]{:S(2)}, u32[]{:S(2)}) collective-permute-start(f32[1,3,128]{2,1,0:T(4,128)S(1)} %get-tuple-element.21), channel_id=1, source_target_pairs={{0,32},{32,64},{64,96},{96,128},{128,160},{160,192},{192,224},{1,3... | collective-permute-start | bytes 4616 | tf_op jit(solution)/shard_map/ppermute | solution.py:14
  20.4 8.0 %collective-permute-start.5 = (f32[1,3,128]{2,1,0:T(4,128)S(1)}, f32[1,3,128]{2,1,0:T(4,128)S(1)}, u32[]{:S(2)}, u32[]{:S(2)}) collective-permute-start(f32[1,3,128]{2,1,0:T(4,128)S(1)} %get-tuple-element.22), channel_id=1, source_target_pairs={{32,0},{64,32},{96,64},{128,96},{160,128},{192,160},{224,192},{33,... | collective-permute-start | bytes 4616 | tf_op jit(solution)/shard_map/ppermute | solution.py:17
  28.6 27.1 %collective-permute-start.6 = (f32[8,128]{1,0:T(8,128)S(1)}, f32[8,128]{1,0:T(8,128)S(1)}, u32[]{:S(2)}, u32[]{:S(2)}) collective-permute-start(f32[8,128]{1,0:T(8,128)S(1)} %pad_bitcast_fusion.3), channel_id=1, source_target_pairs={{0,2},{2,4},{4,6},{6,8},{8,10},{10,12},{12,14},{14,16},{16,18},{18... | collective-permute-start | bytes 12296 | tf_op jit(solution)/shard_map/ppermute | solution.py:37
  31.7 24.2 %collective-permute-start.7 = (f32[8,128]{1,0:T(8,128)S(1)}, f32[8,128]{1,0:T(8,128)S(1)}, u32[]{:S(2)}, u32[]{:S(2)}) collective-permute-start(f32[8,128]{1,0:T(8,128)S(1)} %pad_bitcast_fusion.2), channel_id=1, source_target_pairs={{2,0},{4,2},{6,4},{8,6},{10,8},{12,10},{14,12},{16,14},{18,16},{20... | collective-permute-start | bytes 12296 | tf_op jit(solution)/shard_map/ppermute | solution.py:38
  71.5 5.7 %collective-permute-start = (f32[16,3,128]{2,0,1:T(8,128)S(1)}, f32[16,3,128]{2,0,1:T(8,128)S(1)}, u32[]{:S(2)}, u32[]{:S(2)}) collective-permute-start(f32[16,3,128]{2,0,1:T(8,128)S(1)} %get-tuple-element.7), channel_id=1, source_target_pairs={{0,32},{32,64},{64,96},{96,128},{128,160},{160,192},{192,224},{1,3... | collective-permute-start | bytes 73736 | tf_op jit(solution)/shard_map/ppermute | solution.py:98
  73.6 7.7 %collective-permute-start.1 = (f32[16,3,128]{2,0,1:T(8,128)S(1)}, f32[16,3,128]{2,0,1:T(8,128)S(1)}, u32[]{:S(2)}, u32[]{:S(2)}) collective-permute-start(f32[16,3,128]{2,0,1:T(8,128)S(1)} %get-tuple-element.8), channel_id=1, source_target_pairs={{32,0},{64,32},{96,64},{128,96},{160,128},{192,160},{224,192},{33,... | collective-permute-start | bytes 73736 | tf_op jit(solution)/shard_map/ppermute | solution.py:99
  81.9 9.0 %collective-permute-start.2 = (f32[16,128]{1,0:T(8,128)S(1)}, f32[16,128]{1,0:T(8,128)S(1)}, u32[]{:S(2)}, u32[]{:S(2)}) collective-permute-start(f32[16,128]{1,0:T(8,128)S(1)} %pad_bitcast_fusion.1), channel_id=1, source_target_pairs={{0,2},{2,4},{4,6},{6,8},{8,10},{10,12},{12,14},{14,16},{16,18},{18... | collective-permute-start | bytes 24584 | tf_op jit(solution)/shard_map/ppermute | solution.py:37
  84.2 8.0 %collective-permute-start.3 = (f32[16,128]{1,0:T(8,128)S(1)}, f32[16,128]{1,0:T(8,128)S(1)}, u32[]{:S(2)}, u32[]{:S(2)}) collective-permute-start(f32[16,128]{1,0:T(8,128)S(1)} %pad_bitcast_fusion), channel_id=1, source_target_pairs={{2,0},{4,2},{6,4},{8,6},{10,8},{12,10},{14,12},{16,14},{18,16},{20... | collective-permute-start | bytes 24584 | tf_op jit(solution)/shard_map/ppermute | solution.py:38

commit v10 on v9

--- a/solution.py
+++ b/solution.py
@@ -18,7 +18,7 @@
     return jnp.concatenate([low, block, high], axis=dim)
 
 
-def packed_halo(block, axis, width):
+def packed_strips(block, axis, width):
     count = lax.axis_size(axis)
     forward = [(i, i + 1) for i in range(count - 1)]
     backward = [(target, source) for source, target in forward]
@@ -36,6 +36,11 @@
 
     low = unpack(lax.ppermute(pack(block[:, :, cols - width:]), axis, forward))
     high = unpack(lax.ppermute(pack(block[:, :, :width]), axis, backward))
+    return low, high
+
+
+def packed_halo(block, axis, width):
+    low, high = packed_strips(block, axis, width)
     return jnp.concatenate([low, block, high], axis=2)
 
 
@@ -99,11 +104,23 @@
     high = lax.ppermute(top, "gx", backward)
     middle = remap(PASSES, frows - PASSES)
     carried = jnp.concatenate([low, top, middle, bottom, high], axis=1)
-    field = packed_halo(carried, "gy", PASSES)
-    for _ in range(PASSES):
-        gain = gain[:, 1:-1, 1:-1]
-        field = smooth_step(field, gain)
-    return field
+    low_c, high_c = packed_strips(carried, "gy", PASSES)
+
+    def passes(values, gained):
+        for step in range(1, PASSES + 1):
+            values = smooth_step(values, gained[:, step:gained.shape[1] - step, step:gained.shape[2] - step])
+        return values
+
+    cols = carried.shape[2]
+    inner = passes(carried, gain[:, :, PASSES:PASSES + cols])
+    left = passes(
+        jnp.concatenate([low_c, carried[:, :, :2 * PASSES]], axis=2), gain[:, :, :3 * PASSES]
+    )
+    right = passes(
+        jnp.concatenate([carried[:, :, cols - 2 * PASSES:], high_c], axis=2),
+        gain[:, :, cols - PASSES:],
+    )
+    return jnp.concatenate([left, inner, right], axis=2)
 
 
 def solution(mesh):

time: 96.3 us -> 97.5 us (1.012)
  other arithmetic: 4.1 us -> 6.21 us
  waiting for transfers between devices: 32.4 us -> 31 us
    add x3 -> x8, other arithmetic: 1.67 us -> 3.89 us  [smooth_step(): return values[:, 1:-1, 1:-1] + gained * laplace]
    ppermute x4, waiting for transfers between devices: 19.2 us -> 18.2 us  [the longest x2 18.2 us: packed_strips(): low = unpack(lax.ppermute(pack(block[:, :, cols - width:]), axis, forward))]
  transfers between devices with their start and end apart: 9 -> 9, of which waited for: 4 -> 3; matrix products, arithmetic and copies ran while one was open for 10% -> 12% of each run, Pallas kernels for 0% -> 0%
where the time goes in v10:
time: 97.5 us; the launch traced here: 96.6 us
  starting transfers between devices  41.3 us (42%)
  waiting for transfers between devices  31 us (32%)
  local copies, waits for them, and re-layouts  11.8 us (12%)
  other arithmetic  6.21 us (6%)
  matrix products  5.9 us (6%)
    ppermute x2, waiting for transfers between devices, packed_strips(): low = unpack(lax.ppermute(pack(block[:, :, cols - width:]), axis, forward))  18.2 us
    all_to_all x1, starting transfers between devices, shards(): incoming = lax.all_to_all(outgoing, ('gx', 'gy'), 0, 0, tiled=True)  13 us
    all_to_all x1, waiting for transfers between devices, shards(): incoming = lax.all_to_all(outgoing, ('gx', 'gy'), 0, 0, tiled=True)  12.5 us
    ppermute x2, starting transfers between devices, packed_strips(): high = unpack(lax.ppermute(pack(block[:, :, :width]), axis, backward))  12.1 us
    ppermute x2, starting transfers between devices, packed_strips(): low = unpack(lax.ppermute(pack(block[:, :, cols - width:]), axis, forward))  4.98 us
    dot_general x1, matrix products, remap(): jnp.einsum('iklc,ikcd->lid', picked[lo:hi], remap_weights[lo:hi], precisi...  4.04 us
    add x8, other arithmetic, smooth_step(): return values[:, 1:-1, 1:-1] + gained * laplace  3.89 us
    ppermute x1, starting transfers between devices, shards(): high = lax.ppermute(top, 'gx', backward)  3.64 us
  transfers between devices with their start and end apart: 9, of which 3 were waited for; matrix products, arithmetic and copies ran while one was open for 12% of the time, Pallas kernels for 0%

profile of v10, /device:TPU:10, one launch (start us, length us, event | category | flops | bytes accessed | tf_op | source)
XLA Modules:
  0.0 96.6 jit_solution(13924319898216565971)
XLA Ops:
  0.0 0.9 select_reduce_fusion
  0.9 0.1 reshape.127
  1.3 0.1 sub.42
  1.5 0.1 copy.75
  1.6 0.1 reshape.130
  1.7 1.1 %copy.96 = f32[16,32,128]{2,0,1:T(8,128)S(1)} copy(f32[16,32,128]{2,1,0:T(8,128)} %param.5) | data formatting | bytes 524288 | tf_op args[0]
  2.9 2.3 %gather_fusion = f32[256,16,128]{2,1,0:T(8,128)} fusion(f32[32,16,128]{2,1,0:T(8,128)S(1)} %bitcast.74, s32[1024]{0:T(1024)S(1)} %pad_clamp_fusion.1), kind=kCustom, calls=%fused_computation | custom fusion | bytes 4195328 | tf_op jit(solution)/shard_map/jit(_take)/gather | solution.py:76
  5.2 13.0 %all-to-all-start = ((f32[256,16,128]{2,1,0:T(8,128)}), f32[256,16,128]{2,1,0:T(8,128)S(1)}, u32[]{:S(2)}, u32[]{:S(2)}) async-start(f32[256,16,128]{2,1,0:T(8,128)} %gather_fusion), calls=%async_computation | async-start | bytes 4194304 | tf_op jit(solution)/shard_map/all_to_all | solution.py:77
  18.2 2.1 %collective-permute-start.3 = (f32[1,3,128]{2,1,0:T(4,128)S(1)}, f32[1,3,128]{2,1,0:T(4,128)S(1)}, u32[]{:S(2)}, u32[]{:S(2)}) collective-permute-start(f32[1,3,128]{2,1,0:T(4,128)S(1)} %get-tuple-element.27), channel_id=1, source_target_pairs={{0,32},{32,64},{64,96},{96,128},{128,160},{160,192},{192,224},{1,3... | collective-permute-start | bytes 4616 | tf_op jit(solution)/shard_map/ppermute | solution.py:14
  20.4 3.4 %collective-permute-start.4 = (f32[1,3,128]{2,1,0:T(4,128)S(1)}, f32[1,3,128]{2,1,0:T(4,128)S(1)}, u32[]{:S(2)}, u32[]{:S(2)}) collective-permute-start(f32[1,3,128]{2,1,0:T(4,128)S(1)} %get-tuple-element.28), channel_id=1, source_target_pairs={{32,0},{64,32},{96,64},{128,96},{160,128},{192,160},{224,192},{33,... | collective-permute-start | bytes 4616 | tf_op jit(solution)/shard_map/ppermute | solution.py:17
  23.8 0.8 broadcast_multiply_fusion
  24.6 0.1 copy.77
  24.7 0.1 eq.40
  24.8 0.1 copy.76
  24.9 0.1 mul.152
  25.0 0.2 convert_reduce_fusion
  25.3 2.7 %fusion.55 = (f32[3,4,128,128]{3,2,1,0:T(8,128)}, f32[3,4,128,128]{3,2,1,0:T(8,128)}) fusion(f32[32,4,128,128]{3,2,1,0:T(8,128)} %param.6), kind=kLoop, calls=%fused_computation.125 | loop fusion | bytes 3145728 | tf_op jit(solution)/shard_map/slice | solution.py:95
  28.0 0.3 collective-permute-done.4
  28.3 0.1 slice_bitcast_fusion.9
  28.4 0.1 copy.80
  28.5 0.1 reshape.115
  28.6 3.1 %collective-permute-start.5 = (f32[8,128]{1,0:T(8,128)S(1)}, f32[8,128]{1,0:T(8,128)S(1)}, u32[]{:S(2)}, u32[]{:S(2)}) collective-permute-start(f32[8,128]{1,0:T(8,128)S(1)} %pad_bitcast_fusion.3), channel_id=1, source_target_pairs={{0,2},{2,4},{4,6},{6,8},{8,10},{10,12},{12,14},{14,16},{16,18},{18... | collective-permute-start | bytes 12296 | tf_op jit(solution)/shard_map/ppermute | solution.py:37
  31.7 0.1 copy.86
  31.8 0.1 reshape.123
  31.9 5.5 %collective-permute-start.7 = (f32[8,128]{1,0:T(8,128)S(1)}, f32[8,128]{1,0:T(8,128)S(1)}, u32[]{:S(2)}, u32[]{:S(2)}) collective-permute-start(f32[8,128]{1,0:T(8,128)S(1)} %pad_bitcast_fusion.2), channel_id=1, source_target_pairs={{2,0},{4,2},{6,4},{8,6},{10,8},{12,10},{14,12},{16,14},{18,16},{20... | collective-permute-start | bytes 12296 | tf_op jit(solution)/shard_map/ppermute | solution.py:38
  37.4 0.1 slice_bitcast_fusion.6
  37.5 0.1 slice_bitcast_fusion.5
  37.5 18.2 %collective-permute-done.5 = f32[8,128]{1,0:T(8,128)S(1)} collective-permute-done((f32[8,128]{1,0:T(8,128)S(1)}, f32[8,128]{1,0:T(8,128)S(1)}, u32[]{:S(2)}, u32[]{:S(2)}) %collective-permute-start.5) | collective-permute-done | bytes 4128 | tf_op jit(solution)/shard_map/ppermute | solution.py:37
  55.7 0.1 reshape.118
  55.8 0.1 copy.81
  55.9 0.1 reshape.126
  56.0 0.1 copy.87
  56.1 0.1 maximum_maximum_fusion
  56.2 0.1 slice_bitcast_fusion.3
  56.3 0.1 slice_bitcast_fusion.2
  56.3 12.5 %all-to-all-done = f32[256,16,128]{2,1,0:T(8,128)S(1)} async-done(((f32[256,16,128]{2,1,0:T(8,128)}), f32[256,16,128]{2,1,0:T(8,128)S(1)}, u32[]{:S(2)}, u32[]{:S(2)}) %all-to-all-start) | async-done | bytes 2097184 | tf_op jit(solution)/shard_map/all_to_all | solution.py:77
  68.8 0.8 gather_fusion.1
  69.6 1.9 %fusion.12 = f32[16,6,128]{2,0,1:T(8,128)S(1)} fusion(f32[3,4,128,128]{3,2,1,0:T(8,128)} %get-tuple-element.12, f32[3,4,128,128]{3,2,1,0:T(8,128)} %get-tuple-element.11, f32[3,4,16,128]{3,2,1,0:T(8,128)S(1)} %bitcast.84, f32[3,4,16,128]{3,2,1,0:T(8,128)S(1)} %bitcast.83), kind=kOutput, calls=%fused_computation.10 | convolution fusion | flops 38191104 | bytes 1818624 | tf_op jit(solution)/shard_map/iklc,ikcd->lid/dot_general | solution.py:96
  71.5 1.9 %collective-permute-start = (f32[16,3,128]{2,0,1:T(8,128)S(1)}, f32[16,3,128]{2,0,1:T(8,128)S(1)}, u32[]{:S(2)}, u32[]{:S(2)}) collective-permute-start(f32[16,3,128]{2,0,1:T(8,128)S(1)} %get-tuple-element.7), channel_id=1, source_target_pairs={{0,32},{32,64},{64,96},{96,128},{128,160},{160,192},{192,224},{1,3... | collective-permute-start | bytes 73736 | tf_op jit(solution)/shard_map/ppermute | solution.py:103
  73.4 0.1 slice_bitcast_fusion.8
  73.6 3.6 %collective-permute-start.1 = (f32[16,3,128]{2,0,1:T(8,128)S(1)}, f32[16,3,128]{2,0,1:T(8,128)S(1)}, u32[]{:S(2)}, u32[]{:S(2)}) collective-permute-start(f32[16,3,128]{2,0,1:T(8,128)S(1)} %get-tuple-element.8), channel_id=1, source_target_pairs={{32,0},{64,32},{96,64},{128,96},{160,128},{192,160},{224,192},{33,... | collective-permute-start | bytes 73736 | tf_op jit(solution)/shard_map/ppermute | solution.py:104
  77.3 4.0 %fusion.9 = f32[16,38,128]{2,0,1:T(8,128)S(1)} fusion(f32[16,38,128]{2,0,1:T(8,128)S(1)} %constant_dynamic-update-slice_fusion.2, f32[26,4,16,128]{3,2,1,0:T(8,128)S(1)} %bitcast.75, f32[32,4,128,128]{3,2,1,0:T(8,128)} %param.6), kind=kOutput, calls=%fused_computation.9 | convolution fusion | flops 163577856 | bytes 7880704 | tf_op jit(solution)/shard_map/iklc,ikcd->lid/dot_general | solution.py:87
  81.3 0.2 slice_bitcast_fusion.1
  81.5 0.2 fusion.57
  81.7 0.2 copy.78
  81.9 0.1 reshape.111
  82.0 1.9 %collective-permute-start.2 = (f32[16,128]{1,0:T(8,128)S(1)}, f32[16,128]{1,0:T(8,128)S(1)}, u32[]{:S(2)}, u32[]{:S(2)}) collective-permute-start(f32[16,128]{1,0:T(8,128)S(1)} %pad_bitcast_fusion.1), channel_id=1, source_target_pairs={{0,2},{2,4},{4,6},{6,8},{8,10},{10,12},{12,14},{14,16},{16,18},{18... | collective-permute-start | bytes 24584 | tf_op jit(solution)/shard_map/ppermute | solution.py:37
  83.9 0.2 copy.84
  84.2 0.1 reshape.119
  84.3 6.6 %collective-permute-start.6 = (f32[16,128]{1,0:T(8,128)S(1)}, f32[16,128]{1,0:T(8,128)S(1)}, u32[]{:S(2)}, u32[]{:S(2)}) collective-permute-start(f32[16,128]{1,0:T(8,128)S(1)} %pad_bitcast_fusion), channel_id=1, source_target_pairs={{2,0},{4,2},{6,4},{8,6},{10,8},{12,10},{14,12},{16,14},{18,16},{20... | collective-permute-start | bytes 24584 | tf_op jit(solution)/shard_map/ppermute | solution.py:38
  90.9 0.4 fusion.23
  91.3 0.4 fusion.35
  91.7 0.3 fusion.44
  92.0 0.1 reshape.114
  92.1 0.3 copy.79
  92.4 0.1 reshape.122
  92.5 0.3 copy.85
  92.8 1.4 %fusion.18 = (f32[16,36,7]{2,0,1:T(8,128)S(1)}, f32[16,36,7]{2,0,1:T(8,128)S(1)}) fusion(f32[16,38,3]{2,0,1:T(8,128)S(1)} %bitcast.77, f32[16,38,6]{2,0,1:T(8,128)S(1)} %get-tuple-element.18, f32[36,7]{1,0:T(8,128)S(1)} %slice_bitcast_fusion.3, f32[16,38,6]{2,0,1:T(8,128)S(1)} %get-tuple-element.17, f32[16,38,3]{2,0,1:T(8,128)S(1)} %bitcast.76, ...), kind=kLoop, calls=%fused_computation.17 | loop fusion | flops 96768 | bytes 78048 | tf_op jit(solution)/shard_map/add | solution.py:55
  94.2 0.4 fusion.38
  94.6 0.3 fusion.47
  94.9 0.4 fusion.32
  95.3 0.3 fusion.41
  95.6 0.2 pad_maximum_fusion.2
  95.8 0.8 copy.90
  (37 shorter events, 0.7 us)
Async XLA Ops:
  5.2 13.0 %copy-start = (f32[32,128]{1,0:T(8,128)S(1)}, f32[32,128]{1,0:T(8,128)}, u32[]{:S(2)}) copy-start(f32[32,128]{1,0:T(8,128)} %param.9) | copy-start | bytes 49156
  5.2 63.7 %all-to-all-start = ((f32[256,16,128]{2,1,0:T(8,128)}), f32[256,16,128]{2,1,0:T(8,128)S(1)}, u32[]{:S(2)}, u32[]{:S(2)}) async-start(f32[256,16,128]{2,1,0:T(8,128)} %gather_fusion), calls=%async_computation | async-start | bytes 4194304 | tf_op jit(solution)/shard_map/all_to_all | solution.py:77
  18.2 9.8 %collective-permute-start.3 = (f32[1,3,128]{2,1,0:T(4,128)S(1)}, f32[1,3,128]{2,1,0:T(4,128)S(1)}, u32[]{:S(2)}, u32[]{:S(2)}) collective-permute-start(f32[1,3,128]{2,1,0:T(4,128)S(1)} %get-tuple-element.27), channel_id=1, source_target_pairs={{0,32},{32,64},{64,96},{96,128},{128,160},{160,192},{192,224},{1,3... | collective-permute-start | bytes 4616 | tf_op jit(solution)/shard_map/ppermute | solution.py:14
  20.4 8.0 %collective-permute-start.4 = (f32[1,3,128]{2,1,0:T(4,128)S(1)}, f32[1,3,128]{2,1,0:T(4,128)S(1)}, u32[]{:S(2)}, u32[]{:S(2)}) collective-permute-start(f32[1,3,128]{2,1,0:T(4,128)S(1)} %get-tuple-element.28), channel_id=1, source_target_pairs={{32,0},{64,32},{96,64},{128,96},{160,128},{192,160},{224,192},{33,... | collective-permute-start | bytes 4616 | tf_op jit(solution)/shard_map/ppermute | solution.py:17
  28.6 27.1 %collective-permute-start.5 = (f32[8,128]{1,0:T(8,128)S(1)}, f32[8,128]{1,0:T(8,128)S(1)}, u32[]{:S(2)}, u32[]{:S(2)}) collective-permute-start(f32[8,128]{1,0:T(8,128)S(1)} %pad_bitcast_fusion.3), channel_id=1, source_target_pairs={{0,2},{2,4},{4,6},{6,8},{8,10},{10,12},{12,14},{14,16},{16,18},{18... | collective-permute-start | bytes 12296 | tf_op jit(solution)/shard_map/ppermute | solution.py:37
  31.9 24.1 %collective-permute-start.7 = (f32[8,128]{1,0:T(8,128)S(1)}, f32[8,128]{1,0:T(8,128)S(1)}, u32[]{:S(2)}, u32[]{:S(2)}) collective-permute-start(f32[8,128]{1,0:T(8,128)S(1)} %pad_bitcast_fusion.2), channel_id=1, source_target_pairs={{2,0},{4,2},{6,4},{8,6},{10,8},{12,10},{14,12},{16,14},{18,16},{20... | collective-permute-start | bytes 12296 | tf_op jit(solution)/shard_map/ppermute | solution.py:38
  71.5 5.7 %collective-permute-start = (f32[16,3,128]{2,0,1:T(8,128)S(1)}, f32[16,3,128]{2,0,1:T(8,128)S(1)}, u32[]{:S(2)}, u32[]{:S(2)}) collective-permute-start(f32[16,3,128]{2,0,1:T(8,128)S(1)} %get-tuple-element.7), channel_id=1, source_target_pairs={{0,32},{32,64},{64,96},{96,128},{128,160},{160,192},{192,224},{1,3... | collective-permute-start | bytes 73736 | tf_op jit(solution)/shard_map/ppermute | solution.py:103
  73.6 7.7 %collective-permute-start.1 = (f32[16,3,128]{2,0,1:T(8,128)S(1)}, f32[16,3,128]{2,0,1:T(8,128)S(1)}, u32[]{:S(2)}, u32[]{:S(2)}) collective-permute-start(f32[16,3,128]{2,0,1:T(8,128)S(1)} %get-tuple-element.8), channel_id=1, source_target_pairs={{32,0},{64,32},{96,64},{128,96},{160,128},{192,160},{224,192},{33,... | collective-permute-start | bytes 73736 | tf_op jit(solution)/shard_map/ppermute | solution.py:104
  82.0 10.0 %collective-permute-start.2 = (f32[16,128]{1,0:T(8,128)S(1)}, f32[16,128]{1,0:T(8,128)S(1)}, u32[]{:S(2)}, u32[]{:S(2)}) collective-permute-start(f32[16,128]{1,0:T(8,128)S(1)} %pad_bitcast_fusion.1), channel_id=1, source_target_pairs={{0,2},{2,4},{4,6},{6,8},{8,10},{10,12},{12,14},{14,16},{16,18},{18... | collective-permute-start | bytes 24584 | tf_op jit(solution)/shard_map/ppermute | solution.py:37
  84.3 8.1 %collective-permute-start.6 = (f32[16,128]{1,0:T(8,128)S(1)}, f32[16,128]{1,0:T(8,128)S(1)}, u32[]{:S(2)}, u32[]{:S(2)}) collective-permute-start(f32[16,128]{1,0:T(8,128)S(1)} %pad_bitcast_fusion), channel_id=1, source_target_pairs={{2,0},{4,2},{6,4},{8,6},{10,8},{12,10},{14,12},{16,14},{18,16},{20... | collective-permute-start | bytes 24584 | tf_op jit(solution)/shard_map/ppermute | solution.py:38

commit v11 on v9

--- a/solution.py
+++ b/solution.py
@@ -96,8 +96,8 @@
     )
     top, bottom = lax.optimization_barrier((edges[:, :PASSES], edges[:, PASSES:]))
     low = lax.ppermute(bottom, "gx", forward)
+    top, middle = lax.optimization_barrier((top, remap(PASSES, frows - PASSES)))
     high = lax.ppermute(top, "gx", backward)
-    middle = remap(PASSES, frows - PASSES)
     carried = jnp.concatenate([low, top, middle, bottom, high], axis=1)
     field = packed_halo(carried, "gy", PASSES)
     for _ in range(PASSES):

time: 96.3 us -> 97.9 us (1.017)
  matrix products: 5.9 us -> 4.53 us
  waiting for transfers between devices: 32.4 us -> 33.7 us
  local copies, waits for them, and re-layouts: 11.3 us -> 12.6 us
    ppermute x1, waiting for transfers between devices: 0.01 us -> 1.43 us  [shards(): high = lax.ppermute(top, 'gx', backward)]
    dot_general x1, matrix products: 1.86 us -> 0.49 us  [shards(): jnp.einsum('iklc,ikcd->lid', edge_rows(picked), edge_rows(remap_weights),...]
    unnamed x6 -> x11, local copies, waits for them, and re-layouts: 1.13 us -> 2.41 us
  transfers between devices with their start and end apart: 9 -> 9, of which waited for: 4 -> 5; matrix products, arithmetic and copies ran while one was open for 10% -> 10% of each run, Pallas kernels for 0% -> 0%
where the time goes in v11:
time: 97.9 us; the launch traced here: 96.6 us
  starting transfers between devices  41.3 us (42%)
  waiting for transfers between devices  33.7 us (34%)
  local copies, waits for them, and re-layouts  12.6 us (13%)
  matrix products  4.53 us (5%)
  other arithmetic  4.1 us (4%)
    ppermute x2, waiting for transfers between devices, packed_halo(): low = unpack(lax.ppermute(pack(block[:, :, cols - width:]), axis, forward))  18.3 us
    all_to_all x1, starting transfers between devices, shards(): incoming = lax.all_to_all(outgoing, ('gx', 'gy'), 0, 0, tiled=True)  13 us
    all_to_all x1, waiting for transfers between devices, shards(): incoming = lax.all_to_all(outgoing, ('gx', 'gy'), 0, 0, tiled=True)  12.6 us
    ppermute x2, starting transfers between devices, packed_halo(): high = unpack(lax.ppermute(pack(block[:, :, :width]), axis, backward))  12.3 us
    ppermute x2, starting transfers between devices, packed_halo(): low = unpack(lax.ppermute(pack(block[:, :, cols - width:]), axis, forward))  4.8 us
    dot_general x1, matrix products, remap(): jnp.einsum('iklc,ikcd->lid', picked[lo:hi], remap_weights[lo:hi], precisi...  4.05 us
    ppermute x1, starting transfers between devices, shards(): high = lax.ppermute(top, 'gx', backward)  3.64 us
    ppermute x1, starting transfers between devices, with_halo(): lax.ppermute(lax.slice_in_dim(block, 0, width, axis=dim), axis, backward)  3.43 us
  transfers between devices with their start and end apart: 9, of which 5 were waited for; matrix products, arithmetic and copies ran while one was open for 10% of the time, Pallas kernels for 0%

profile of v11, /device:TPU:10, one launch (start us, length us, event | category | flops | bytes accessed | tf_op | source)
XLA Modules:
  0.0 96.6 jit_solution(2970810499647827987)
XLA Ops:
  0.0 0.9 select_reduce_fusion
  0.9 0.1 reshape.128
  1.0 0.1 copy.35
  1.1 0.1 reduce_window_sum.11
  1.2 0.1 copy.34
  1.3 0.1 sub.24
  1.4 0.1 copy.37
  1.5 0.1 copy.38
  1.6 0.1 reshape.131
  1.7 1.1 %copy.53 = f32[16,32,128]{2,0,1:T(8,128)S(1)} copy(f32[16,32,128]{2,1,0:T(8,128)} %param.5) | data formatting | bytes 524288 | tf_op args[0]
  2.9 2.4 %gather_fusion = f32[256,16,128]{2,1,0:T(8,128)} fusion(f32[32,16,128]{2,1,0:T(8,128)S(1)} %bitcast.58, s32[1024]{0:T(1024)S(1)} %pad_clamp_fusion.1), kind=kCustom, calls=%fused_computation | custom fusion | bytes 4195328 | tf_op jit(solution)/shard_map/jit(_take)/gather | solution.py:71
  5.2 13.0 %all-to-all-start = ((f32[256,16,128]{2,1,0:T(8,128)}), f32[256,16,128]{2,1,0:T(8,128)S(1)}, u32[]{:S(2)}, u32[]{:S(2)}) async-start(f32[256,16,128]{2,1,0:T(8,128)} %gather_fusion), calls=%async_computation | async-start | bytes 4194304 | tf_op jit(solution)/shard_map/all_to_all | solution.py:72
  18.2 2.1 %collective-permute-start.4 = (f32[1,3,128]{2,1,0:T(4,128)S(1)}, f32[1,3,128]{2,1,0:T(4,128)S(1)}, u32[]{:S(2)}, u32[]{:S(2)}) collective-permute-start(f32[1,3,128]{2,1,0:T(4,128)S(1)} %get-tuple-element.25), channel_id=1, source_target_pairs={{0,32},{32,64},{64,96},{96,128},{128,160},{160,192},{192,224},{1,3... | collective-permute-start | bytes 4616 | tf_op jit(solution)/shard_map/ppermute | solution.py:14
  20.4 3.4 %collective-permute-start.5 = (f32[1,3,128]{2,1,0:T(4,128)S(1)}, f32[1,3,128]{2,1,0:T(4,128)S(1)}, u32[]{:S(2)}, u32[]{:S(2)}) collective-permute-start(f32[1,3,128]{2,1,0:T(4,128)S(1)} %get-tuple-element.26), channel_id=1, source_target_pairs={{32,0},{64,32},{96,64},{128,96},{160,128},{192,160},{224,192},{33,... | collective-permute-start | bytes 4616 | tf_op jit(solution)/shard_map/ppermute | solution.py:17
  23.8 0.8 broadcast_multiply_fusion
  24.6 0.1 copy.40
  24.7 0.1 eq.40
  24.8 0.1 copy.39
  24.9 0.1 mul.72
  25.0 0.2 convert_reduce_fusion
  25.2 2.7 %fusion.28 = (f32[3,4,128,128]{3,2,1,0:T(8,128)}, f32[3,4,128,128]{3,2,1,0:T(8,128)}) fusion(f32[32,4,128,128]{3,2,1,0:T(8,128)} %param.6), kind=kLoop, calls=%fused_computation.67 | loop fusion | bytes 3145728 | tf_op jit(solution)/shard_map/slice | solution.py:90
  27.8 0.5 collective-permute-done.5
  28.4 0.1 slice_bitcast_fusion.5
  28.4 0.1 copy.45
  28.5 0.1 reshape.120
  28.6 2.9 %collective-permute-start.6 = (f32[8,128]{1,0:T(8,128)S(1)}, f32[8,128]{1,0:T(8,128)S(1)}, u32[]{:S(2)}, u32[]{:S(2)}) collective-permute-start(f32[8,128]{1,0:T(8,128)S(1)} %pad_bitcast_fusion.3), channel_id=1, source_target_pairs={{0,2},{2,4},{4,6},{6,8},{8,10},{10,12},{12,14},{14,16},{16,18},{18... | collective-permute-start | bytes 12296 | tf_op jit(solution)/shard_map/ppermute | solution.py:37
  31.5 0.1 copy.46
  31.6 0.1 reshape.124
  31.7 5.7 %collective-permute-start.7 = (f32[8,128]{1,0:T(8,128)S(1)}, f32[8,128]{1,0:T(8,128)S(1)}, u32[]{:S(2)}, u32[]{:S(2)}) collective-permute-start(f32[8,128]{1,0:T(8,128)S(1)} %pad_bitcast_fusion.2), channel_id=1, source_target_pairs={{2,0},{4,2},{6,4},{8,6},{10,8},{12,10},{14,12},{16,14},{18,16},{20... | collective-permute-start | bytes 12296 | tf_op jit(solution)/shard_map/ppermute | solution.py:38
  37.4 18.3 %collective-permute-done.6 = f32[8,128]{1,0:T(8,128)S(1)} collective-permute-done((f32[8,128]{1,0:T(8,128)S(1)}, f32[8,128]{1,0:T(8,128)S(1)}, u32[]{:S(2)}, u32[]{:S(2)}) %collective-permute-start.6) | collective-permute-done | bytes 4128 | tf_op jit(solution)/shard_map/ppermute | solution.py:37
  55.7 0.1 reshape.123
  55.8 0.1 copy.47
  55.9 0.1 reshape.127
  56.0 0.1 copy.48
  56.1 0.1 pad_maximum_fusion.1
  56.2 0.1 slice_bitcast_fusion.3
  56.3 12.6 %all-to-all-done = f32[256,16,128]{2,1,0:T(8,128)S(1)} async-done(((f32[256,16,128]{2,1,0:T(8,128)}), f32[256,16,128]{2,1,0:T(8,128)S(1)}, u32[]{:S(2)}, u32[]{:S(2)}) %all-to-all-start) | async-done | bytes 2097184 | tf_op jit(solution)/shard_map/all_to_all | solution.py:72
  68.9 0.8 gather_fusion.1
  69.7 0.1 slice.167
  69.7 1.0 %copy-done = f32[3,4,128,128]{3,2,1,0:T(8,128)S(1)} copy-done((f32[3,4,128,128]{3,2,1,0:T(8,128)S(1)}, f32[3,4,128,128]{3,2,1,0:T(8,128)}, u32[]{:S(2)}) %copy-start) | copy-done | bytes 786456
  70.8 0.2 copy-done.1
  71.0 0.5 fusion.9
  71.5 1.9 %collective-permute-start = (f32[16,3,128]{2,0,1:T(8,128)S(1)}, f32[16,3,128]{2,0,1:T(8,128)S(1)}, u32[]{:S(2)}, u32[]{:S(2)}) collective-permute-start(f32[16,3,128]{2,0,1:T(8,128)S(1)} %get-tuple-element.9), channel_id=1, source_target_pairs={{0,32},{32,64},{64,96},{96,128},{128,160},{160,192},{192,224},{1,3... | collective-permute-start | bytes 73736 | tf_op jit(solution)/shard_map/ppermute | solution.py:98
  73.4 4.0 %fusion.6 = f32[16,26,128]{2,0,1:T(8,128)S(1)} fusion(f32[26,4,16,128]{3,2,1,0:T(8,128)S(1)} %bitcast.59, f32[32,4,128,128]{3,2,1,0:T(8,128)} %param.6), kind=kOutput, calls=%fused_computation.8 | convolution fusion | flops 163577856 | bytes 7880704 | tf_op jit(solution)/shard_map/iklc,ikcd->lid/dot_general | solution.py:82
  77.5 3.6 %collective-permute-start.1 = (f32[16,3,128]{2,0,1:T(8,128)S(1)}, f32[16,3,128]{2,0,1:T(8,128)S(1)}, u32[]{:S(2)}, u32[]{:S(2)}) collective-permute-start(f32[16,3,128]{2,0,1:T(8,128)S(1)} %get-tuple-element.11), channel_id=1, source_target_pairs={{32,0},{64,32},{96,64},{128,96},{160,128},{192,160},{224,192},{33,... | collective-permute-start | bytes 73736 | tf_op jit(solution)/shard_map/ppermute | solution.py:100
  81.2 1.4 %collective-permute-done.1 = f32[16,3,128]{2,0,1:T(8,128)S(1)} collective-permute-done((f32[16,3,128]{2,0,1:T(8,128)S(1)}, f32[16,3,128]{2,0,1:T(8,128)S(1)}, u32[]{:S(2)}, u32[]{:S(2)}) %collective-permute-start.1) | collective-permute-done | bytes 24608 | tf_op jit(solution)/shard_map/ppermute | solution.py:100
  82.6 0.1 slice_bitcast_fusion.1
  82.8 0.2 copy.41
  83.0 0.1 reshape.112
  83.2 1.9 %collective-permute-start.2 = (f32[16,128]{1,0:T(8,128)S(1)}, f32[16,128]{1,0:T(8,128)S(1)}, u32[]{:S(2)}, u32[]{:S(2)}) collective-permute-start(f32[16,128]{1,0:T(8,128)S(1)} %pad_bitcast_fusion.1), channel_id=1, source_target_pairs={{0,2},{2,4},{4,6},{6,8},{8,10},{10,12},{12,14},{14,16},{16,18},{18... | collective-permute-start | bytes 24584 | tf_op jit(solution)/shard_map/ppermute | solution.py:37
  85.1 0.2 copy.43
  85.3 0.1 reshape.116
  85.4 6.6 %collective-permute-start.3 = (f32[16,128]{1,0:T(8,128)S(1)}, f32[16,128]{1,0:T(8,128)S(1)}, u32[]{:S(2)}, u32[]{:S(2)}) collective-permute-start(f32[16,128]{1,0:T(8,128)S(1)} %pad_bitcast_fusion), channel_id=1, source_target_pairs={{2,0},{4,2},{6,4},{8,6},{10,8},{12,10},{14,12},{16,14},{18,16},{20... | collective-permute-start | bytes 24584 | tf_op jit(solution)/shard_map/ppermute | solution.py:38
  92.1 0.1 slice_bitcast_fusion.2
  92.2 0.1 reshape.115
  92.3 0.3 copy.42
  92.5 0.9 collective-permute-done.3
  93.4 0.1 reshape.119
  93.5 0.3 copy.44
  93.8 0.3 pad_maximum_fusion
  94.1 0.7 fusion.14
  94.8 0.6 fusion.17
  95.4 0.3 fusion.20
  95.8 0.8 copy.49
  (31 shorter events, 0.2 us)
Async XLA Ops:
  5.2 13.0 %copy-start.2 = (f32[32,128]{1,0:T(8,128)S(1)}, f32[32,128]{1,0:T(8,128)}, u32[]{:S(2)}) copy-start(f32[32,128]{1,0:T(8,128)} %param.9) | copy-start | bytes 49156
  5.2 63.7 %all-to-all-start = ((f32[256,16,128]{2,1,0:T(8,128)}), f32[256,16,128]{2,1,0:T(8,128)S(1)}, u32[]{:S(2)}, u32[]{:S(2)}) async-start(f32[256,16,128]{2,1,0:T(8,128)} %gather_fusion), calls=%async_computation | async-start | bytes 4194304 | tf_op jit(solution)/shard_map/all_to_all | solution.py:72
  18.2 9.6 %collective-permute-start.4 = (f32[1,3,128]{2,1,0:T(4,128)S(1)}, f32[1,3,128]{2,1,0:T(4,128)S(1)}, u32[]{:S(2)}, u32[]{:S(2)}) collective-permute-start(f32[1,3,128]{2,1,0:T(4,128)S(1)} %get-tuple-element.25), channel_id=1, source_target_pairs={{0,32},{32,64},{64,96},{96,128},{128,160},{160,192},{192,224},{1,3... | collective-permute-start | bytes 4616 | tf_op jit(solution)/shard_map/ppermute | solution.py:14
  20.4 8.0 %collective-permute-start.5 = (f32[1,3,128]{2,1,0:T(4,128)S(1)}, f32[1,3,128]{2,1,0:T(4,128)S(1)}, u32[]{:S(2)}, u32[]{:S(2)}) collective-permute-start(f32[1,3,128]{2,1,0:T(4,128)S(1)} %get-tuple-element.26), channel_id=1, source_target_pairs={{32,0},{64,32},{96,64},{128,96},{160,128},{192,160},{224,192},{33,... | collective-permute-start | bytes 4616 | tf_op jit(solution)/shard_map/ppermute | solution.py:17
  28.6 27.1 %collective-permute-start.6 = (f32[8,128]{1,0:T(8,128)S(1)}, f32[8,128]{1,0:T(8,128)S(1)}, u32[]{:S(2)}, u32[]{:S(2)}) collective-permute-start(f32[8,128]{1,0:T(8,128)S(1)} %pad_bitcast_fusion.3), channel_id=1, source_target_pairs={{0,2},{2,4},{4,6},{6,8},{8,10},{10,12},{12,14},{14,16},{16,18},{18... | collective-permute-start | bytes 12296 | tf_op jit(solution)/shard_map/ppermute | solution.py:37
  31.7 24.3 %collective-permute-start.7 = (f32[8,128]{1,0:T(8,128)S(1)}, f32[8,128]{1,0:T(8,128)S(1)}, u32[]{:S(2)}, u32[]{:S(2)}) collective-permute-start(f32[8,128]{1,0:T(8,128)S(1)} %pad_bitcast_fusion.2), channel_id=1, source_target_pairs={{2,0},{4,2},{6,4},{8,6},{10,8},{12,10},{14,12},{16,14},{18,16},{20... | collective-permute-start | bytes 12296 | tf_op jit(solution)/shard_map/ppermute | solution.py:38
  69.6 1.1 %copy-start = (f32[3,4,128,128]{3,2,1,0:T(8,128)S(1)}, f32[3,4,128,128]{3,2,1,0:T(8,128)}, u32[]{:S(2)}) copy-start(f32[3,4,128,128]{3,2,1,0:T(8,128)} %get-tuple-element.15) | copy-start | bytes 2359300
  69.6 1.4 %copy-start.1 = (f32[3,4,128,128]{3,2,1,0:T(8,128)S(1)}, f32[3,4,128,128]{3,2,1,0:T(8,128)}, u32[]{:S(2)}) copy-start(f32[3,4,128,128]{3,2,1,0:T(8,128)} %get-tuple-element.16) | copy-start | bytes 2359300
  71.5 9.6 %collective-permute-start = (f32[16,3,128]{2,0,1:T(8,128)S(1)}, f32[16,3,128]{2,0,1:T(8,128)S(1)}, u32[]{:S(2)}, u32[]{:S(2)}) collective-permute-start(f32[16,3,128]{2,0,1:T(8,128)S(1)} %get-tuple-element.9), channel_id=1, source_target_pairs={{0,32},{32,64},{64,96},{96,128},{128,160},{160,192},{192,224},{1,3... | collective-permute-start | bytes 73736 | tf_op jit(solution)/shard_map/ppermute | solution.py:98
  77.5 5.1 %collective-permute-start.1 = (f32[16,3,128]{2,0,1:T(8,128)S(1)}, f32[16,3,128]{2,0,1:T(8,128)S(1)}, u32[]{:S(2)}, u32[]{:S(2)}) collective-permute-start(f32[16,3,128]{2,0,1:T(8,128)S(1)} %get-tuple-element.11), channel_id=1, source_target_pairs={{32,0},{64,32},{96,64},{128,96},{160,128},{192,160},{224,192},{33,... | collective-permute-start | bytes 73736 | tf_op jit(solution)/shard_map/ppermute | solution.py:100
  83.2 9.0 %collective-permute-start.2 = (f32[16,128]{1,0:T(8,128)S(1)}, f32[16,128]{1,0:T(8,128)S(1)}, u32[]{:S(2)}, u32[]{:S(2)}) collective-permute-start(f32[16,128]{1,0:T(8,128)S(1)} %pad_bitcast_fusion.1), channel_id=1, source_target_pairs={{0,2},{2,4},{4,6},{6,8},{8,10},{10,12},{12,14},{14,16},{16,18},{18... | collective-permute-start | bytes 24584 | tf_op jit(solution)/shard_map/ppermute | solution.py:37
  85.4 8.0 %collective-permute-start.3 = (f32[16,128]{1,0:T(8,128)S(1)}, f32[16,128]{1,0:T(8,128)S(1)}, u32[]{:S(2)}, u32[]{:S(2)}) collective-permute-start(f32[16,128]{1,0:T(8,128)S(1)} %pad_bitcast_fusion), channel_id=1, source_target_pairs={{2,0},{4,2},{6,4},{8,6},{10,8},{12,10},{14,12},{16,14},{18,16},{20... | collective-permute-start | bytes 24584 | tf_op jit(solution)/shard_map/ppermute | solution.py:38

commit v12 on v9

--- a/solution.py
+++ b/solution.py
@@ -78,22 +78,29 @@
     picked = jnp.take(incoming, mine * CAP + mine_slot, axis=0, mode="clip")
     picked = picked.reshape(frows, fanin, levels, block)
 
+    def split(x):
+        high = lax.reduce_precision(x, exponent_bits=8, mantissa_bits=7)
+        return high.astype(jnp.bfloat16), (x - high).astype(jnp.bfloat16)
+
+    w_hi, w_lo = split(remap_weights)
+    p_hi, p_lo = split(picked)
+
+    def product(a, w):
+        return jnp.einsum("iklc,ikcd->lid", a, w, preferred_element_type=jnp.float32)
+
+    def remap_parts(pick):
+        both = product(jnp.concatenate([pick(p_hi), pick(p_lo)], axis=2), pick(w_hi))
+        return (both[:levels] + both[levels:]) + product(pick(p_hi), pick(w_lo))
+
     def remap(lo, hi):
-        return jnp.einsum(
-            "iklc,ikcd->lid", picked[lo:hi], remap_weights[lo:hi], precision=lax.Precision.HIGH
-        )
+        return remap_parts(lambda a: a[lo:hi])
 
     count = lax.axis_size("gx")
     forward = [(i, i + 1) for i in range(count - 1)]
     backward = [(target, source) for source, target in forward]
     gain = packed_halo(with_halo(smoothing[None], "gx", 1, PASSES), "gy", PASSES)
     edge_rows = lambda a: jnp.concatenate([a[:PASSES], a[frows - PASSES:]], axis=0)
-    edges = jnp.einsum(
-        "iklc,ikcd->lid",
-        edge_rows(picked),
-        edge_rows(remap_weights),
-        precision=lax.Precision.HIGH,
-    )
+    edges = remap_parts(edge_rows)
     top, bottom = lax.optimization_barrier((edges[:, :PASSES], edges[:, PASSES:]))
     low = lax.ppermute(bottom, "gx", forward)
     high = lax.ppermute(top, "gx", backward)

time: 96.3 us -> 94.1 us (0.977)
  waiting for transfers between devices: 32.4 us -> 24.8 us
  other arithmetic: 4.1 us -> 10.8 us
  matrix products: 5.9 us -> 1.62 us
  local copies, waits for them, and re-layouts: 11.3 us -> 13.8 us
    ppermute x2, waiting for transfers between devices: 18.3 us -> 11.5 us  [packed_halo(): low = unpack(lax.ppermute(pack(block[:, :, cols - width:]), axis, forward))]
    convert_element_type x0 -> x2, other arithmetic: none -> 6.07 us  [split(): return (high.astype(jnp.bfloat16), (x - high).astype(jnp.bfloat16))]
    dot_general x2 -> x4, matrix products: 5.9 us -> 1.62 us  [product(): jnp.einsum('iklc,ikcd->lid', a, w, preferred_element_type=jnp.float32)]
    unnamed x6 -> x26, local copies, waits for them, and re-layouts: 1.13 us -> 3.83 us
    slice x2, local copies, waits for them, and re-layouts: 2.7 us -> 1.68 us  [shards(): a[:PASSES]]
  transfers between devices with their start and end apart: 9 -> 9, of which waited for: 4 -> 4; matrix products, arithmetic and copies ran while one was open for 10% -> 14% of each run, Pallas kernels for 0% -> 0%
where the time goes in v12:
time: 94.1 us; the launch traced here: 92.8 us
  starting transfers between devices  41.3 us (44%)
  waiting for transfers between devices  24.8 us (26%)
  local copies, waits for them, and re-layouts  13.8 us (15%)
  other arithmetic  10.8 us (11%)
  matrix products  1.62 us (2%)
    all_to_all x1, starting transfers between devices, shards(): incoming = lax.all_to_all(outgoing, ('gx', 'gy'), 0, 0, tiled=True)  12.9 us
    all_to_all x1, waiting for transfers between devices, shards(): incoming = lax.all_to_all(outgoing, ('gx', 'gy'), 0, 0, tiled=True)  11.9 us
    ppermute x2, starting transfers between devices, packed_halo(): high = unpack(lax.ppermute(pack(block[:, :, :width]), axis, backward))  11.8 us
    ppermute x2, waiting for transfers between devices, packed_halo(): low = unpack(lax.ppermute(pack(block[:, :, cols - width:]), axis, forward))  11.5 us
    convert_element_type x2, other arithmetic, split(): return (high.astype(jnp.bfloat16), (x - high).astype(jnp.bfloat16))  6.07 us
    ppermute x2, starting transfers between devices, packed_halo(): low = unpack(lax.ppermute(pack(block[:, :, cols - width:]), axis, forward))  5.29 us
    unnamed x26, local copies, waits for them, and re-layouts  3.83 us
    ppermute x1, starting transfers between devices, shards(): high = lax.ppermute(top, 'gx', backward)  3.64 us
  transfers between devices with their start and end apart: 9, of which 4 were waited for; matrix products, arithmetic and copies ran while one was open for 14% of the time, Pallas kernels for 0%

profile of v12, /device:TPU:10, one launch (start us, length us, event | category | flops | bytes accessed | tf_op | source)
XLA Modules:
  0.0 92.8 jit_solution(12474516922309975028)
XLA Ops:
  0.0 0.9 select_reduce_fusion
  1.0 0.1 reshape.128
  1.3 0.1 sub.30
  1.5 0.1 copy.36
  1.6 0.1 reshape.131
  1.7 1.1 %copy.53 = f32[16,32,128]{2,0,1:T(8,128)S(1)} copy(f32[16,32,128]{2,1,0:T(8,128)} %param.5) | data formatting | bytes 524288 | tf_op args[0]
  2.9 2.4 %gather_fusion = f32[256,16,128]{2,1,0:T(8,128)} fusion(f32[32,16,128]{2,1,0:T(8,128)S(1)} %bitcast.71, s32[1024]{0:T(1024)S(1)} %pad_clamp_fusion.1), kind=kCustom, calls=%fused_computation | custom fusion | bytes 4195328 | tf_op jit(solution)/shard_map/jit(_take)/gather | solution.py:71
  5.3 12.9 %all-to-all-start = ((f32[256,16,128]{2,1,0:T(8,128)}), f32[256,16,128]{2,1,0:T(8,128)S(1)}, u32[]{:S(2)}, u32[]{:S(2)}) async-start(f32[256,16,128]{2,1,0:T(8,128)} %gather_fusion), calls=%async_computation | async-start | bytes 4194304 | tf_op jit(solution)/shard_map/all_to_all | solution.py:72
  18.2 2.1 %collective-permute-start.4 = (f32[1,3,128]{2,1,0:T(4,128)S(1)}, f32[1,3,128]{2,1,0:T(4,128)S(1)}, u32[]{:S(2)}, u32[]{:S(2)}) collective-permute-start(f32[1,3,128]{2,1,0:T(4,128)S(1)} %get-tuple-element.29), channel_id=1, source_target_pairs={{0,32},{32,64},{64,96},{96,128},{128,160},{160,192},{192,224},{1,3... | collective-permute-start | bytes 4616 | tf_op jit(solution)/shard_map/ppermute | solution.py:14
  20.3 3.4 %collective-permute-start.5 = (f32[1,3,128]{2,1,0:T(4,128)S(1)}, f32[1,3,128]{2,1,0:T(4,128)S(1)}, u32[]{:S(2)}, u32[]{:S(2)}) collective-permute-start(f32[1,3,128]{2,1,0:T(4,128)S(1)} %get-tuple-element.30), channel_id=1, source_target_pairs={{32,0},{64,32},{96,64},{128,96},{160,128},{192,160},{224,192},{33,... | collective-permute-start | bytes 4616 | tf_op jit(solution)/shard_map/ppermute | solution.py:17
  23.8 0.8 broadcast_multiply_fusion
  24.5 0.1 copy.37
  24.6 0.1 mul.72
  24.7 0.1 copy.38
  24.8 0.1 eq.40
  24.9 0.2 convert_reduce_fusion
  25.1 5.8 %reduce-precision_convert_fusion = (bf16[32,4,128,128]{3,2,1,0:T(8,128)(2,1)S(1)}, bf16[32,4,128,128]{3,2,1,0:T(8,128)(2,1)S(1)}) fusion(f32[32,4,128,128]{3,2,1,0:T(8,128)} %param.6), kind=kLoop, calls=%fused_computation.3 | loop fusion | flops 8388608 | bytes 16777216 | tf_op jit(solution)/shard_map/convert_element_type | solution.py:83
  30.9 1.9 %copy-done = bf16[32,4,128,128]{3,2,1,0:T(8,128)(2,1)} copy-done((bf16[32,4,128,128]{3,2,1,0:T(8,128)(2,1)}, bf16[32,4,128,128]{3,2,1,0:T(8,128)(2,1)S(1)}, u32[]{:S(2)}) %copy-start) | copy-done | bytes 4194328
  32.9 1.7 %fusion.54 = (bf16[3,4,128,128]{3,2,1,0:T(8,128)(2,1)}, bf16[3,4,128,128]{3,2,1,0:T(8,128)(2,1)}, bf16[3,4,128,128]{3,2,1,0:T(8,128)(2,1)S(1)}, bf16[3,4,128,128]{3,2,1,0:T(8,128)(2,1)}) fusion(bf16[32,4,128,128]{3,2,1,0:T(8,128)(2,1)S(1)} %get-tuple-element.11, bf16[32,4,128,128]{3,2,1,0:T(8,128)(2,1)S(1)} %get-tuple-element.12), kind=kLoop, calls=%fused_computation.96 | loop fusion | bytes 3145728 | tf_op jit(solution)/shard_map/slice | solution.py:102
  34.6 0.1 slice_bitcast_fusion.5
  34.7 0.1 copy.43
  34.7 0.1 reshape.120
  34.8 0.1 copy.44
  34.9 0.1 reshape.124
  35.0 3.4 %collective-permute-start.6 = (f32[8,128]{1,0:T(8,128)S(1)}, f32[8,128]{1,0:T(8,128)S(1)}, u32[]{:S(2)}, u32[]{:S(2)}) collective-permute-start(f32[8,128]{1,0:T(8,128)S(1)} %pad_bitcast_fusion.3), channel_id=1, source_target_pairs={{0,2},{2,4},{4,6},{6,8},{8,10},{10,12},{12,14},{14,16},{16,18},{18... | collective-permute-start | bytes 12296 | tf_op jit(solution)/shard_map/ppermute | solution.py:37
  38.4 5.2 %collective-permute-start.7 = (f32[8,128]{1,0:T(8,128)S(1)}, f32[8,128]{1,0:T(8,128)S(1)}, u32[]{:S(2)}, u32[]{:S(2)}) collective-permute-start(f32[8,128]{1,0:T(8,128)S(1)} %pad_bitcast_fusion.2), channel_id=1, source_target_pairs={{2,0},{4,2},{6,4},{8,6},{10,8},{12,10},{14,12},{16,14},{18,16},{20... | collective-permute-start | bytes 12296 | tf_op jit(solution)/shard_map/ppermute | solution.py:38
  43.6 0.6 pad_clamp_fusion
  44.2 11.5 %collective-permute-done.6 = f32[8,128]{1,0:T(8,128)S(1)} collective-permute-done((f32[8,128]{1,0:T(8,128)S(1)}, f32[8,128]{1,0:T(8,128)S(1)}, u32[]{:S(2)}, u32[]{:S(2)}) %collective-permute-start.6) | collective-permute-done | bytes 4128 | tf_op jit(solution)/shard_map/ppermute | solution.py:37
  55.7 0.1 reshape.123
  55.8 0.1 reshape.127
  55.8 0.1 copy.46
  55.9 0.1 copy.45
  56.0 0.1 pad_maximum_fusion.1
  56.2 0.7 slice_bitcast_fusion.2
  56.9 11.9 %all-to-all-done = f32[256,16,128]{2,1,0:T(8,128)S(1)} async-done(((f32[256,16,128]{2,1,0:T(8,128)}), f32[256,16,128]{2,1,0:T(8,128)S(1)}, u32[]{:S(2)}, u32[]{:S(2)}) %all-to-all-start) | async-done | bytes 2097184 | tf_op jit(solution)/shard_map/all_to_all | solution.py:72
  68.8 0.9 gather_fusion.1
  69.7 0.3 fusion.18
  70.1 0.6 copy-done.5
  70.7 0.1 copy-done.6
  70.8 0.2 convolution_bitcast_fusion
  71.1 0.2 fusion.17
  71.3 2.2 %collective-permute-start = (f32[16,3,128]{2,0,1:T(8,128)S(1)}, f32[16,3,128]{2,0,1:T(8,128)S(1)}, u32[]{:S(2)}, u32[]{:S(2)}) collective-permute-start(f32[16,3,128]{2,0,1:T(8,128)S(1)} %get-tuple-element.7), channel_id=1, source_target_pairs={{0,32},{32,64},{64,96},{96,128},{128,160},{160,192},{192,224},{1,3... | collective-permute-start | bytes 73736 | tf_op jit(solution)/shard_map/ppermute | solution.py:105
  73.5 3.6 %collective-permute-start.1 = (f32[16,3,128]{2,0,1:T(8,128)S(1)}, f32[16,3,128]{2,0,1:T(8,128)S(1)}, u32[]{:S(2)}, u32[]{:S(2)}) collective-permute-start(f32[16,3,128]{2,0,1:T(8,128)S(1)} %get-tuple-element.8), channel_id=1, source_target_pairs={{32,0},{64,32},{96,64},{128,96},{160,128},{192,160},{224,192},{33,... | collective-permute-start | bytes 73736 | tf_op jit(solution)/shard_map/ppermute | solution.py:106
  77.1 0.6 fusion.5
  77.8 0.6 fusion.14
  78.4 0.2 collective-permute-done.1
  78.6 0.1 slice_bitcast_fusion.1
  78.8 0.2 copy.39
  79.0 0.1 reshape.112
  79.1 1.9 %collective-permute-start.2 = (f32[16,128]{1,0:T(8,128)S(1)}, f32[16,128]{1,0:T(8,128)S(1)}, u32[]{:S(2)}, u32[]{:S(2)}) collective-permute-start(f32[16,128]{1,0:T(8,128)S(1)} %pad_bitcast_fusion.1), channel_id=1, source_target_pairs={{0,2},{2,4},{4,6},{6,8},{8,10},{10,12},{12,14},{14,16},{16,18},{18... | collective-permute-start | bytes 24584 | tf_op jit(solution)/shard_map/ppermute | solution.py:37
  81.1 0.2 copy.41
  81.3 0.1 reshape.116
  81.4 6.6 %collective-permute-start.3 = (f32[16,128]{1,0:T(8,128)S(1)}, f32[16,128]{1,0:T(8,128)S(1)}, u32[]{:S(2)}, u32[]{:S(2)}) collective-permute-start(f32[16,128]{1,0:T(8,128)S(1)} %pad_bitcast_fusion), channel_id=1, source_target_pairs={{2,0},{4,2},{6,4},{8,6},{10,8},{12,10},{14,12},{16,14},{18,16},{20... | collective-permute-start | bytes 24584 | tf_op jit(solution)/shard_map/ppermute | solution.py:38
  88.1 0.1 slice_bitcast_fusion.3
  88.1 0.1 reshape.115
  88.3 1.1 %collective-permute-done.3 = f32[16,128]{1,0:T(8,128)S(1)} collective-permute-done((f32[16,128]{1,0:T(8,128)S(1)}, f32[16,128]{1,0:T(8,128)S(1)}, u32[]{:S(2)}, u32[]{:S(2)}) %collective-permute-start.3) | collective-permute-done | bytes 8224 | tf_op jit(solution)/shard_map/ppermute | solution.py:38
  89.4 0.1 reshape.119
  89.5 0.3 copy.42
  89.8 0.2 copy.40
  90.0 0.3 pad_maximum_fusion
  90.3 0.7 fusion.30
  91.0 0.6 fusion.33
  91.7 0.3 fusion.36
  92.0 0.8 copy.47
  (51 shorter events, 0.6 us)
Async XLA Ops:
  2.9 15.3 %copy-start.9 = (f32[32,128]{1,0:T(8,128)S(1)}, f32[32,128]{1,0:T(8,128)}, u32[]{:S(2)}) copy-start(f32[32,128]{1,0:T(8,128)} %param.9) | copy-start | bytes 49156
  5.3 63.5 %all-to-all-start = ((f32[256,16,128]{2,1,0:T(8,128)}), f32[256,16,128]{2,1,0:T(8,128)S(1)}, u32[]{:S(2)}, u32[]{:S(2)}) async-start(f32[256,16,128]{2,1,0:T(8,128)} %gather_fusion), calls=%async_computation | async-start | bytes 4194304 | tf_op jit(solution)/shard_map/all_to_all | solution.py:72
  18.2 16.4 %collective-permute-start.4 = (f32[1,3,128]{2,1,0:T(4,128)S(1)}, f32[1,3,128]{2,1,0:T(4,128)S(1)}, u32[]{:S(2)}, u32[]{:S(2)}) collective-permute-start(f32[1,3,128]{2,1,0:T(4,128)S(1)} %get-tuple-element.29), channel_id=1, source_target_pairs={{0,32},{32,64},{64,96},{96,128},{128,160},{160,192},{192,224},{1,3... | collective-permute-start | bytes 4616 | tf_op jit(solution)/shard_map/ppermute | solution.py:14
  20.3 14.2 %collective-permute-start.5 = (f32[1,3,128]{2,1,0:T(4,128)S(1)}, f32[1,3,128]{2,1,0:T(4,128)S(1)}, u32[]{:S(2)}, u32[]{:S(2)}) collective-permute-start(f32[1,3,128]{2,1,0:T(4,128)S(1)} %get-tuple-element.30), channel_id=1, source_target_pairs={{32,0},{64,32},{96,64},{128,96},{160,128},{192,160},{224,192},{33,... | collective-permute-start | bytes 4616 | tf_op jit(solution)/shard_map/ppermute | solution.py:17
  30.9 2.0 %copy-start = (bf16[32,4,128,128]{3,2,1,0:T(8,128)(2,1)}, bf16[32,4,128,128]{3,2,1,0:T(8,128)(2,1)S(1)}, u32[]{:S(2)}) copy-start(bf16[32,4,128,128]{3,2,1,0:T(8,128)(2,1)S(1)} %get-tuple-element.12) | copy-start | bytes 12582916
  30.9 3.7 %copy-start.2 = (bf16[32,4,128,128]{3,2,1,0:T(8,128)(2,1)}, bf16[32,4,128,128]{3,2,1,0:T(8,128)(2,1)S(1)}, u32[]{:S(2)}) copy-start(bf16[32,4,128,128]{3,2,1,0:T(8,128)(2,1)S(1)} %get-tuple-element.11) | copy-start | bytes 12582916
  35.0 20.7 %collective-permute-start.6 = (f32[8,128]{1,0:T(8,128)S(1)}, f32[8,128]{1,0:T(8,128)S(1)}, u32[]{:S(2)}, u32[]{:S(2)}) collective-permute-start(f32[8,128]{1,0:T(8,128)S(1)} %pad_bitcast_fusion.3), channel_id=1, source_target_pairs={{0,2},{2,4},{4,6},{6,8},{8,10},{10,12},{12,14},{14,16},{16,18},{18... | collective-permute-start | bytes 12296 | tf_op jit(solution)/shard_map/ppermute | solution.py:37
  38.4 17.4 %collective-permute-start.7 = (f32[8,128]{1,0:T(8,128)S(1)}, f32[8,128]{1,0:T(8,128)S(1)}, u32[]{:S(2)}, u32[]{:S(2)}) collective-permute-start(f32[8,128]{1,0:T(8,128)S(1)} %pad_bitcast_fusion.2), channel_id=1, source_target_pairs={{2,0},{4,2},{6,4},{8,6},{10,8},{12,10},{14,12},{16,14},{18,16},{20... | collective-permute-start | bytes 12296 | tf_op jit(solution)/shard_map/ppermute | solution.py:38
  56.1 0.7 copy-start.7
  69.7 1.0 %copy-start.5 = (bf16[3,4,128,128]{3,2,1,0:T(8,128)(2,1)S(1)}, bf16[3,4,128,128]{3,2,1,0:T(8,128)(2,1)}, u32[]{:S(2)}) copy-start(bf16[3,4,128,128]{3,2,1,0:T(8,128)(2,1)} %get-tuple-element.13) | copy-start | bytes 1179652
  69.7 1.1 %copy-start.6 = (bf16[3,4,128,128]{3,2,1,0:T(8,128)(2,1)S(1)}, bf16[3,4,128,128]{3,2,1,0:T(8,128)(2,1)}, u32[]{:S(2)}) copy-start(bf16[3,4,128,128]{3,2,1,0:T(8,128)(2,1)} %get-tuple-element.14) | copy-start | bytes 1179652
  69.7 1.3 %copy-start.4 = (bf16[3,4,128,128]{3,2,1,0:T(8,128)(2,1)S(1)}, bf16[3,4,128,128]{3,2,1,0:T(8,128)(2,1)}, u32[]{:S(2)}) copy-start(bf16[3,4,128,128]{3,2,1,0:T(8,128)(2,1)} %get-tuple-element.32) | copy-start | bytes 1179652
  69.7 7.4 %copy-start.3 = (bf16[32,4,128,128]{3,2,1,0:T(8,128)(2,1)S(1)}, bf16[32,4,128,128]{3,2,1,0:T(8,128)(2,1)}, u32[]{:S(2)}) copy-start(bf16[32,4,128,128]{3,2,1,0:T(8,128)(2,1)} %copy-done.2) | copy-start | bytes 12582916
  71.0 6.8 %copy-start.1 = (bf16[32,4,128,128]{3,2,1,0:T(8,128)(2,1)S(1)}, bf16[32,4,128,128]{3,2,1,0:T(8,128)(2,1)}, u32[]{:S(2)}) copy-start(bf16[32,4,128,128]{3,2,1,0:T(8,128)(2,1)} %copy-done) | copy-start | bytes 12582916
  71.3 6.5 %collective-permute-start = (f32[16,3,128]{2,0,1:T(8,128)S(1)}, f32[16,3,128]{2,0,1:T(8,128)S(1)}, u32[]{:S(2)}, u32[]{:S(2)}) collective-permute-start(f32[16,3,128]{2,0,1:T(8,128)S(1)} %get-tuple-element.7), channel_id=1, source_target_pairs={{0,32},{32,64},{64,96},{96,128},{128,160},{160,192},{192,224},{1,3... | collective-permute-start | bytes 73736 | tf_op jit(solution)/shard_map/ppermute | solution.py:105
  73.5 5.1 %collective-permute-start.1 = (f32[16,3,128]{2,0,1:T(8,128)S(1)}, f32[16,3,128]{2,0,1:T(8,128)S(1)}, u32[]{:S(2)}, u32[]{:S(2)}) collective-permute-start(f32[16,3,128]{2,0,1:T(8,128)S(1)} %get-tuple-element.8), channel_id=1, source_target_pairs={{32,0},{64,32},{96,64},{128,96},{160,128},{192,160},{224,192},{33,... | collective-permute-start | bytes 73736 | tf_op jit(solution)/shard_map/ppermute | solution.py:106
  77.8 10.3 %copy-start.8 = (f32[1,38,134]{2,1,0:T(8,128)S(1)}, f32[1,38,134]{2,1,0:T(8,128)}, u32[]{:S(2)}) copy-start(f32[1,38,134]{2,1,0:T(8,128)} %copy-done.7) | copy-start | bytes 61108
  78.8 12.2 %copy-start.10 = (f32[34,130]{1,0:T(8,128)S(1)}, f32[34,130]{1,0:T(8,128)}, u32[]{:S(2)}) copy-start(f32[34,130]{1,0:T(8,128)} %slice_bitcast_fusion.2) | copy-start | bytes 53044
  79.1 9.0 %collective-permute-start.2 = (f32[16,128]{1,0:T(8,128)S(1)}, f32[16,128]{1,0:T(8,128)S(1)}, u32[]{:S(2)}, u32[]{:S(2)}) collective-permute-start(f32[16,128]{1,0:T(8,128)S(1)} %pad_bitcast_fusion.1), channel_id=1, source_target_pairs={{0,2},{2,4},{4,6},{6,8},{8,10},{10,12},{12,14},{14,16},{16,18},{18... | collective-permute-start | bytes 24584 | tf_op jit(solution)/shard_map/ppermute | solution.py:37
  81.4 8.0 %collective-permute-start.3 = (f32[16,128]{1,0:T(8,128)S(1)}, f32[16,128]{1,0:T(8,128)S(1)}, u32[]{:S(2)}, u32[]{:S(2)}) collective-permute-start(f32[16,128]{1,0:T(8,128)S(1)} %pad_bitcast_fusion), channel_id=1, source_target_pairs={{2,0},{4,2},{6,4},{8,6},{10,8},{12,10},{14,12},{16,14},{18,16},{20... | collective-permute-start | bytes 24584 | tf_op jit(solution)/shard_map/ppermute | solution.py:38

commit v13 on v12

--- a/solution.py
+++ b/solution.py
@@ -27,12 +27,12 @@
     padded = -(-size // 1024) * 1024
 
     def pack(part):
-        flat = jnp.transpose(part, (2, 0, 1)).reshape(size)
+        flat = jnp.transpose(part, (1, 0, 2)).reshape(size)
         return jnp.pad(flat, (0, padded - size)).reshape(padded // 128, 128)
 
     def unpack(tile):
         flat = tile.reshape(padded)[:size]
-        return jnp.transpose(flat.reshape(width, channels, rows), (1, 2, 0))
+        return jnp.transpose(flat.reshape(rows, channels, width), (1, 0, 2))
 
     low = unpack(lax.ppermute(pack(block[:, :, cols - width:]), axis, forward))
     high = unpack(lax.ppermute(pack(block[:, :, :width]), axis, backward))

time: 94.1 us -> 96.2 us (1.022)
  waiting for transfers between devices: 24.8 us -> 30.2 us
  starting transfers between devices: 41.3 us -> 39.4 us
    ppermute x2, waiting for transfers between devices: 11.5 us -> 17.8 us  [packed_halo(): low = unpack(lax.ppermute(pack(block[:, :, cols - width:]), axis, forward))]
    ppermute x2, starting transfers between devices: 11.8 us -> 9.79 us  [packed_halo(): high = unpack(lax.ppermute(pack(block[:, :, :width]), axis, backward))]
    ppermute x2, waiting for transfers between devices: 1.14 us -> 0.01 us  [packed_halo(): high = unpack(lax.ppermute(pack(block[:, :, :width]), axis, backward))]
  transfers between devices with their start and end apart: 9 -> 9, of which waited for: 4 -> 4; matrix products, arithmetic and copies ran while one was open for 14% -> 13% of each run, Pallas kernels for 0% -> 0%
where the time goes in v13:
time: 96.2 us; the launch traced here: 95.4 us
  starting transfers between devices  39.4 us (41%)
  waiting for transfers between devices  30.2 us (31%)
  local copies, waits for them, and re-layouts  13 us (14%)
  other arithmetic  10.8 us (11%)
  matrix products  1.62 us (2%)
    ppermute x2, waiting for transfers between devices, packed_halo(): low = unpack(lax.ppermute(pack(block[:, :, cols - width:]), axis, forward))  17.8 us
    all_to_all x1, starting transfers between devices, shards(): incoming = lax.all_to_all(outgoing, ('gx', 'gy'), 0, 0, tiled=True)  12.9 us
    all_to_all x1, waiting for transfers between devices, shards(): incoming = lax.all_to_all(outgoing, ('gx', 'gy'), 0, 0, tiled=True)  12.1 us
    ppermute x2, starting transfers between devices, packed_halo(): high = unpack(lax.ppermute(pack(block[:, :, :width]), axis, backward))  9.79 us
    convert_element_type x2, other arithmetic, split(): return (high.astype(jnp.bfloat16), (x - high).astype(jnp.bfloat16))  6.07 us
    ppermute x2, starting transfers between devices, packed_halo(): low = unpack(lax.ppermute(pack(block[:, :, cols - width:]), axis, forward))  5.3 us
    unnamed x26, local copies, waits for them, and re-layouts  3.83 us
    ppermute x1, starting transfers between devices, shards(): high = lax.ppermute(top, 'gx', backward)  3.64 us
  transfers between devices with their start and end apart: 9, of which 4 were waited for; matrix products, arithmetic and copies ran while one was open for 13% of the time, Pallas kernels for 0%

profile of v13, /device:TPU:10, one launch (start us, length us, event | category | flops | bytes accessed | tf_op | source)
XLA Modules:
  0.0 95.4 jit_solution(9165981808605718262)
XLA Ops:
  0.0 0.9 select_reduce_fusion
  1.0 0.1 reshape.112
  1.0 0.1 copy.21
  1.1 0.1 copy.20
  1.2 0.1 reduce_window_sum.11
  1.3 0.1 sub.30
  1.4 0.1 copy.23
  1.5 0.1 copy.24
  1.6 0.1 reshape.115
  1.7 1.1 %copy.33 = f32[16,32,128]{2,0,1:T(8,128)S(1)} copy(f32[16,32,128]{2,1,0:T(8,128)} %param.5) | data formatting | bytes 524288 | tf_op args[0]
  2.9 0.0 copy-start.9
  2.9 2.4 %gather_fusion = f32[256,16,128]{2,1,0:T(8,128)} fusion(f32[32,16,128]{2,1,0:T(8,128)S(1)} %bitcast.61, s32[1024]{0:T(1024)S(1)} %pad_clamp_fusion.1), kind=kCustom, calls=%fused_computation | custom fusion | bytes 4195328 | tf_op jit(solution)/shard_map/jit(_take)/gather | solution.py:71
  5.3 12.9 %all-to-all-start = ((f32[256,16,128]{2,1,0:T(8,128)}), f32[256,16,128]{2,1,0:T(8,128)S(1)}, u32[]{:S(2)}, u32[]{:S(2)}) async-start(f32[256,16,128]{2,1,0:T(8,128)} %gather_fusion), calls=%async_computation | async-start | bytes 4194304 | tf_op jit(solution)/shard_map/all_to_all | solution.py:72
  18.2 2.1 %collective-permute-start.4 = (f32[1,3,128]{2,1,0:T(4,128)S(1)}, f32[1,3,128]{2,1,0:T(4,128)S(1)}, u32[]{:S(2)}, u32[]{:S(2)}) collective-permute-start(f32[1,3,128]{2,1,0:T(4,128)S(1)} %get-tuple-element.29), channel_id=1, source_target_pairs={{0,32},{32,64},{64,96},{96,128},{128,160},{160,192},{192,224},{1,3... | collective-permute-start | bytes 4616 | tf_op jit(solution)/shard_map/ppermute | solution.py:14
  20.3 3.4 %collective-permute-start.5 = (f32[1,3,128]{2,1,0:T(4,128)S(1)}, f32[1,3,128]{2,1,0:T(4,128)S(1)}, u32[]{:S(2)}, u32[]{:S(2)}) collective-permute-start(f32[1,3,128]{2,1,0:T(4,128)S(1)} %get-tuple-element.30), channel_id=1, source_target_pairs={{32,0},{64,32},{96,64},{128,96},{160,128},{192,160},{224,192},{33,... | collective-permute-start | bytes 4616 | tf_op jit(solution)/shard_map/ppermute | solution.py:17
  23.8 0.8 broadcast_multiply_fusion
  24.5 0.1 copy.25
  24.6 0.1 mul.72
  24.7 0.1 copy.26
  24.8 0.1 eq.40
  24.9 0.2 convert_reduce_fusion
  25.1 5.8 %reduce-precision_convert_fusion = (bf16[32,4,128,128]{3,2,1,0:T(8,128)(2,1)S(1)}, bf16[32,4,128,128]{3,2,1,0:T(8,128)(2,1)S(1)}) fusion(f32[32,4,128,128]{3,2,1,0:T(8,128)} %param.6), kind=kLoop, calls=%fused_computation.3 | loop fusion | flops 8388608 | bytes 16777216 | tf_op jit(solution)/shard_map/convert_element_type | solution.py:83
  30.9 1.9 %copy-done = bf16[32,4,128,128]{3,2,1,0:T(8,128)(2,1)} copy-done((bf16[32,4,128,128]{3,2,1,0:T(8,128)(2,1)}, bf16[32,4,128,128]{3,2,1,0:T(8,128)(2,1)S(1)}, u32[]{:S(2)}) %copy-start) | copy-done | bytes 4194328
  32.9 1.7 %fusion.54 = (bf16[3,4,128,128]{3,2,1,0:T(8,128)(2,1)}, bf16[3,4,128,128]{3,2,1,0:T(8,128)(2,1)}, bf16[3,4,128,128]{3,2,1,0:T(8,128)(2,1)S(1)}, bf16[3,4,128,128]{3,2,1,0:T(8,128)(2,1)}) fusion(bf16[32,4,128,128]{3,2,1,0:T(8,128)(2,1)S(1)} %get-tuple-element.11, bf16[32,4,128,128]{3,2,1,0:T(8,128)(2,1)S(1)} %get-tuple-element.12), kind=kLoop, calls=%fused_computation.94 | loop fusion | bytes 3145728 | tf_op jit(solution)/shard_map/slice | solution.py:102
  34.5 0.0 copy-done.2
  34.6 0.1 fusion.59
  34.7 0.1 reshape_transpose.6
  34.8 0.1 reshape_transpose.7
  34.9 3.4 %collective-permute-start.6 = (f32[8,128]{1,0:T(8,128)S(1)}, f32[8,128]{1,0:T(8,128)S(1)}, u32[]{:S(2)}, u32[]{:S(2)}) collective-permute-start(f32[8,128]{1,0:T(8,128)S(1)} %pad_bitcast_fusion.3), channel_id=1, source_target_pairs={{0,2},{2,4},{4,6},{6,8},{8,10},{10,12},{12,14},{14,16},{16,18},{18... | collective-permute-start | bytes 12296 | tf_op jit(solution)/shard_map/ppermute | solution.py:37
  38.3 5.2 %collective-permute-start.7 = (f32[8,128]{1,0:T(8,128)S(1)}, f32[8,128]{1,0:T(8,128)S(1)}, u32[]{:S(2)}, u32[]{:S(2)}) collective-permute-start(f32[8,128]{1,0:T(8,128)S(1)} %pad_bitcast_fusion.2), channel_id=1, source_target_pairs={{2,0},{4,2},{6,4},{8,6},{10,8},{12,10},{14,12},{16,14},{18,16},{20... | collective-permute-start | bytes 12296 | tf_op jit(solution)/shard_map/ppermute | solution.py:38
  43.5 0.6 pad_clamp_fusion
  44.1 11.6 %collective-permute-done.6 = f32[8,128]{1,0:T(8,128)S(1)} collective-permute-done((f32[8,128]{1,0:T(8,128)S(1)}, f32[8,128]{1,0:T(8,128)S(1)}, u32[]{:S(2)}, u32[]{:S(2)}) %collective-permute-start.6) | collective-permute-done | bytes 4128 | tf_op jit(solution)/shard_map/ppermute | solution.py:37
  55.7 0.1 transpose_reshape.7
  55.8 0.1 transpose_reshape.6
  55.9 0.1 pad_maximum_fusion.1
  56.0 0.0 copy-start.7
  56.0 0.7 slice_bitcast_fusion.2
  56.7 12.1 %all-to-all-done = f32[256,16,128]{2,1,0:T(8,128)S(1)} async-done(((f32[256,16,128]{2,1,0:T(8,128)}), f32[256,16,128]{2,1,0:T(8,128)S(1)}, u32[]{:S(2)}, u32[]{:S(2)}) %all-to-all-start) | async-done | bytes 2097184 | tf_op jit(solution)/shard_map/all_to_all | solution.py:72
  68.8 0.9 gather_fusion.1
  69.7 0.3 fusion.18
  70.1 0.6 copy-done.5
  70.7 0.1 copy-done.6
  70.8 0.2 convolution_bitcast_fusion
  71.1 0.2 fusion.17
  71.3 2.2 %collective-permute-start = (f32[16,3,128]{2,0,1:T(8,128)S(1)}, f32[16,3,128]{2,0,1:T(8,128)S(1)}, u32[]{:S(2)}, u32[]{:S(2)}) collective-permute-start(f32[16,3,128]{2,0,1:T(8,128)S(1)} %get-tuple-element.7), channel_id=1, source_target_pairs={{0,32},{32,64},{64,96},{96,128},{128,160},{160,192},{192,224},{1,3... | collective-permute-start | bytes 73736 | tf_op jit(solution)/shard_map/ppermute | solution.py:105
  73.5 3.6 %collective-permute-start.1 = (f32[16,3,128]{2,0,1:T(8,128)S(1)}, f32[16,3,128]{2,0,1:T(8,128)S(1)}, u32[]{:S(2)}, u32[]{:S(2)}) collective-permute-start(f32[16,3,128]{2,0,1:T(8,128)S(1)} %get-tuple-element.8), channel_id=1, source_target_pairs={{32,0},{64,32},{96,64},{128,96},{160,128},{192,160},{224,192},{33,... | collective-permute-start | bytes 73736 | tf_op jit(solution)/shard_map/ppermute | solution.py:106
  77.1 0.6 fusion.5
  77.8 0.0 copy-start.8
  77.8 0.6 fusion.14
  78.4 0.2 collective-permute-done.1
  78.6 0.1 slice_bitcast_fusion.1
  78.8 0.2 reshape.100
  79.0 0.2 reshape.104
  79.2 4.6 %collective-permute-start.3 = (f32[16,128]{1,0:T(8,128)S(1)}, f32[16,128]{1,0:T(8,128)S(1)}, u32[]{:S(2)}, u32[]{:S(2)}) collective-permute-start(f32[16,128]{1,0:T(8,128)S(1)} %pad_bitcast_fusion), channel_id=1, source_target_pairs={{2,0},{4,2},{6,4},{8,6},{10,8},{12,10},{14,12},{16,14},{18,16},{20... | collective-permute-start | bytes 24584 | tf_op jit(solution)/shard_map/ppermute | solution.py:38
  83.9 1.9 %collective-permute-start.2 = (f32[16,128]{1,0:T(8,128)S(1)}, f32[16,128]{1,0:T(8,128)S(1)}, u32[]{:S(2)}, u32[]{:S(2)}) collective-permute-start(f32[16,128]{1,0:T(8,128)S(1)} %pad_bitcast_fusion.1), channel_id=1, source_target_pairs={{0,2},{2,4},{4,6},{6,8},{8,10},{10,12},{12,14},{14,16},{16,18},{18... | collective-permute-start | bytes 24584 | tf_op jit(solution)/shard_map/ppermute | solution.py:37
  85.8 0.1 slice_bitcast_fusion.3
  85.9 6.2 %collective-permute-done.2 = f32[16,128]{1,0:T(8,128)S(1)} collective-permute-done((f32[16,128]{1,0:T(8,128)S(1)}, f32[16,128]{1,0:T(8,128)S(1)}, u32[]{:S(2)}, u32[]{:S(2)}) %collective-permute-start.2) | collective-permute-done | bytes 8224 | tf_op jit(solution)/shard_map/ppermute | solution.py:37
  92.1 0.2 reshape.103
  92.4 0.2 reshape.107
  92.6 0.3 pad_maximum_fusion
  92.9 0.7 fusion.30
  93.6 0.6 fusion.33
  94.3 0.3 fusion.36
  94.6 0.8 copy.27
  (43 shorter events, 0.3 us)
Async XLA Ops:
  2.9 15.3 %copy-start.9 = (f32[32,128]{1,0:T(8,128)S(1)}, f32[32,128]{1,0:T(8,128)}, u32[]{:S(2)}) copy-start(f32[32,128]{1,0:T(8,128)} %param.9) | copy-start | bytes 49156
  5.3 63.5 %all-to-all-start = ((f32[256,16,128]{2,1,0:T(8,128)}), f32[256,16,128]{2,1,0:T(8,128)S(1)}, u32[]{:S(2)}, u32[]{:S(2)}) async-start(f32[256,16,128]{2,1,0:T(8,128)} %gather_fusion), calls=%async_computation | async-start | bytes 4194304 | tf_op jit(solution)/shard_map/all_to_all | solution.py:72
  18.2 16.4 %collective-permute-start.4 = (f32[1,3,128]{2,1,0:T(4,128)S(1)}, f32[1,3,128]{2,1,0:T(4,128)S(1)}, u32[]{:S(2)}, u32[]{:S(2)}) collective-permute-start(f32[1,3,128]{2,1,0:T(4,128)S(1)} %get-tuple-element.29), channel_id=1, source_target_pairs={{0,32},{32,64},{64,96},{96,128},{128,160},{160,192},{192,224},{1,3... | collective-permute-start | bytes 4616 | tf_op jit(solution)/shard_map/ppermute | solution.py:14
  20.3 14.2 %collective-permute-start.5 = (f32[1,3,128]{2,1,0:T(4,128)S(1)}, f32[1,3,128]{2,1,0:T(4,128)S(1)}, u32[]{:S(2)}, u32[]{:S(2)}) collective-permute-start(f32[1,3,128]{2,1,0:T(4,128)S(1)} %get-tuple-element.30), channel_id=1, source_target_pairs={{32,0},{64,32},{96,64},{128,96},{160,128},{192,160},{224,192},{33,... | collective-permute-start | bytes 4616 | tf_op jit(solution)/shard_map/ppermute | solution.py:17
  30.9 2.0 %copy-start = (bf16[32,4,128,128]{3,2,1,0:T(8,128)(2,1)}, bf16[32,4,128,128]{3,2,1,0:T(8,128)(2,1)S(1)}, u32[]{:S(2)}) copy-start(bf16[32,4,128,128]{3,2,1,0:T(8,128)(2,1)S(1)} %get-tuple-element.12) | copy-start | bytes 12582916
  30.9 3.7 %copy-start.2 = (bf16[32,4,128,128]{3,2,1,0:T(8,128)(2,1)}, bf16[32,4,128,128]{3,2,1,0:T(8,128)(2,1)S(1)}, u32[]{:S(2)}) copy-start(bf16[32,4,128,128]{3,2,1,0:T(8,128)(2,1)S(1)} %get-tuple-element.11) | copy-start | bytes 12582916
  34.9 20.8 %collective-permute-start.6 = (f32[8,128]{1,0:T(8,128)S(1)}, f32[8,128]{1,0:T(8,128)S(1)}, u32[]{:S(2)}, u32[]{:S(2)}) collective-permute-start(f32[8,128]{1,0:T(8,128)S(1)} %pad_bitcast_fusion.3), channel_id=1, source_target_pairs={{0,2},{2,4},{4,6},{6,8},{8,10},{10,12},{12,14},{14,16},{16,18},{18... | collective-permute-start | bytes 12296 | tf_op jit(solution)/shard_map/ppermute | solution.py:37
  38.3 17.4 %collective-permute-start.7 = (f32[8,128]{1,0:T(8,128)S(1)}, f32[8,128]{1,0:T(8,128)S(1)}, u32[]{:S(2)}, u32[]{:S(2)}) collective-permute-start(f32[8,128]{1,0:T(8,128)S(1)} %pad_bitcast_fusion.2), channel_id=1, source_target_pairs={{2,0},{4,2},{6,4},{8,6},{10,8},{12,10},{14,12},{16,14},{18,16},{20... | collective-permute-start | bytes 12296 | tf_op jit(solution)/shard_map/ppermute | solution.py:38
  56.0 0.7 copy-start.7
  69.7 1.0 %copy-start.5 = (bf16[3,4,128,128]{3,2,1,0:T(8,128)(2,1)S(1)}, bf16[3,4,128,128]{3,2,1,0:T(8,128)(2,1)}, u32[]{:S(2)}) copy-start(bf16[3,4,128,128]{3,2,1,0:T(8,128)(2,1)} %get-tuple-element.13) | copy-start | bytes 1179652
  69.7 1.1 %copy-start.6 = (bf16[3,4,128,128]{3,2,1,0:T(8,128)(2,1)S(1)}, bf16[3,4,128,128]{3,2,1,0:T(8,128)(2,1)}, u32[]{:S(2)}) copy-start(bf16[3,4,128,128]{3,2,1,0:T(8,128)(2,1)} %get-tuple-element.14) | copy-start | bytes 1179652
  69.7 1.3 %copy-start.4 = (bf16[3,4,128,128]{3,2,1,0:T(8,128)(2,1)S(1)}, bf16[3,4,128,128]{3,2,1,0:T(8,128)(2,1)}, u32[]{:S(2)}) copy-start(bf16[3,4,128,128]{3,2,1,0:T(8,128)(2,1)} %get-tuple-element.32) | copy-start | bytes 1179652
  69.7 7.4 %copy-start.3 = (bf16[32,4,128,128]{3,2,1,0:T(8,128)(2,1)S(1)}, bf16[32,4,128,128]{3,2,1,0:T(8,128)(2,1)}, u32[]{:S(2)}) copy-start(bf16[32,4,128,128]{3,2,1,0:T(8,128)(2,1)} %copy-done.2) | copy-start | bytes 12582916
  71.0 6.8 %copy-start.1 = (bf16[32,4,128,128]{3,2,1,0:T(8,128)(2,1)S(1)}, bf16[32,4,128,128]{3,2,1,0:T(8,128)(2,1)}, u32[]{:S(2)}) copy-start(bf16[32,4,128,128]{3,2,1,0:T(8,128)(2,1)} %copy-done) | copy-start | bytes 12582916
  71.3 6.5 %collective-permute-start = (f32[16,3,128]{2,0,1:T(8,128)S(1)}, f32[16,3,128]{2,0,1:T(8,128)S(1)}, u32[]{:S(2)}, u32[]{:S(2)}) collective-permute-start(f32[16,3,128]{2,0,1:T(8,128)S(1)} %get-tuple-element.7), channel_id=1, source_target_pairs={{0,32},{32,64},{64,96},{96,128},{128,160},{160,192},{192,224},{1,3... | collective-permute-start | bytes 73736 | tf_op jit(solution)/shard_map/ppermute | solution.py:105
  73.5 5.1 %collective-permute-start.1 = (f32[16,3,128]{2,0,1:T(8,128)S(1)}, f32[16,3,128]{2,0,1:T(8,128)S(1)}, u32[]{:S(2)}, u32[]{:S(2)}) collective-permute-start(f32[16,3,128]{2,0,1:T(8,128)S(1)} %get-tuple-element.8), channel_id=1, source_target_pairs={{32,0},{64,32},{96,64},{128,96},{160,128},{192,160},{224,192},{33,... | collective-permute-start | bytes 73736 | tf_op jit(solution)/shard_map/ppermute | solution.py:106
  77.8 8.0 %copy-start.8 = (f32[1,38,134]{2,1,0:T(8,128)S(1)}, f32[1,38,134]{2,1,0:T(8,128)}, u32[]{:S(2)}) copy-start(f32[1,38,134]{2,1,0:T(8,128)} %copy-done.7) | copy-start | bytes 61108
  78.8 14.8 %copy-start.10 = (f32[34,130]{1,0:T(8,128)S(1)}, f32[34,130]{1,0:T(8,128)}, u32[]{:S(2)}) copy-start(f32[34,130]{1,0:T(8,128)} %slice_bitcast_fusion.2) | copy-start | bytes 53044
  79.2 13.1 %collective-permute-start.3 = (f32[16,128]{1,0:T(8,128)S(1)}, f32[16,128]{1,0:T(8,128)S(1)}, u32[]{:S(2)}, u32[]{:S(2)}) collective-permute-start(f32[16,128]{1,0:T(8,128)S(1)} %pad_bitcast_fusion), channel_id=1, source_target_pairs={{2,0},{4,2},{6,4},{8,6},{10,8},{12,10},{14,12},{16,14},{18,16},{20... | collective-permute-start | bytes 24584 | tf_op jit(solution)/shard_map/ppermute | solution.py:38
  83.9 8.2 %collective-permute-start.2 = (f32[16,128]{1,0:T(8,128)S(1)}, f32[16,128]{1,0:T(8,128)S(1)}, u32[]{:S(2)}, u32[]{:S(2)}) collective-permute-start(f32[16,128]{1,0:T(8,128)S(1)} %pad_bitcast_fusion.1), channel_id=1, source_target_pairs={{0,2},{2,4},{4,6},{6,8},{8,10},{10,12},{12,14},{14,16},{16,18},{18... | collective-permute-start | bytes 24584 | tf_op jit(solution)/shard_map/ppermute | solution.py:37

commit v14 on v12

--- a/solution.py
+++ b/solution.py
@@ -1,6 +1,7 @@
 import jax
 import jax.numpy as jnp
 from jax import lax
+from jax.experimental.layout import Layout, with_layout_constraint
 from jax.sharding import PartitionSpec as P
 
 PASSES = 3
@@ -106,7 +107,7 @@
     high = lax.ppermute(top, "gx", backward)
     middle = remap(PASSES, frows - PASSES)
     carried = jnp.concatenate([low, top, middle, bottom, high], axis=1)
-    field = packed_halo(carried, "gy", PASSES)
+    field = with_layout_constraint(packed_halo(carried, "gy", PASSES), Layout((0, 1, 2)))
     for _ in range(PASSES):
         gain = gain[:, 1:-1, 1:-1]
         field = smooth_step(field, gain)

time: 94.1 us -> 97.4 us (1.035)
  matrix products: 1.62 us -> 3.7 us
  waiting for transfers between devices: 24.8 us -> 25.8 us
    dot_general x4, matrix products: 1.62 us -> 3.7 us  [product(): jnp.einsum('iklc,ikcd->lid', a, w, preferred_element_type=jnp.float32)]
    ppermute x1, waiting for transfers between devices: 0.25 us -> 1.46 us  [shards(): high = lax.ppermute(top, 'gx', backward)]
    unnamed x26 -> x21, local copies, waits for them, and re-layouts: 3.83 us -> 3.54 us
  transfers between devices with their start and end apart: 9 -> 9, of which waited for: 4 -> 4; matrix products, arithmetic and copies ran while one was open for 14% -> 12% of each run, Pallas kernels for 0% -> 0%
where the time goes in v14:
time: 97.4 us; the launch traced here: 96 us
  starting transfers between devices  41.1 us (42%)
  waiting for transfers between devices  25.8 us (26%)
  local copies, waits for them, and re-layouts  13.3 us (14%)
  other arithmetic  11.7 us (12%)
  matrix products  3.7 us (4%)
    all_to_all x1, starting transfers between devices, shards(): incoming = lax.all_to_all(outgoing, ('gx', 'gy'), 0, 0, tiled=True)  12.9 us
    all_to_all x1, waiting for transfers between devices, shards(): incoming = lax.all_to_all(outgoing, ('gx', 'gy'), 0, 0, tiled=True)  11.9 us
    ppermute x2, starting transfers between devices, packed_halo(): high = unpack(lax.ppermute(pack(block[:, :, :width]), axis, backward))  11.8 us
    ppermute x2, waiting for transfers between devices, packed_halo(): low = unpack(lax.ppermute(pack(block[:, :, cols - width:]), axis, forward))  11.5 us
    convert_element_type x2, other arithmetic, split(): return (high.astype(jnp.bfloat16), (x - high).astype(jnp.bfloat16))  5.98 us
    ppermute x2, starting transfers between devices, packed_halo(): low = unpack(lax.ppermute(pack(block[:, :, cols - width:]), axis, forward))  5.29 us
    dot_general x4, matrix products, product(): jnp.einsum('iklc,ikcd->lid', a, w, preferred_element_type=jnp.float32)  3.7 us
    ppermute x1, starting transfers between devices, shards(): high = lax.ppermute(top, 'gx', backward)  3.64 us
  transfers between devices with their start and end apart: 9, of which 4 were waited for; matrix products, arithmetic and copies ran while one was open for 12% of the time, Pallas kernels for 0%

profile of v14, /device:TPU:10, one launch (start us, length us, event | category | flops | bytes accessed | tf_op | source)
XLA Modules:
  0.0 96.0 jit_solution(15630247436475012788)
XLA Ops:
  0.0 0.9 select_reduce_fusion
  1.3 0.1 sub.30
  1.5 0.1 copy.42
  1.6 0.1 reshape.131
  1.7 1.1 %copy.67 = f32[16,32,128]{2,0,1:T(8,128)S(1)} copy(f32[16,32,128]{2,1,0:T(8,128)} %param.5) | data formatting | bytes 524288 | tf_op args[0]
  2.9 2.4 %gather_fusion = f32[256,16,128]{2,1,0:T(8,128)} fusion(f32[32,16,128]{2,1,0:T(8,128)S(1)} %bitcast.67, s32[1024]{0:T(1024)S(1)} %pad_clamp_fusion.1), kind=kCustom, calls=%fused_computation | custom fusion | bytes 4195328 | tf_op jit(solution)/shard_map/jit(_take)/gather | solution.py:72
  5.3 12.9 %all-to-all-start = ((f32[256,16,128]{2,1,0:T(8,128)}), f32[256,16,128]{2,1,0:T(8,128)S(1)}, u32[]{:S(2)}, u32[]{:S(2)}) async-start(f32[256,16,128]{2,1,0:T(8,128)} %gather_fusion), calls=%async_computation | async-start | bytes 4194304 | tf_op jit(solution)/shard_map/all_to_all | solution.py:73
  18.2 2.1 %collective-permute-start.4 = (f32[1,3,128]{2,1,0:T(4,128)S(1)}, f32[1,3,128]{2,1,0:T(4,128)S(1)}, u32[]{:S(2)}, u32[]{:S(2)}) collective-permute-start(f32[1,3,128]{2,1,0:T(4,128)S(1)} %get-tuple-element.29), channel_id=1, source_target_pairs={{0,32},{32,64},{64,96},{96,128},{128,160},{160,192},{192,224},{1,3... | collective-permute-start | bytes 4616 | tf_op jit(solution)/shard_map/ppermute | solution.py:15
  20.3 3.4 %collective-permute-start.5 = (f32[1,3,128]{2,1,0:T(4,128)S(1)}, f32[1,3,128]{2,1,0:T(4,128)S(1)}, u32[]{:S(2)}, u32[]{:S(2)}) collective-permute-start(f32[1,3,128]{2,1,0:T(4,128)S(1)} %get-tuple-element.30), channel_id=1, source_target_pairs={{32,0},{64,32},{96,64},{128,96},{160,128},{192,160},{224,192},{33,... | collective-permute-start | bytes 4616 | tf_op jit(solution)/shard_map/ppermute | solution.py:18
  23.7 0.8 broadcast_multiply_fusion
  24.5 0.1 copy.44
  24.6 0.1 eq.40
  24.7 0.1 copy.43
  24.8 0.1 mul.72
  24.9 0.2 convert_reduce_fusion
  25.1 5.8 %fusion = (bf16[32,4,128,128]{3,2,1,0:T(8,128)(2,1)S(1)}, bf16[32,4,128,128]{3,2,1,0:T(8,128)(2,1)S(1)}) fusion(f32[32,4,128,128]{3,2,1,0:T(8,128)} %param.6), kind=kLoop, calls=%fused_computation.4 | loop fusion | flops 8388608 | bytes 16777216 | tf_op jit(solution)/shard_map/convert_element_type | solution.py:84
  30.9 1.9 %copy-done = bf16[32,4,128,128]{3,2,1,0:T(8,128)(2,1)} copy-done((bf16[32,4,128,128]{3,2,1,0:T(8,128)(2,1)}, bf16[32,4,128,128]{3,2,1,0:T(8,128)(2,1)S(1)}, u32[]{:S(2)}) %copy-start) | copy-done | bytes 4194328
  32.8 1.6 %fusion.49 = (bf16[3,4,128,128]{3,2,1,0:T(8,128)(2,1)S(1)}, bf16[3,4,128,128]{3,2,1,0:T(8,128)(2,1)}, bf16[3,4,128,128]{3,2,1,0:T(8,128)(2,1)}, bf16[3,4,128,128]{3,2,1,0:T(8,128)(2,1)}) fusion(bf16[32,4,128,128]{3,2,1,0:T(8,128)(2,1)S(1)} %get-tuple-element.11, bf16[32,4,128,128]{3,2,1,0:T(8,128)(2,1)S(1)} %get-tuple-element.12), kind=kLoop, calls=%fused_computation.93 | loop fusion | bytes 3145728 | tf_op jit(solution)/shard_map/slice | solution.py:103
  34.6 0.1 slice_bitcast_fusion.5
  34.6 0.1 copy.53
  34.7 0.1 reshape.120
  34.8 3.4 %collective-permute-start.6 = (f32[8,128]{1,0:T(8,128)S(1)}, f32[8,128]{1,0:T(8,128)S(1)}, u32[]{:S(2)}, u32[]{:S(2)}) collective-permute-start(f32[8,128]{1,0:T(8,128)S(1)} %pad_bitcast_fusion.3), channel_id=1, source_target_pairs={{0,2},{2,4},{4,6},{6,8},{8,10},{10,12},{12,14},{14,16},{16,18},{18... | collective-permute-start | bytes 12296 | tf_op jit(solution)/shard_map/ppermute | solution.py:38
  38.2 0.1 copy.54
  38.3 0.1 reshape.124
  38.4 5.2 %collective-permute-start.7 = (f32[8,128]{1,0:T(8,128)S(1)}, f32[8,128]{1,0:T(8,128)S(1)}, u32[]{:S(2)}, u32[]{:S(2)}) collective-permute-start(f32[8,128]{1,0:T(8,128)S(1)} %pad_bitcast_fusion.2), channel_id=1, source_target_pairs={{2,0},{4,2},{6,4},{8,6},{10,8},{12,10},{14,12},{16,14},{18,16},{20... | collective-permute-start | bytes 12296 | tf_op jit(solution)/shard_map/ppermute | solution.py:39
  43.5 0.6 pad_clamp_fusion
  44.1 11.5 %collective-permute-done.6 = f32[8,128]{1,0:T(8,128)S(1)} collective-permute-done((f32[8,128]{1,0:T(8,128)S(1)}, f32[8,128]{1,0:T(8,128)S(1)}, u32[]{:S(2)}, u32[]{:S(2)}) %collective-permute-start.6) | collective-permute-done | bytes 4128 | tf_op jit(solution)/shard_map/ppermute | solution.py:38
  55.7 0.1 reshape.123
  55.7 0.1 copy.55
  55.8 0.1 reshape.127
  55.9 0.1 copy.56
  56.0 0.1 pad_maximum_fusion.1
  56.1 0.7 slice_bitcast_fusion.3
  56.8 11.9 %all-to-all-done = f32[256,16,128]{2,1,0:T(8,128)S(1)} async-done(((f32[256,16,128]{2,1,0:T(8,128)}), f32[256,16,128]{2,1,0:T(8,128)S(1)}, u32[]{:S(2)}, u32[]{:S(2)}) %all-to-all-start) | async-done | bytes 2097184 | tf_op jit(solution)/shard_map/all_to_all | solution.py:73
  68.8 0.9 gather_fusion.1
  69.7 0.2 reduce-precision_convert_fusion.1
  69.9 2.7 %fusion.8 = f32[26,128,16]{1,2,0:T(8,128)S(1)} fusion(bf16[32,4,128,128]{3,2,1,0:T(8,128)(2,1)} %copy-done.2, bf16[32,4,16,128]{3,2,1,0:T(8,128)(2,1)S(1)} %get-tuple-element.17), kind=kOutput, calls=%fused_computation.12 | convolution fusion | flops 54525952 | bytes 4046848 | tf_op jit(solution)/shard_map/iklc,ikcd->lid/dot_general | solution.py:90
  72.7 0.4 copy-done.1
  73.1 0.6 fusion.5
  73.7 0.3 copy.66
  74.0 0.2 convolution_bitcast_fusion
  74.3 0.2 convolution_bitcast_fusion.1
  74.6 1.9 %collective-permute-start = (f32[16,3,128]{2,1,0:T(4,128)S(1)}, f32[16,3,128]{2,1,0:T(4,128)S(1)}, u32[]{:S(2)}, u32[]{:S(2)}) collective-permute-start(f32[16,3,128]{2,1,0:T(4,128)S(1)} %get-tuple-element.7), channel_id=1, source_target_pairs={{0,32},{32,64},{64,96},{96,128},{128,160},{160,192},{192,224},{1,3... | collective-permute-start | bytes 73736 | tf_op jit(solution)/shard_map/ppermute | solution.py:106
  76.5 3.6 %collective-permute-start.1 = (f32[16,3,128]{2,1,0:T(4,128)S(1)}, f32[16,3,128]{2,1,0:T(4,128)S(1)}, u32[]{:S(2)}, u32[]{:S(2)}) collective-permute-start(f32[16,3,128]{2,1,0:T(4,128)S(1)} %get-tuple-element.8), channel_id=1, source_target_pairs={{32,0},{64,32},{96,64},{128,96},{160,128},{192,160},{224,192},{33,... | collective-permute-start | bytes 73736 | tf_op jit(solution)/shard_map/ppermute | solution.py:107
  80.1 0.1 fusion.30
  80.3 1.5 %collective-permute-done.1 = f32[16,3,128]{2,1,0:T(4,128)S(1)} collective-permute-done((f32[16,3,128]{2,1,0:T(4,128)S(1)}, f32[16,3,128]{2,1,0:T(4,128)S(1)}, u32[]{:S(2)}, u32[]{:S(2)}) %collective-permute-start.1) | collective-permute-done | bytes 24608 | tf_op jit(solution)/shard_map/ppermute | solution.py:107
  81.7 0.3 concatenate.37
  82.0 0.2 slice_bitcast_fusion.1
  82.2 0.2 copy.49
  82.4 0.1 reshape.112
  82.6 1.9 %collective-permute-start.2 = (f32[16,128]{1,0:T(8,128)S(1)}, f32[16,128]{1,0:T(8,128)S(1)}, u32[]{:S(2)}, u32[]{:S(2)}) collective-permute-start(f32[16,128]{1,0:T(8,128)S(1)} %pad_bitcast_fusion.1), channel_id=1, source_target_pairs={{0,2},{2,4},{4,6},{6,8},{8,10},{10,12},{12,14},{14,16},{16,18},{18... | collective-permute-start | bytes 24584 | tf_op jit(solution)/shard_map/ppermute | solution.py:38
  84.5 0.2 copy.51
  84.7 0.1 reshape.116
  84.8 6.6 %collective-permute-start.3 = (f32[16,128]{1,0:T(8,128)S(1)}, f32[16,128]{1,0:T(8,128)S(1)}, u32[]{:S(2)}, u32[]{:S(2)}) collective-permute-start(f32[16,128]{1,0:T(8,128)S(1)} %pad_bitcast_fusion), channel_id=1, source_target_pairs={{2,0},{4,2},{6,4},{8,6},{10,8},{12,10},{14,12},{16,14},{18,16},{20... | collective-permute-start | bytes 24584 | tf_op jit(solution)/shard_map/ppermute | solution.py:39
  91.5 0.1 slice_bitcast_fusion.2
  91.5 0.1 reshape.115
  91.7 0.2 copy.50
  91.9 0.9 collective-permute-done.3
  92.8 0.1 reshape.119
  92.9 0.2 copy.52
  93.1 0.3 pad_maximum_fusion
  93.5 0.8 fusion.26
  94.2 0.8 fusion.23
  95.0 1.0 %fusion.29 = f32[16,32,128]{2,1,0:T(8,128)} fusion(f32[16,34,130]{2,1,0:T(8,128)S(1)} %fusion.23, f32[32,128]{1,0:T(8,128)S(1)} %copy-done.8), kind=kLoop, calls=%fused_computation.44 | loop fusion | flops 458752 | bytes 1589248 | tf_op jit(solution)/shard_map/add | solution.py:51
  (49 shorter events, 0.7 us)
Async XLA Ops:
  2.9 15.3 %copy-start.8 = (f32[32,128]{1,0:T(8,128)S(1)}, f32[32,128]{1,0:T(8,128)}, u32[]{:S(2)}) copy-start(f32[32,128]{1,0:T(8,128)} %param.9) | copy-start | bytes 49156
  5.3 63.5 %all-to-all-start = ((f32[256,16,128]{2,1,0:T(8,128)}), f32[256,16,128]{2,1,0:T(8,128)S(1)}, u32[]{:S(2)}, u32[]{:S(2)}) async-start(f32[256,16,128]{2,1,0:T(8,128)} %gather_fusion), calls=%async_computation | async-start | bytes 4194304 | tf_op jit(solution)/shard_map/all_to_all | solution.py:73
  18.2 16.4 %collective-permute-start.4 = (f32[1,3,128]{2,1,0:T(4,128)S(1)}, f32[1,3,128]{2,1,0:T(4,128)S(1)}, u32[]{:S(2)}, u32[]{:S(2)}) collective-permute-start(f32[1,3,128]{2,1,0:T(4,128)S(1)} %get-tuple-element.29), channel_id=1, source_target_pairs={{0,32},{32,64},{64,96},{96,128},{128,160},{160,192},{192,224},{1,3... | collective-permute-start | bytes 4616 | tf_op jit(solution)/shard_map/ppermute | solution.py:15
  20.3 14.2 %collective-permute-start.5 = (f32[1,3,128]{2,1,0:T(4,128)S(1)}, f32[1,3,128]{2,1,0:T(4,128)S(1)}, u32[]{:S(2)}, u32[]{:S(2)}) collective-permute-start(f32[1,3,128]{2,1,0:T(4,128)S(1)} %get-tuple-element.30), channel_id=1, source_target_pairs={{32,0},{64,32},{96,64},{128,96},{160,128},{192,160},{224,192},{33,... | collective-permute-start | bytes 4616 | tf_op jit(solution)/shard_map/ppermute | solution.py:18
  30.9 2.0 %copy-start = (bf16[32,4,128,128]{3,2,1,0:T(8,128)(2,1)}, bf16[32,4,128,128]{3,2,1,0:T(8,128)(2,1)S(1)}, u32[]{:S(2)}) copy-start(bf16[32,4,128,128]{3,2,1,0:T(8,128)(2,1)S(1)} %get-tuple-element.12) | copy-start | bytes 12582916
  30.9 3.6 %copy-start.2 = (bf16[32,4,128,128]{3,2,1,0:T(8,128)(2,1)}, bf16[32,4,128,128]{3,2,1,0:T(8,128)(2,1)S(1)}, u32[]{:S(2)}) copy-start(bf16[32,4,128,128]{3,2,1,0:T(8,128)(2,1)S(1)} %get-tuple-element.11) | copy-start | bytes 12582916
  34.8 20.8 %collective-permute-start.6 = (f32[8,128]{1,0:T(8,128)S(1)}, f32[8,128]{1,0:T(8,128)S(1)}, u32[]{:S(2)}, u32[]{:S(2)}) collective-permute-start(f32[8,128]{1,0:T(8,128)S(1)} %pad_bitcast_fusion.3), channel_id=1, source_target_pairs={{0,2},{2,4},{4,6},{6,8},{8,10},{10,12},{12,14},{14,16},{16,18},{18... | collective-permute-start | bytes 12296 | tf_op jit(solution)/shard_map/ppermute | solution.py:38
  38.4 17.5 %collective-permute-start.7 = (f32[8,128]{1,0:T(8,128)S(1)}, f32[8,128]{1,0:T(8,128)S(1)}, u32[]{:S(2)}, u32[]{:S(2)}) collective-permute-start(f32[8,128]{1,0:T(8,128)S(1)} %pad_bitcast_fusion.2), channel_id=1, source_target_pairs={{2,0},{4,2},{6,4},{8,6},{10,8},{12,10},{14,12},{16,14},{18,16},{20... | collective-permute-start | bytes 12296 | tf_op jit(solution)/shard_map/ppermute | solution.py:39
  56.1 0.7 copy-start.6
  69.9 3.2 %copy-start.1 = (bf16[32,4,128,128]{3,2,1,0:T(8,128)(2,1)S(1)}, bf16[32,4,128,128]{3,2,1,0:T(8,128)(2,1)}, u32[]{:S(2)}) copy-start(bf16[32,4,128,128]{3,2,1,0:T(8,128)(2,1)} %copy-done) | copy-start | bytes 12582916
  72.6 1.3 %copy-start.4 = (bf16[3,4,128,128]{3,2,1,0:T(8,128)(2,1)S(1)}, bf16[3,4,128,128]{3,2,1,0:T(8,128)(2,1)}, u32[]{:S(2)}) copy-start(bf16[3,4,128,128]{3,2,1,0:T(8,128)(2,1)} %get-tuple-element.33) | copy-start | bytes 1179652
  72.6 1.3 %copy-start.5 = (bf16[3,4,128,128]{3,2,1,0:T(8,128)(2,1)S(1)}, bf16[3,4,128,128]{3,2,1,0:T(8,128)(2,1)}, u32[]{:S(2)}) copy-start(bf16[3,4,128,128]{3,2,1,0:T(8,128)(2,1)} %get-tuple-element.34) | copy-start | bytes 1179652
  73.1 1.2 %copy-start.3 = (bf16[3,4,128,128]{3,2,1,0:T(8,128)(2,1)S(1)}, bf16[3,4,128,128]{3,2,1,0:T(8,128)(2,1)}, u32[]{:S(2)}) copy-start(bf16[3,4,128,128]{3,2,1,0:T(8,128)(2,1)} %get-tuple-element.14) | copy-start | bytes 1179652
  74.0 17.5 %copy-start.7 = (f32[1,38,134]{2,1,0:T(8,128)S(1)}, f32[1,38,134]{2,1,0:T(8,128)}, u32[]{:S(2)}) copy-start(f32[1,38,134]{2,1,0:T(8,128)} %copy-done.6) | copy-start | bytes 61108
  74.5 19.0 %copy-start.9 = (f32[36,132]{1,0:T(8,128)S(1)}, f32[36,132]{1,0:T(8,128)}, u32[]{:S(2)}) copy-start(f32[36,132]{1,0:T(8,128)} %slice_bitcast_fusion.3) | copy-start | bytes 57028
  74.6 5.7 %collective-permute-start = (f32[16,3,128]{2,1,0:T(4,128)S(1)}, f32[16,3,128]{2,1,0:T(4,128)S(1)}, u32[]{:S(2)}, u32[]{:S(2)}) collective-permute-start(f32[16,3,128]{2,1,0:T(4,128)S(1)} %get-tuple-element.7), channel_id=1, source_target_pairs={{0,32},{32,64},{64,96},{96,128},{128,160},{160,192},{192,224},{1,3... | collective-permute-start | bytes 73736 | tf_op jit(solution)/shard_map/ppermute | solution.py:106
  76.5 5.2 %collective-permute-start.1 = (f32[16,3,128]{2,1,0:T(4,128)S(1)}, f32[16,3,128]{2,1,0:T(4,128)S(1)}, u32[]{:S(2)}, u32[]{:S(2)}) collective-permute-start(f32[16,3,128]{2,1,0:T(4,128)S(1)} %get-tuple-element.8), channel_id=1, source_target_pairs={{32,0},{64,32},{96,64},{128,96},{160,128},{192,160},{224,192},{33,... | collective-permute-start | bytes 73736 | tf_op jit(solution)/shard_map/ppermute | solution.py:107
  82.6 9.0 %collective-permute-start.2 = (f32[16,128]{1,0:T(8,128)S(1)}, f32[16,128]{1,0:T(8,128)S(1)}, u32[]{:S(2)}, u32[]{:S(2)}) collective-permute-start(f32[16,128]{1,0:T(8,128)S(1)} %pad_bitcast_fusion.1), channel_id=1, source_target_pairs={{0,2},{2,4},{4,6},{6,8},{8,10},{10,12},{12,14},{14,16},{16,18},{18... | collective-permute-start | bytes 24584 | tf_op jit(solution)/shard_map/ppermute | solution.py:38
  84.8 8.0 %collective-permute-start.3 = (f32[16,128]{1,0:T(8,128)S(1)}, f32[16,128]{1,0:T(8,128)S(1)}, u32[]{:S(2)}, u32[]{:S(2)}) collective-permute-start(f32[16,128]{1,0:T(8,128)S(1)} %pad_bitcast_fusion), channel_id=1, source_target_pairs={{2,0},{4,2},{6,4},{8,6},{10,8},{12,10},{14,12},{16,14},{18,16},{20... | collective-permute-start | bytes 24584 | tf_op jit(solution)/shard_map/ppermute | solution.py:39
